TPU v7x, 128 devices: a whole 4x4x4 slice. The times are simulated.
128 devices in a mesh: chan: 8 (over y, core), pix: 16 (over x, z).
Axes of the slice: x: 4, y: 4, z: 4, core: 2. Of those that a mesh axis runs over, the one named last changes fastest.
Arguments:
- sky_cube: bfloat16 [512, 262144], P('chan', 'pix')
- beam_blocks: bfloat16 [512, 9, 128, 128], P('chan'), may hold values from -0.1875 to 0.1875
- pattern: int32 [512, 128, 9], P('chan'), may hold values from 0 to 127, as said below
- start_modes: float32 [512, 32], replicated, may hold values from -6 to 6
Outputs:
- cleaned: bfloat16 [512, 262144], P('chan', 'pix')
- mode_basis: float32 [512, 32], replicated
Inputs may be any that keep to these rules, and one draw needn't show every extreme that they name: `pattern`: each source block is within 6 blocks of its output block, taken cyclically within the pixel group.
All inputs are finite; a program needn't handle non-finite values.
Results may differ from a plain program's by a relative error of at most 0.0062.
Values may be sent and summed in bfloat16 or wider, within the bound.
No kernel may reach another device: no remote copies, remote signals or barrier semaphores. Data moves between devices by JAX's collectives and lax.ppermute only.
A program may use at most 128 MiB of HBM per device.

v0:
```python
import jax
import jax.numpy as jnp
from jax import lax
from jax.sharding import PartitionSpec as P

BLK = 128
ITERS = 3


def orthonormal(images):
    square = jnp.dot(images.T, images, precision=lax.Precision.HIGHEST)
    factor = jnp.linalg.cholesky(square)
    return lax.linalg.triangular_solve(
        factor, images, left_side=False, lower=True, transpose_a=True
    )


def local(sky_cube, beam_blocks, pattern, start_modes):
    chans = sky_cube.shape[0]
    pix_group = sky_cube.shape[1]
    block_count = pix_group // BLK
    blocks = sky_cube.reshape(chans, block_count, BLK)
    block_ids = lax.broadcasted_iota(jnp.int32, (1, 1, 1, block_count), 3)
    selector = (pattern[:, :, :, None] == block_ids).astype(jnp.bfloat16)
    sources = jnp.einsum(
        "cbkn,cnj->cbkj", selector, blocks, preferred_element_type=jnp.float32
    ).astype(jnp.bfloat16)
    smoothed = jnp.einsum(
        "cbkj,ckij->cbi", sources, beam_blocks, preferred_element_type=jnp.float32
    ).astype(jnp.bfloat16)
    smoothed = smoothed.reshape(chans, pix_group)
    by_pixel = lax.all_to_all(smoothed, "chan", split_axis=1, concat_axis=0, tiled=True)
    all_pixels = pix_group * lax.axis_size("pix")
    basis = start_modes
    partial_value = jnp.dot(by_pixel, by_pixel.T, preferred_element_type=jnp.float32)
    total = lax.psum(partial_value, ("chan", "pix"))
    gram = total / all_pixels
    for sweep in range(ITERS):
        images = jnp.dot(gram, basis, precision=lax.Precision.HIGHEST)
        basis = orthonormal(images)
    modes_low = basis.astype(jnp.bfloat16)
    coeffs = jnp.dot(modes_low.T, by_pixel, preferred_element_type=jnp.float32).astype(jnp.bfloat16)
    removed = jnp.dot(modes_low, coeffs, preferred_element_type=jnp.float32)
    cleaned_pixels = (by_pixel.astype(jnp.float32) - removed).astype(jnp.bfloat16)
    cleaned = lax.all_to_all(cleaned_pixels, "chan", split_axis=0, concat_axis=1, tiled=True)
    return (cleaned, basis)


def solution(mesh):
    return jax.shard_map(
        local,
        mesh=mesh,
        in_specs=(P("chan", "pix"), P("chan", None, None, None), P("chan", None, None), P()),
        out_specs=(P("chan", "pix"), P()),
        check_vma=False,
    )
```

profile of v0, /device:TPU:1, one launch (start us, length us, event | category | flops | bytes accessed | tf_op | source)
XLA Modules:
  0.0 301.7 jit_solution(801119934314081547)
XLA Ops:
  7.2 1.1 copy.18
  8.4 2.2 copy.27
  10.5 20.5 %fusion.61 = bf16[64,128,9,128]{3,1,2,0:T(8,128)(2,1)} fusion(s32[64,128,9]{1,2,0:T(8,128)S(1)} %copy.18, bf16[64,128,128,1]{2,1,0,3:T(8,128)(2,1)S(1)} %bitcast.79), kind=kOutput, calls=%fused_computation.3.clone.clone.clone.1 | convolution fusion | flops 2434793472 | bytes 21266432 | tf_op jit(solution)/shard_map/cbkn,cnj->cbkj/dot_general | solution.py:25
  31.1 15.1 %bitcast_convert_fusion = bf16[64,128,128]{2,1,0:T(8,128)(2,1)S(1)} fusion(bf16[64,9,128,128]{3,2,1,0:T(8,128)(2,1)} %param.8, bf16[64,128,9,128]{3,1,2,0:T(8,128)(2,1)} %fusion.61), kind=kOutput, calls=%fused_computation.5 | convolution fusion | flops 2416967680 | bytes 39845888 | tf_op jit(solution)/shard_map/cbkj,ckij->cbi/dot_general | solution.py:28
  46.1 2.3 all_to_all.28
  48.4 2.7 copy.19
  51.2 31.9 %all_to_all.38 = bf16[64,8,2048]{2,0,1:T(8,128)(2,1)S(1)} all-to-all(bf16[64,8,2048]{2,0,1:T(8,128)(2,1)S(1)} %copy.19), channel_id=1, replica_groups=mesh['chan'=8,'pix'=16] {'chan'}, dimensions={1} | all-to-all | bytes 4194304 | tf_op jit(solution)/shard_map/all_to_all | solution.py:32
  83.1 2.3 fusion.35
  85.4 149.2 %all-reduce.2.cloned.1.call-done = f32[512,512]{1,0:T(8,128)} async-done(((f32[512,512]{1,0:T(8,128)}), f32[512,512]{1,0:T(8,128)}) %all-reduce.2.cloned.1.call-update) | async-done | bytes 1048592 | tf_op jit(solution)/shard_map/psum | solution.py:36
  234.5 2.4 fusion.12
  237.2 2.9 cholesky.59
  240.8 0.7 fusion.19
  241.5 2.4 custom-call.7
  244.2 1.1 fusion.10
  245.6 2.9 cholesky.70
  249.2 0.7 fusion.20
  249.9 2.4 custom-call.8
  252.6 1.1 fusion.8
  254.0 2.9 cholesky.81
  257.6 0.7 fusion.21
  258.2 2.4 custom-call.9
  260.9 2.4 subtract_convert_fusion
  263.3 30.0 %all_to_all.39 = bf16[8,64,2048]{2,1,0:T(8,128)(2,1)S(1)} all-to-all(bf16[8,64,2048]{2,1,0:T(8,128)(2,1)} %bitcast.75), channel_id=1, replica_groups=mesh['chan'=8,'pix'=16] {'chan'}, dimensions={0} | all-to-all | bytes 4194304 | tf_op jit(solution)/shard_map/all_to_all | solution.py:45
  293.3 1.6 copy.26
  (26 shorter events, 3.8 us)
Async XLA Ops:
  7.2 227.4 %copy-start = (f32[512,32]{0,1:T(8,128)S(1)}, f32[512,32]{0,1:T(8,128)}, u32[]{:S(2)}) copy-start(f32[512,32]{0,1:T(8,128)} %param.10) | copy-start | bytes 196612
  7.2 227.4 %all-reduce.2.cloned.1.call-start = ((), (), s32[]{:S(2)}) async-start(), calls=%async_computation.2 | async-start | bytes 2097152 | tf_op jit(solution)/shard_map/psum | solution.py:36
  234.5 9.7 %copy-start.1 = (f32[512,512]{1,0:T(8,128)S(1)}, f32[512,512]{1,0:T(8,128)}, u32[]{:S(2)}) copy-start(f32[512,512]{1,0:T(8,128)} %all-reduce.2.cloned.1.call-done) | copy-start | bytes 3145732
  260.9 2.4 copy-start.2
Sparse Core Ops, SparseCore 0:
  85.5 148.9 all-reduce.1
where the time goes:
time: 302 us
  waiting for transfers between devices  149 us (49%)
  blocking collectives  61.9 us (20%)
  matrix products  46.2 us (15%)
  other arithmetic  20.1 us (7%)
  between operations  14.2 us (5%)
  local copies, waits for them, and re-layouts  10.1 us (3%)
    psum x1, waiting for transfers between devices, local(): total = lax.psum(partial_value, ('chan', 'pix'))  149 us
    all_to_all x1, blocking collectives, local(): lax.all_to_all(smoothed, 'chan', split_axis=1, concat_axis=0, tiled=True)  31.9 us
    all_to_all x1, blocking collectives, local(): lax.all_to_all(cleaned_pixels, 'chan', split_axis=0, concat_axis=1, tiled...  30 us
    dot_general x1, matrix products, local(): jnp.einsum('cbkn,cnj->cbkj', selector, blocks, preferred_element_type=jnp...  20.5 us
    dot_general x1, matrix products, local(): jnp.einsum('cbkj,ckij->cbi', sources, beam_blocks, preferred_element_type...  15.1 us
    another operation x9, other arithmetic, orthonormal(): factor = jnp.linalg.cholesky(square)  10.8 us
    another operation x6, other arithmetic, orthonormal(): lax.linalg.triangular_solve(factor, images, left_side=False, lower=True,...  9.26 us
  transfers between devices with their start and end apart: 1, of which 1 were waited for; matrix products, arithmetic and copies ran while one was open for 0% of the time, Pallas kernels for 0%

commit v1 on v0

--- a/solution.py
+++ b/solution.py
@@ -1,3 +1,4 @@
+import numpy as np
 import jax
 import jax.numpy as jnp
 from jax import lax
@@ -5,6 +6,7 @@
 
 BLK = 128
 ITERS = 3
+AXES = ("chan", "pix")
 
 
 def orthonormal(images):
@@ -13,6 +15,38 @@
     return lax.linalg.triangular_solve(
         factor, images, left_side=False, lower=True, transpose_a=True
     )
+
+
+def sum_all(pieces):
+    n = pieces.shape[0]
+    got = lax.all_to_all(pieces, AXES, 0, 0, tiled=False)
+    mine = jnp.sum(got, axis=0)
+    spread = jnp.broadcast_to(mine[None], (n,) + mine.shape)
+    return lax.all_to_all(spread, AXES, 0, 0, tiled=False)
+
+
+def symmetric_sum(partial, nb):
+    size = partial.shape[0]
+    bs = size // nb
+    upper = [(i, j) for i in range(nb) for j in range(i, nb)]
+    blocks = partial.reshape(nb, bs, nb, bs).transpose(0, 2, 1, 3)
+    iu = np.array([p[0] for p in upper])
+    ju = np.array([p[1] for p in upper])
+    packed = blocks[iu, ju].reshape(-1)
+    n = lax.axis_size(AXES)
+    total = packed.shape[0]
+    width = -(-total // n)
+    packed = jnp.pad(packed, (0, width * n - total))
+    summed = sum_all(packed.reshape(n, width)).reshape(-1)[:total]
+    summed = summed.reshape(len(upper), bs, bs)
+    kmap = np.zeros((nb, nb), np.int32)
+    for k, (i, j) in enumerate(upper):
+        kmap[i, j] = k
+        kmap[j, i] = k
+    picked = summed[kmap]
+    lower = np.array([[i > j for j in range(nb)] for i in range(nb)])
+    full = jnp.where(lower[:, :, None, None], jnp.swapaxes(picked, -1, -2), picked)
+    return full.transpose(0, 2, 1, 3).reshape(size, size)
 
 
 def local(sky_cube, beam_blocks, pattern, start_modes):
@@ -30,19 +64,24 @@
     ).astype(jnp.bfloat16)
     smoothed = smoothed.reshape(chans, pix_group)
     by_pixel = lax.all_to_all(smoothed, "chan", split_axis=1, concat_axis=0, tiled=True)
+    n_chan = lax.axis_size("chan")
     all_pixels = pix_group * lax.axis_size("pix")
     basis = start_modes
     partial_value = jnp.dot(by_pixel, by_pixel.T, preferred_element_type=jnp.float32)
-    total = lax.psum(partial_value, ("chan", "pix"))
+    total = symmetric_sum(partial_value, n_chan)
     gram = total / all_pixels
     for sweep in range(ITERS):
         images = jnp.dot(gram, basis, precision=lax.Precision.HIGHEST)
         basis = orthonormal(images)
     modes_low = basis.astype(jnp.bfloat16)
     coeffs = jnp.dot(modes_low.T, by_pixel, preferred_element_type=jnp.float32).astype(jnp.bfloat16)
-    removed = jnp.dot(modes_low, coeffs, preferred_element_type=jnp.float32)
-    cleaned_pixels = (by_pixel.astype(jnp.float32) - removed).astype(jnp.bfloat16)
-    cleaned = lax.all_to_all(cleaned_pixels, "chan", split_axis=0, concat_axis=1, tiled=True)
+    spread = jnp.broadcast_to(coeffs[None], (n_chan,) + coeffs.shape)
+    gathered = lax.all_to_all(spread, "chan", 0, 0, tiled=False)
+    all_coeffs = gathered.transpose(1, 0, 2).reshape(coeffs.shape[0], pix_group)
+    me = lax.axis_index("chan")
+    my_modes = lax.dynamic_slice_in_dim(modes_low, me * chans, chans, axis=0)
+    removed = jnp.dot(my_modes, all_coeffs, preferred_element_type=jnp.float32)
+    cleaned = (smoothed.astype(jnp.float32) - removed).astype(jnp.bfloat16)
     return (cleaned, basis)
 
 

time: 302 us -> 201 us (0.67)
  waiting for transfers between devices: 149 us -> 26.7 us
  local copies, waits for them, and re-layouts: 10.1 us -> 26.2 us
  between operations: 14.2 us -> 0.85 us
  starting transfers between devices: 0.04 us -> 9.39 us
  other arithmetic: 20.1 us -> 29.1 us
  blocking collectives: 61.9 us -> 55 us
  matrix products: 46.2 us -> 53 us
    psum x1 -> x0, waiting for transfers between devices: 149 us -> none  [local(): total = lax.psum(partial_value, ('chan', 'pix'))]
    all_to_all x0 -> x2, waiting for transfers between devices: none -> 26.7 us  [the longest x1 14.2 us: sum_all(): return lax.all_to_all(spread, AXES, 0, 0, tiled=False)]
    all_to_all x0 -> x2, starting transfers between devices: none -> 9.39 us  [the longest x1 4.71 us: local(): gathered = lax.all_to_all(spread, 'chan', 0, 0, tiled=False)]
    gather x0 -> x3, local copies, waits for them, and re-layouts: none -> 7.22 us  [the longest x2 4.9 us: symmetric_sum(): picked = summed[kmap]]
    all_to_all x1, blocking collectives: 30 us -> 23.1 us  [sum_all(): got = lax.all_to_all(pieces, AXES, 0, 0, tiled=False)]
    dot_general x1 -> x2, matrix products: 2.35 us -> 8.45 us  [the longest x1 6.4 us: local(): removed = jnp.dot(my_modes, all_coeffs, preferred_element_type=jnp.float32)]
    div x0 -> x2, local copies, waits for them, and re-layouts: none -> 4.82 us  [local(): gram = total / all_pixels]
    div x0 -> x1, other arithmetic: none -> 3.81 us  [local(): gram = total / all_pixels]
  transfers between devices with their start and end apart: 1 -> 2, of which waited for: 1 -> 2; matrix products, arithmetic and copies ran while one was open for 0% -> 1% of each run, Pallas kernels for 0% -> 0%
where the time goes in v1:
time: 201 us; the launch traced here: 200 us
  blocking collectives  55 us (27%)
  matrix products  53 us (26%)
  other arithmetic  29.1 us (14%)
  waiting for transfers between devices  26.7 us (13%)
  local copies, waits for them, and re-layouts  26.2 us (13%)
  starting transfers between devices  9.39 us (5%)
    all_to_all x1, blocking collectives, local(): lax.all_to_all(smoothed, 'chan', split_axis=1, concat_axis=0, tiled=True)  31.9 us
    all_to_all x1, blocking collectives, sum_all(): got = lax.all_to_all(pieces, AXES, 0, 0, tiled=False)  23.1 us
    dot_general x1, matrix products, local(): jnp.einsum('cbkn,cnj->cbkj', selector, blocks, preferred_element_type=jnp...  20.5 us
    dot_general x1, matrix products, local(): jnp.einsum('cbkj,ckij->cbi', sources, beam_blocks, preferred_element_type...  15.1 us
    all_to_all x1, waiting for transfers between devices, sum_all(): return lax.all_to_all(spread, AXES, 0, 0, tiled=False)  14.2 us
    all_to_all x1, waiting for transfers between devices, local(): gathered = lax.all_to_all(spread, 'chan', 0, 0, tiled=False)  12.5 us
    another operation x9, other arithmetic, orthonormal(): factor = jnp.linalg.cholesky(square)  10.8 us
    another operation x6, other arithmetic, orthonormal(): lax.linalg.triangular_solve(factor, images, left_side=False, lower=True,...  9.26 us
  transfers between devices with their start and end apart: 2, of which 2 were waited for; matrix products, arithmetic and copies ran while one was open for 1% of the time, Pallas kernels for 0%

profile of v1, /device:TPU:1, one launch (start us, length us, event | category | flops | bytes accessed | tf_op | source)
XLA Modules:
  0.0 200.2 jit_solution(10440474436983871851)
XLA Ops:
  3.1 20.5 %fusion.65 = bf16[64,128,9,128]{3,1,2,0:T(8,128)(2,1)} fusion(s32[64,128,9]{1,2,0:T(8,128)S(1)} %copy.32, bf16[64,128,128,1]{2,1,0,3:T(8,128)(2,1)S(1)} %bitcast.111), kind=kOutput, calls=%fused_computation.5.clone.clone.clone.1 | convolution fusion | flops 2434793472 | bytes 21266432 | tf_op jit(solution)/shard_map/cbkn,cnj->cbkj/dot_general | solution.py:59
  23.6 15.1 %bitcast_convert_fusion = bf16[64,128,128]{2,1,0:T(8,128)(2,1)S(1)} fusion(bf16[64,9,128,128]{3,2,1,0:T(8,128)(2,1)} %param.15, bf16[64,128,9,128]{3,1,2,0:T(8,128)(2,1)} %fusion.65), kind=kOutput, calls=%fused_computation.9 | convolution fusion | flops 2416967680 | bytes 39845888 | tf_op jit(solution)/shard_map/cbkj,ckij->cbi/dot_general | solution.py:62
  38.7 2.3 %all_to_all.27 = bf16[64,8,2048]{2,1,0:T(8,128)(2,1)} reshape(bf16[64,128,128]{2,1,0:T(8,128)(2,1)S(1)} %bitcast_convert_fusion) | data formatting | bytes 4194304 | tf_op jit(solution)/shard_map/all_to_all | solution.py:66
  41.0 2.7 %copy.33 = bf16[64,8,2048]{2,0,1:T(8,128)(2,1)S(1)} copy(bf16[64,8,2048]{2,1,0:T(8,128)(2,1)} %all_to_all.27) | data formatting | bytes 4194304 | tf_op jit(solution)/shard_map/all_to_all | solution.py:66
  43.7 31.9 %all_to_all.40 = bf16[64,8,2048]{2,0,1:T(8,128)(2,1)S(1)} all-to-all(bf16[64,8,2048]{2,0,1:T(8,128)(2,1)S(1)} %copy.33), channel_id=1, replica_groups=mesh['chan'=8,'pix'=16] {'chan'}, dimensions={1} | all-to-all | bytes 4194304 | tf_op jit(solution)/shard_map/all_to_all | solution.py:66
  77.0 3.7 %fusion.13 = f32[8,8,64,64]{3,2,1,0:T(8,128)} fusion(bf16[64,8,2048]{2,0,1:T(8,128)(2,1)S(1)} %all_to_all.40), kind=kOutput, calls=%fused_computation.17 | convolution fusion | flops 1073741824 | bytes 3145728 | tf_op jit(solution)/shard_map/dot_general | solution.py:70
  80.7 2.3 %gather_fusion = f32[36,64,64]{2,1,0:T(8,128)S(1)} fusion(f32[8,8,64,64]{3,2,1,0:T(8,128)} %fusion.13, s32[36]{0:T(128)S(1)} %copy-done.2), kind=kCustom, calls=%fused_computation | custom fusion | bytes 1179936 | tf_op jit(solution)/shard_map/gather | solution.py:35
  84.5 23.1 %all_to_all.41 = f32[128,1,1152]{2,1,0:T(1,128)S(1)} all-to-all(f32[128,1,1152]{2,1,0:T(1,128)} %all_to_all.35), channel_id=1, replica_groups=mesh['chan'=8,'pix'=16] {'chan','pix'}, dimensions={0} | all-to-all | bytes 1179648 | tf_op jit(solution)/shard_map/all_to_all | solution.py:22
  109.1 4.7 %all-to-all-start.2 = ((f32[128,1,1152]{2,1,0:T(1,128)}), f32[128,1,1152]{2,1,0:T(1,128)S(1)}, u32[]{:S(2)}, u32[]{:S(2)}) async-start(f32[128,1,1152]{2,1,0:T(1,128)} %broadcast_in_dim.37), calls=%async_computation.2 | async-start | bytes 1179648 | tf_op jit(solution)/shard_map/all_to_all | solution.py:25
  113.8 14.2 %all-to-all-done.2 = f32[128,1,1152]{2,1,0:T(1,128)S(1)} async-done(((f32[128,1,1152]{2,1,0:T(1,128)}), f32[128,1,1152]{2,1,0:T(1,128)S(1)}, u32[]{:S(2)}, u32[]{:S(2)}) %all-to-all-start.2) | async-done | bytes 589856 | tf_op jit(solution)/shard_map/all_to_all | solution.py:25
  128.0 2.3 %reduce.5 = f32[128,1152]{1,0:T(8,128)} reduce(f32[128,1,1152]{2,1,0:T(1,128)S(1)} %all-to-all-done.2, f32[]{:T(128)} %constant.94), dimensions={1}, to_apply=%all_to_all.32.reduce_sub_computation | reduce | bytes 1179652 | tf_op jit(solution)/shard_map/all_to_all | solution.py:25
  133.7 2.9 %copy.35 = f32[8,8,64,64]{2,3,1,0:T(8,128)} copy(f32[8,8,64,64]{3,2,1,0:T(8,128)} %bitcast.105) | data formatting | bytes 2097152 | tf_op jit(solution)/shard_map/gather | solution.py:46
  136.6 3.8 %fusion.10 = f32[8,64,8,64]{1,3,2,0:T(8,128)} fusion(f32[8,64,8,64]{1,3,2,0:T(8,128)} %bitcast.106, f32[8,8,64,64]{2,3,1,0:T(8,128)} %copy.35, pred[8,8]{1,0:T(8,128)(4,1)S(1)} %copy-done.4), kind=kLoop, calls=%fused_computation.15 | loop fusion | flops 524288 | bytes 3145792 | tf_op jit(solution)/shard_map/div | solution.py:72
  140.4 2.9 %copy.36 = f32[8,64,8,64]{3,2,1,0:T(8,128)} copy(f32[8,64,8,64]{1,3,2,0:T(8,128)} %fusion.10) | data formatting | bytes 2097152 | tf_op jit(solution)/shard_map/div | solution.py:72
  146.6 2.9 %cholesky.59 = f32[32,32]{1,0:T(8,128)S(1)} custom-call(f32[32,32]{1,0:T(8,128)S(1)} %fusion.26), custom_call_target="Cholesky" | custom-call | tf_op jit(solution)/shard_map/jit(cholesky)/cholesky | solution.py:14
  150.9 2.4 %custom-call.9 = f32[1,32,32]{1,2,0:T(8,128)S(1)} custom-call(f32[1,32,32]{2,1,0:T(8,128)S(1)} %fusion.18), custom_call_target="InvertDiagBlocksLowerTriangular" | custom-call | tf_op jit(solution)/shard_map/triangular_solve/custom-call.0 | solution.py:15
  155.0 2.9 %cholesky.70 = f32[32,32]{1,0:T(8,128)S(1)} custom-call(f32[32,32]{1,0:T(8,128)S(1)} %fusion.24), custom_call_target="Cholesky" | custom-call | tf_op jit(solution)/shard_map/jit(cholesky)/cholesky | solution.py:14
  159.2 2.4 %custom-call.10 = f32[1,32,32]{1,2,0:T(8,128)S(1)} custom-call(f32[1,32,32]{2,1,0:T(8,128)S(1)} %fusion.19), custom_call_target="InvertDiagBlocksLowerTriangular" | custom-call | tf_op jit(solution)/shard_map/triangular_solve/custom-call.0 | solution.py:15
  163.3 2.9 %cholesky.81 = f32[32,32]{1,0:T(8,128)S(1)} custom-call(f32[32,32]{1,0:T(8,128)S(1)} %fusion.22), custom_call_target="Cholesky" | custom-call | tf_op jit(solution)/shard_map/jit(cholesky)/cholesky | solution.py:14
  167.5 2.4 %custom-call.11 = f32[1,32,32]{1,2,0:T(8,128)S(1)} custom-call(f32[1,32,32]{2,1,0:T(8,128)S(1)} %fusion.20), custom_call_target="InvertDiagBlocksLowerTriangular" | custom-call | tf_op jit(solution)/shard_map/triangular_solve/custom-call.0 | solution.py:15
  174.0 4.7 %all-to-all-start.3 = ((bf16[8,32,2048]{2,1,0:T(8,128)(2,1)}), bf16[8,32,2048]{2,1,0:T(8,128)(2,1)S(1)}, u32[]{:S(2)}, u32[]{:S(2)}) async-start(bf16[8,32,2048]{2,1,0:T(8,128)(2,1)} %broadcast_in_dim.39), calls=%async_computation.3 | async-start | bytes 2097152 | tf_op jit(solution)/shard_map/all_to_all | solution.py:79
  178.8 2.5 %convert.2 = f32[8,8,128,128]{3,2,1,0:T(8,128)} convert(bf16[8,8,128,128]{3,2,1,0:T(8,128)(2,1)S(1)} %bitcast.104) | non-fusion elementwise | flops 1048576 | bytes 6291456
  181.2 12.5 %all-to-all-done.3 = bf16[8,32,2048]{2,1,0:T(8,128)(2,1)S(1)} async-done(((bf16[8,32,2048]{2,1,0:T(8,128)(2,1)}), bf16[8,32,2048]{2,1,0:T(8,128)(2,1)S(1)}, u32[]{:S(2)}, u32[]{:S(2)}) %all-to-all-start.3) | async-done | bytes 1048608 | tf_op jit(solution)/shard_map/all_to_all | solution.py:79
  193.8 6.4 %fusion.4 = bf16[64,16384]{1,0:T(8,128)(2,1)} fusion(bf16[32,16384]{1,0:T(8,128)(2,1)S(1)} %bitcast.109, f32[8,8,128,128]{3,2,1,0:T(8,128)} %convert.2, bf16[512,32]{0,1:T(8,128)(2,1)S(1)} %get-tuple-element.4, s32[]{:T(128)S(6)} %select_n.24), kind=kOutput, calls=%fused_computation.8 | convolution fusion | flops 69206016 | bytes 7348228 | tf_op jit(solution)/shard_map/dot_general | solution.py:83
  (48 shorter events, 24.8 us)
Async XLA Ops:
  0.6 144.6 %copy-start = (f32[512,32]{0,1:T(8,128)S(1)}, f32[512,32]{0,1:T(8,128)}, u32[]{:S(2)}) copy-start(f32[512,32]{0,1:T(8,128)} %param.17) | copy-start | bytes 196612
  0.6 2.2 %copy-start.3 = (s32[64,128,9]{1,0,2:T(8,128)S(1)}, s32[64,128,9]{1,0,2:T(8,128)}, u32[]{:S(2)}) copy-start(s32[64,128,9]{1,0,2:T(8,128)} %param.16) | copy-start | bytes 884740
  75.6 1.4 copy-start.1
  77.0 3.7 %copy-start.2 = (s32[36]{0:T(128)S(1)}, s32[36]{0:T(128)}, u32[]{:S(2)}) copy-start(s32[36]{0:T(128)} %constant.92) | copy-start | bytes 436
  84.5 29.3 %copy-start.5 = (s32[64]{0:T(128)S(1)}, s32[64]{0:T(128)}, u32[]{:S(2)}) copy-start(s32[64]{0:T(128)} %constant.93) | copy-start | bytes 772
  109.1 18.9 %all-to-all-start.2 = ((f32[128,1,1152]{2,1,0:T(1,128)}), f32[128,1,1152]{2,1,0:T(1,128)S(1)}, u32[]{:S(2)}, u32[]{:S(2)}) async-start(f32[128,1,1152]{2,1,0:T(1,128)} %broadcast_in_dim.37), calls=%async_computation.2 | async-start | bytes 1179648 | tf_op jit(solution)/shard_map/all_to_all | solution.py:25
  133.7 2.9 %copy-start.4 = (pred[8,8]{1,0:T(8,128)(4,1)S(1)}, pred[8,8]{1,0:T(8,128)(4,1)}, u32[]{:S(2)}) copy-start(pred[8,8]{1,0:T(8,128)(4,1)} %constant.67) | copy-start | bytes 196
  174.0 19.7 %all-to-all-start.3 = ((bf16[8,32,2048]{2,1,0:T(8,128)(2,1)}), bf16[8,32,2048]{2,1,0:T(8,128)(2,1)S(1)}, u32[]{:S(2)}, u32[]{:S(2)}) async-start(bf16[8,32,2048]{2,1,0:T(8,128)(2,1)} %broadcast_in_dim.39), calls=%async_computation.3 | async-start | bytes 2097152 | tf_op jit(solution)/shard_map/all_to_all | solution.py:79

commit v2 on v0

--- a/solution.py
+++ b/solution.py
@@ -5,6 +5,7 @@
 
 BLK = 128
 ITERS = 3
+AXES = ("chan", "pix")
 
 
 def orthonormal(images):
@@ -13,6 +14,37 @@
     return lax.linalg.triangular_solve(
         factor, images, left_side=False, lower=True, transpose_a=True
     )
+
+
+def sum_all(pieces):
+    n = pieces.shape[0]
+    got = lax.all_to_all(pieces, AXES, 0, 0, tiled=False)
+    mine = jnp.sum(got, axis=0)
+    spread = jnp.broadcast_to(mine[None], (n,) + mine.shape)
+    return lax.all_to_all(spread, AXES, 0, 0, tiled=False)
+
+
+def symmetric_sum(partial, nb, scale):
+    size = partial.shape[0]
+    bs = size // nb
+    rows = []
+    for i in range(nb // 2):
+        k = nb - 1 - i
+        rows.append(jnp.concatenate(
+            [partial[i * bs:(i + 1) * bs, i * bs:], partial[k * bs:(k + 1) * bs, k * bs:]], axis=1))
+    packed = jnp.stack(rows)
+    n = lax.axis_size(AXES)
+    summed = sum_all(packed.reshape(n, -1)).reshape(packed.shape)
+    upper = [None] * nb
+    for i in range(nb // 2):
+        k = nb - 1 - i
+        width = (nb - i) * bs
+        upper[i] = jnp.concatenate([jnp.zeros((bs, i * bs), jnp.float32), summed[i, :, :width]], axis=1)
+        upper[k] = jnp.concatenate([jnp.zeros((bs, k * bs), jnp.float32), summed[i, :, width:]], axis=1)
+    half = jnp.concatenate(upper, axis=0)
+    blk = lax.broadcasted_iota(jnp.int32, (size, size), 0) // bs
+    blk_t = lax.broadcasted_iota(jnp.int32, (size, size), 1) // bs
+    return jnp.where(blk <= blk_t, half, half.T) * scale
 
 
 def local(sky_cube, beam_blocks, pattern, start_modes):
@@ -30,19 +62,23 @@
     ).astype(jnp.bfloat16)
     smoothed = smoothed.reshape(chans, pix_group)
     by_pixel = lax.all_to_all(smoothed, "chan", split_axis=1, concat_axis=0, tiled=True)
+    n_chan = lax.axis_size("chan")
     all_pixels = pix_group * lax.axis_size("pix")
     basis = start_modes
     partial_value = jnp.dot(by_pixel, by_pixel.T, preferred_element_type=jnp.float32)
-    total = lax.psum(partial_value, ("chan", "pix"))
-    gram = total / all_pixels
+    gram = symmetric_sum(partial_value, n_chan, 1.0 / all_pixels)
     for sweep in range(ITERS):
         images = jnp.dot(gram, basis, precision=lax.Precision.HIGHEST)
         basis = orthonormal(images)
     modes_low = basis.astype(jnp.bfloat16)
     coeffs = jnp.dot(modes_low.T, by_pixel, preferred_element_type=jnp.float32).astype(jnp.bfloat16)
-    removed = jnp.dot(modes_low, coeffs, preferred_element_type=jnp.float32)
-    cleaned_pixels = (by_pixel.astype(jnp.float32) - removed).astype(jnp.bfloat16)
-    cleaned = lax.all_to_all(cleaned_pixels, "chan", split_axis=0, concat_axis=1, tiled=True)
+    spread = jnp.broadcast_to(coeffs[None], (n_chan,) + coeffs.shape)
+    gathered = lax.all_to_all(spread, "chan", 0, 0, tiled=False)
+    me = lax.axis_index("chan")
+    my_modes = lax.dynamic_slice_in_dim(modes_low, me * chans, chans, axis=0)
+    removed = jnp.einsum("cm,jmp->cjp", my_modes, gathered, preferred_element_type=jnp.float32)
+    removed = removed.reshape(chans, pix_group)
+    cleaned = (smoothed.astype(jnp.float32) - removed).astype(jnp.bfloat16)
     return (cleaned, basis)
 
 

time: 302 us -> 191 us (0.63)
  waiting for transfers between devices: 149 us -> 26.7 us
  between operations: 14.2 us -> 0.96 us
  local copies, waits for them, and re-layouts: 10.1 us -> 23 us
  other arithmetic: 20.1 us -> 30.1 us
  starting transfers between devices: 0.04 us -> 9.38 us
  blocking collectives: 61.9 us -> 54.8 us
    psum x1 -> x0, waiting for transfers between devices: 149 us -> none  [local(): total = lax.psum(partial_value, ('chan', 'pix'))]
    all_to_all x0 -> x2, waiting for transfers between devices: none -> 26.7 us  [the longest x1 14.2 us: sum_all(): return lax.all_to_all(spread, AXES, 0, 0, tiled=False)]
    all_to_all x0 -> x2, starting transfers between devices: none -> 9.38 us  [the longest x1 4.71 us: local(): gathered = lax.all_to_all(spread, 'chan', 0, 0, tiled=False)]
    all_to_all x1, blocking collectives: 30 us -> 22.9 us  [sum_all(): got = lax.all_to_all(pieces, AXES, 0, 0, tiled=False)]
    squeeze x0 -> x7, local copies, waits for them, and re-layouts: none -> 6.21 us  [the longest x4 3.5 us: symmetric_sum(): summed[i, :, width:]]
    convert_element_type x0 -> x1, other arithmetic: none -> 3.76 us  [local(): cleaned = (smoothed.astype(jnp.float32) - removed).astype(jnp.bfloat16)]
  transfers between devices with their start and end apart: 1 -> 2, of which waited for: 1 -> 2; matrix products, arithmetic and copies ran while one was open for 0% -> 1% of each run, Pallas kernels for 0% -> 0%
where the time goes in v2:
time: 191 us; the launch traced here: 190 us
  blocking collectives  54.8 us (29%)
  matrix products  45 us (24%)
  other arithmetic  30.1 us (16%)
  waiting for transfers between devices  26.7 us (14%)
  local copies, waits for them, and re-layouts  23 us (12%)
  starting transfers between devices  9.38 us (5%)
    all_to_all x1, blocking collectives, local(): lax.all_to_all(smoothed, 'chan', split_axis=1, concat_axis=0, tiled=True)  31.9 us
    all_to_all x1, blocking collectives, sum_all(): got = lax.all_to_all(pieces, AXES, 0, 0, tiled=False)  22.9 us
    dot_general x1, matrix products, local(): jnp.einsum('cbkn,cnj->cbkj', selector, blocks, preferred_element_type=jnp...  20.5 us
    dot_general x1, matrix products, local(): jnp.einsum('cbkj,ckij->cbi', sources, beam_blocks, preferred_element_type...  15.1 us
    all_to_all x1, waiting for transfers between devices, sum_all(): return lax.all_to_all(spread, AXES, 0, 0, tiled=False)  14.2 us
    all_to_all x1, waiting for transfers between devices, local(): gathered = lax.all_to_all(spread, 'chan', 0, 0, tiled=False)  12.5 us
    another operation x9, other arithmetic, orthonormal(): factor = jnp.linalg.cholesky(square)  10.8 us
    another operation x6, other arithmetic, orthonormal(): lax.linalg.triangular_solve(factor, images, left_side=False, lower=True,...  9.26 us
  transfers between devices with their start and end apart: 2, of which 2 were waited for; matrix products, arithmetic and copies ran while one was open for 1% of the time, Pallas kernels for 0%

profile of v2, /device:TPU:1, one launch (start us, length us, event | category | flops | bytes accessed | tf_op | source)
XLA Modules:
  0.0 190.0 jit_solution(18037630466739325279)
XLA Ops:
  0.7 2.2 %copy.29 = bf16[8,8,128,128]{3,2,1,0:T(8,128)(2,1)S(1)} copy(bf16[8,8,128,128]{3,1,2,0:T(8,128)(2,1)} %bitcast.122) | data formatting | bytes 4194304
  3.1 20.5 %fusion.65 = bf16[64,128,9,128]{3,1,2,0:T(8,128)(2,1)} fusion(s32[64,128,9]{1,2,0:T(8,128)S(1)} %copy.18, bf16[64,128,128,1]{2,1,0,3:T(8,128)(2,1)S(1)} %bitcast.123), kind=kOutput, calls=%fused_computation.3.clone.clone.clone.1 | convolution fusion | flops 2434793472 | bytes 21266432 | tf_op jit(solution)/shard_map/cbkn,cnj->cbkj/dot_general | solution.py:57
  23.6 15.1 %bitcast_convert_fusion = bf16[64,128,128]{2,1,0:T(8,128)(2,1)S(1)} fusion(bf16[64,9,128,128]{3,2,1,0:T(8,128)(2,1)} %param.8, bf16[64,128,9,128]{3,1,2,0:T(8,128)(2,1)} %fusion.65), kind=kOutput, calls=%fused_computation.7 | convolution fusion | flops 2416967680 | bytes 39845888 | tf_op jit(solution)/shard_map/cbkj,ckij->cbi/dot_general | solution.py:60
  38.7 2.3 %all_to_all.27 = bf16[64,8,2048]{2,1,0:T(8,128)(2,1)} reshape(bf16[64,128,128]{2,1,0:T(8,128)(2,1)S(1)} %bitcast_convert_fusion) | data formatting | bytes 4194304 | tf_op jit(solution)/shard_map/all_to_all | solution.py:64
  41.0 2.7 %copy.19 = bf16[64,8,2048]{2,0,1:T(8,128)(2,1)S(1)} copy(bf16[64,8,2048]{2,1,0:T(8,128)(2,1)} %all_to_all.27) | data formatting | bytes 4194304 | tf_op jit(solution)/shard_map/all_to_all | solution.py:64
  43.7 31.9 %all_to_all.40 = bf16[64,8,2048]{2,0,1:T(8,128)(2,1)S(1)} all-to-all(bf16[64,8,2048]{2,0,1:T(8,128)(2,1)S(1)} %copy.19), channel_id=1, replica_groups=mesh['chan'=8,'pix'=16] {'chan'}, dimensions={1} | all-to-all | bytes 4194304 | tf_op jit(solution)/shard_map/all_to_all | solution.py:64
  78.3 22.9 %all_to_all.41 = f32[128,1,1152]{2,1,0:T(1,128)S(1)} all-to-all(f32[128,1,1152]{2,1,0:T(1,128)S(1)} %all_to_all.35), channel_id=1, replica_groups=mesh['chan'=8,'pix'=16] {'chan','pix'}, dimensions={0} | all-to-all | bytes 1179648 | tf_op jit(solution)/shard_map/all_to_all | solution.py:21
  102.7 4.7 %all-to-all-start.2 = ((f32[128,1,1152]{2,1,0:T(1,128)}), f32[128,1,1152]{2,1,0:T(1,128)S(1)}, u32[]{:S(2)}, u32[]{:S(2)}) async-start(f32[128,1,1152]{2,1,0:T(1,128)} %broadcast_in_dim.4), calls=%async_computation.2 | async-start | bytes 1179648 | tf_op jit(solution)/shard_map/all_to_all | solution.py:24
  107.4 14.2 %all-to-all-done.2 = f32[128,1,1152]{2,1,0:T(1,128)S(1)} async-done(((f32[128,1,1152]{2,1,0:T(1,128)}), f32[128,1,1152]{2,1,0:T(1,128)S(1)}, u32[]{:S(2)}, u32[]{:S(2)}) %all-to-all-start.2) | async-done | bytes 589856 | tf_op jit(solution)/shard_map/all_to_all | solution.py:24
  121.6 1.4 reduce.5
  131.5 1.4 copy.21
  132.9 1.8 fusion.9
  136.1 2.9 %cholesky.59 = f32[32,32]{1,0:T(8,128)S(1)} custom-call(f32[32,32]{1,0:T(8,128)S(1)} %fusion.19), custom_call_target="Cholesky" | custom-call | tf_op jit(solution)/shard_map/jit(cholesky)/cholesky | solution.py:13
  140.3 2.4 %custom-call.7 = f32[1,32,32]{1,2,0:T(8,128)S(1)} custom-call(f32[1,32,32]{2,1,0:T(8,128)S(1)} %fusion.11), custom_call_target="InvertDiagBlocksLowerTriangular" | custom-call | tf_op jit(solution)/shard_map/triangular_solve/custom-call.0 | solution.py:14
  144.4 2.9 %cholesky.70 = f32[32,32]{1,0:T(8,128)S(1)} custom-call(f32[32,32]{1,0:T(8,128)S(1)} %fusion.17), custom_call_target="Cholesky" | custom-call | tf_op jit(solution)/shard_map/jit(cholesky)/cholesky | solution.py:13
  148.7 2.4 %custom-call.8 = f32[1,32,32]{1,2,0:T(8,128)S(1)} custom-call(f32[1,32,32]{2,1,0:T(8,128)S(1)} %fusion.12), custom_call_target="InvertDiagBlocksLowerTriangular" | custom-call | tf_op jit(solution)/shard_map/triangular_solve/custom-call.0 | solution.py:14
  152.8 2.9 %cholesky.81 = f32[32,32]{1,0:T(8,128)S(1)} custom-call(f32[32,32]{1,0:T(8,128)S(1)} %fusion.15), custom_call_target="Cholesky" | custom-call | tf_op jit(solution)/shard_map/jit(cholesky)/cholesky | solution.py:13
  157.0 2.4 %custom-call.9 = f32[1,32,32]{1,2,0:T(8,128)S(1)} custom-call(f32[1,32,32]{2,1,0:T(8,128)S(1)} %fusion.13), custom_call_target="InvertDiagBlocksLowerTriangular" | custom-call | tf_op jit(solution)/shard_map/triangular_solve/custom-call.0 | solution.py:14
  160.4 2.1 %convolution_convert_fusion = bf16[32,2048]{1,0:T(8,128)(2,1)S(1)} fusion(bf16[512,32]{0,1:T(8,128)(2,1)S(1)} %get-tuple-element.4, bf16[512,2048]{1,0:T(8,128)(2,1)} %bitcast.121), kind=kOutput, calls=%fused_computation.9 | convolution fusion | flops 67174400 | bytes 2260992 | tf_op jit(solution)/shard_map/dot_general | solution.py:74
  163.5 4.7 %all-to-all-start.3 = ((bf16[8,32,2048]{2,1,0:T(8,128)(2,1)}), bf16[8,32,2048]{2,1,0:T(8,128)(2,1)S(1)}, u32[]{:S(2)}, u32[]{:S(2)}) async-start(bf16[8,32,2048]{2,1,0:T(8,128)(2,1)} %broadcast_in_dim.5), calls=%async_computation.3 | async-start | bytes 2097152 | tf_op jit(solution)/shard_map/all_to_all | solution.py:76
  168.2 2.5 %convert.1 = f32[8,8,128,128]{3,2,1,0:T(8,128)} convert(bf16[8,8,128,128]{3,2,1,0:T(8,128)(2,1)S(1)} %bitcast.118) | non-fusion elementwise | flops 1048576 | bytes 6291456
  170.7 12.5 %all-to-all-done.3 = bf16[8,32,2048]{2,1,0:T(8,128)(2,1)S(1)} async-done(((bf16[8,32,2048]{2,1,0:T(8,128)(2,1)}), bf16[8,32,2048]{2,1,0:T(8,128)(2,1)S(1)}, u32[]{:S(2)}, u32[]{:S(2)}) %all-to-all-start.3) | async-done | bytes 1048608 | tf_op jit(solution)/shard_map/all_to_all | solution.py:76
  184.3 1.9 %copy-done.1 = f32[8,8,128,128]{3,2,1,0:T(8,128)S(1)} copy-done((f32[8,8,128,128]{3,2,1,0:T(8,128)S(1)}, f32[8,8,128,128]{3,2,1,0:T(8,128)}, u32[]{:S(2)}) %copy-start.1) | copy-done | bytes 4194328
  186.2 3.8 %fusion.4 = bf16[64,16384]{1,0:T(8,128)(2,1)} fusion(f32[64,16384]{1,0:T(8,128)S(1)} %bitcast.119, f32[8,8,128,128]{3,2,1,0:T(8,128)S(1)} %copy-done.1), kind=kLoop, calls=%fused_computation.6 | loop fusion | flops 2097152 | bytes 10485760 | tf_op jit(solution)/shard_map/convert_element_type | solution.py:81
  (70 shorter events, 24.4 us)
Async XLA Ops:
  0.6 134.1 %copy-start = (f32[512,32]{0,1:T(8,128)S(1)}, f32[512,32]{0,1:T(8,128)}, u32[]{:S(2)}) copy-start(f32[512,32]{0,1:T(8,128)} %param.10) | copy-start | bytes 196612
  0.6 2.2 %copy-start.4 = (s32[64,128,9]{1,0,2:T(8,128)S(1)}, s32[64,128,9]{1,0,2:T(8,128)}, u32[]{:S(2)}) copy-start(s32[64,128,9]{1,0,2:T(8,128)} %param.9) | copy-start | bytes 884740
  75.6 1.3 copy-start.2
  102.7 18.9 %all-to-all-start.2 = ((f32[128,1,1152]{2,1,0:T(1,128)}), f32[128,1,1152]{2,1,0:T(1,128)S(1)}, u32[]{:S(2)}, u32[]{:S(2)}) async-start(f32[128,1,1152]{2,1,0:T(1,128)} %broadcast_in_dim.4), calls=%async_computation.2 | async-start | bytes 1179648 | tf_op jit(solution)/shard_map/all_to_all | solution.py:24
  131.5 1.4 copy-start.3
  163.5 19.7 %all-to-all-start.3 = ((bf16[8,32,2048]{2,1,0:T(8,128)(2,1)}), bf16[8,32,2048]{2,1,0:T(8,128)(2,1)S(1)}, u32[]{:S(2)}, u32[]{:S(2)}) async-start(bf16[8,32,2048]{2,1,0:T(8,128)(2,1)} %broadcast_in_dim.5), calls=%async_computation.3 | async-start | bytes 2097152 | tf_op jit(solution)/shard_map/all_to_all | solution.py:76
  184.0 2.2 %copy-start.1 = (f32[8,8,128,128]{3,2,1,0:T(8,128)S(1)}, f32[8,8,128,128]{3,2,1,0:T(8,128)}, u32[]{:S(2)}) copy-start(f32[8,8,128,128]{3,2,1,0:T(8,128)} %convert.1) | copy-start | bytes 12582916

commit v3 on v2

--- a/solution.py
+++ b/solution.py
@@ -2,10 +2,41 @@
 import jax.numpy as jnp
 from jax import lax
 from jax.sharding import PartitionSpec as P
+from jax.experimental import pallas as pl
 
 BLK = 128
 ITERS = 3
 AXES = ("chan", "pix")
+CT = 4
+
+def smooth_kernel(pat_ref, sky_ref, beam_ref, out_ref):
+    taps = beam_ref.shape[1]
+    nblk = sky_ref.shape[1]
+    lane = lax.broadcasted_iota(jnp.int32, (nblk, nblk), 1)
+    one = jnp.ones((nblk, nblk), jnp.float32)
+    zero = jnp.zeros((nblk, nblk), jnp.float32)
+    for c in range(sky_ref.shape[0]):
+        p = pat_ref[c]
+        sel = jnp.concatenate(
+            [jnp.where(p[:, k:k + 1] == lane, one, zero).astype(jnp.bfloat16) for k in range(taps)], axis=0)
+        src = jnp.dot(sel, sky_ref[c], preferred_element_type=jnp.float32).astype(jnp.bfloat16)
+        lhs = jnp.concatenate([src[k * nblk:(k + 1) * nblk] for k in range(taps)], axis=1)
+        rhs = jnp.concatenate([beam_ref[c, k] for k in range(taps)], axis=1)
+        out = lax.dot_general(lhs, rhs, (((1,), (1,)), ((), ())), preferred_element_type=jnp.float32)
+        out_ref[c] = out.astype(out_ref.dtype)
+
+def smooth(sky3, beam, pattern):
+    chans, nblk, blk = sky3.shape
+    taps = beam.shape[1]
+    return pl.pallas_call(
+        smooth_kernel,
+        out_shape=jax.ShapeDtypeStruct((chans, nblk, blk), jnp.bfloat16),
+        grid=(chans // CT,),
+        in_specs=[pl.BlockSpec((CT, nblk, taps), lambda i: (i, 0, 0)),
+                  pl.BlockSpec((CT, nblk, blk), lambda i: (i, 0, 0)),
+                  pl.BlockSpec((CT, taps, blk, blk), lambda i: (i, 0, 0, 0))],
+        out_specs=pl.BlockSpec((CT, nblk, blk), lambda i: (i, 0, 0)),
+    )(pattern, sky3, beam)
 
 
 def orthonormal(images):
@@ -52,14 +83,7 @@
     pix_group = sky_cube.shape[1]
     block_count = pix_group // BLK
     blocks = sky_cube.reshape(chans, block_count, BLK)
-    block_ids = lax.broadcasted_iota(jnp.int32, (1, 1, 1, block_count), 3)
-    selector = (pattern[:, :, :, None] == block_ids).astype(jnp.bfloat16)
-    sources = jnp.einsum(
-        "cbkn,cnj->cbkj", selector, blocks, preferred_element_type=jnp.float32
-    ).astype(jnp.bfloat16)
-    smoothed = jnp.einsum(
-        "cbkj,ckij->cbi", sources, beam_blocks, preferred_element_type=jnp.float32
-    ).astype(jnp.bfloat16)
+    smoothed = smooth(blocks, beam_blocks, pattern)
     smoothed = smoothed.reshape(chans, pix_group)
     by_pixel = lax.all_to_all(smoothed, "chan", split_axis=1, concat_axis=0, tiled=True)
     n_chan = lax.axis_size("chan")

time: 191 us -> 174 us (0.911)
  matrix products: 45 us -> 7.8 us
  Pallas kernels: 0 us -> 24.1 us
  local copies, waits for them, and re-layouts: 23 us -> 19.4 us
    dot_general x2 -> x0, matrix products: 35.6 us -> none  [the longest x1 20.5 us: local(): jnp.einsum('cbkn,cnj->cbkj', selector, blocks, preferred_element_type=jnp...]
    pallas_call x0 -> x1, Pallas kernels: none -> 24.1 us  [smooth(): pl.pallas_call(smooth_kernel, out_shape=jax.ShapeDtypeStruct((chans, nblk...]
    unnamed x19 -> x21, local copies, waits for them, and re-layouts: 5.55 us -> 9.93 us
    squeeze x4, local copies, waits for them, and re-layouts: 3.5 us -> 0.16 us  [symmetric_sum(): summed[i, :, width:]]
    squeeze x3, local copies, waits for them, and re-layouts: 2.71 us -> 0.03 us  [symmetric_sum(): summed[i, :, :width]]
where the time goes in v3:
time: 174 us; the launch traced here: 173 us
  blocking collectives  54.8 us (31%)
  other arithmetic  30.1 us (17%)
  waiting for transfers between devices  26.7 us (15%)
  Pallas kernels  24.1 us (14%)
  local copies, waits for them, and re-layouts  19.4 us (11%)
  starting transfers between devices  9.38 us (5%)
  matrix products  7.8 us (4%)
    all_to_all x1, blocking collectives, local(): lax.all_to_all(smoothed, 'chan', split_axis=1, concat_axis=0, tiled=True)  31.9 us
    pallas_call x1, Pallas kernels, smooth(): pl.pallas_call(smooth_kernel, out_shape=jax.ShapeDtypeStruct((chans, nblk...  24.1 us
    all_to_all x1, blocking collectives, sum_all(): got = lax.all_to_all(pieces, AXES, 0, 0, tiled=False)  22.9 us
    all_to_all x1, waiting for transfers between devices, sum_all(): return lax.all_to_all(spread, AXES, 0, 0, tiled=False)  14.2 us
    all_to_all x1, waiting for transfers between devices, local(): gathered = lax.all_to_all(spread, 'chan', 0, 0, tiled=False)  12.5 us
    another operation x9, other arithmetic, orthonormal(): factor = jnp.linalg.cholesky(square)  10.8 us
    unnamed x21, local copies, waits for them, and re-layouts  9.93 us
    another operation x6, other arithmetic, orthonormal(): lax.linalg.triangular_solve(factor, images, left_side=False, lower=True,...  9.26 us
  transfers between devices with their start and end apart: 2, of which 2 were waited for; matrix products, arithmetic and copies ran while one was open for 1% of the time, Pallas kernels for 0%

profile of v3, /device:TPU:1, one launch (start us, length us, event | category | flops | bytes accessed | tf_op | source)
XLA Modules:
  0.0 173.3 jit_solution(12868986310206452213)
XLA Ops:
  0.7 3.5 %copy.27 = bf16[8,8,128,128]{3,2,1,0:T(8,128)(2,1)} copy(bf16[8,8,128,128]{3,1,2,0:T(8,128)(2,1)} %bitcast.107) | data formatting | bytes 4194304
  4.2 2.6 %copy.18.pat_ref = s32[64,128,9]{2,1,0:T(8,128)} copy(s32[64,128,9]{1,0,2:T(8,128)S(1)} %copy-done.5) | data formatting | bytes 589824 | tf_op args[2]
  6.8 24.1 %shard_map.59 = bf16[64,128,128]{2,1,0:T(8,128)(2,1)} custom-call(s32[64,128,9]{2,1,0:T(8,128)} %copy.18.pat_ref, bf16[64,128,128]{2,1,0:T(8,128)(2,1)} %bitcast.106, bf16[64,9,128,128]{3,2,1,0:T(8,128)(2,1)} %beam_ref.1), custom_call_target="tpu_custom_call" | custom-call | tf_op jit(solution)/shard_map/pallas_call | solution.py:31
  30.9 2.8 %all_to_all.27 = bf16[64,8,2048]{2,1,0:T(8,128)(2,1)S(1)} reshape(bf16[64,128,128]{2,1,0:T(8,128)(2,1)} %shard_map.59) | data formatting | bytes 4194304 | tf_op jit(solution)/shard_map/all_to_all | solution.py:88
  33.7 1.2 copy.19
  34.9 31.9 %all_to_all.40 = bf16[64,8,2048]{2,0,1:T(8,128)(2,1)S(1)} all-to-all(bf16[64,8,2048]{2,0,1:T(8,128)(2,1)S(1)} %copy.19), channel_id=1, replica_groups=mesh['chan'=8,'pix'=16] {'chan'}, dimensions={1} | all-to-all | bytes 4194304 | tf_op jit(solution)/shard_map/all_to_all | solution.py:88
  66.8 1.3 fusion.23
  69.5 22.9 %all_to_all.41 = f32[128,1,1152]{2,1,0:T(1,128)S(1)} all-to-all(f32[128,1,1152]{2,1,0:T(1,128)S(1)} %all_to_all.35), channel_id=1, replica_groups=mesh['chan'=8,'pix'=16] {'chan','pix'}, dimensions={0} | all-to-all | bytes 1179648 | tf_op jit(solution)/shard_map/all_to_all | solution.py:52
  93.8 4.7 %all-to-all-start.2 = ((f32[128,1,1152]{2,1,0:T(1,128)}), f32[128,1,1152]{2,1,0:T(1,128)S(1)}, u32[]{:S(2)}, u32[]{:S(2)}) async-start(f32[128,1,1152]{2,1,0:T(1,128)} %broadcast_in_dim.4), calls=%async_computation.2 | async-start | bytes 1179648 | tf_op jit(solution)/shard_map/all_to_all | solution.py:55
  98.6 14.2 %all-to-all-done.2 = f32[128,1,1152]{2,1,0:T(1,128)S(1)} async-done(((f32[128,1,1152]{2,1,0:T(1,128)}), f32[128,1,1152]{2,1,0:T(1,128)S(1)}, u32[]{:S(2)}, u32[]{:S(2)}) %all-to-all-start.2) | async-done | bytes 589856 | tf_op jit(solution)/shard_map/all_to_all | solution.py:55
  112.7 1.4 reduce.5
  116.5 1.3 copy.21
  117.8 1.8 %fusion.1 = f32[512,512]{1,0:T(8,128)S(1)} fusion(f32[512,512]{1,0:T(8,128)} %copy-done.3, f32[512,512]{0,1:T(8,128)} %copy.21, s32[512]{0:T(512)S(1)} %get-tuple-element.10, s32[512]{0:T(512)S(1)} %get-tuple-element.11, pred[512]{0:T(512)(128)(4,1)S(1)} %fusion.20), kind=kLoop, calls=%fused_computation.8 | loop fusion | flops 1310720 | bytes 3150336 | tf_op jit(solution)/shard_map/mul | solution.py:78
  121.0 2.9 %cholesky.59 = f32[32,32]{1,0:T(8,128)S(1)} custom-call(f32[32,32]{1,0:T(8,128)S(1)} %fusion.11), custom_call_target="Cholesky" | custom-call | tf_op jit(solution)/shard_map/jit(cholesky)/cholesky | solution.py:44
  125.3 2.4 %custom-call.7 = f32[1,32,32]{1,2,0:T(8,128)S(1)} custom-call(f32[1,32,32]{2,1,0:T(8,128)S(1)} %fusion.3), custom_call_target="InvertDiagBlocksLowerTriangular" | custom-call | tf_op jit(solution)/shard_map/triangular_solve/custom-call.0 | solution.py:45
  129.4 2.9 %cholesky.70 = f32[32,32]{1,0:T(8,128)S(1)} custom-call(f32[32,32]{1,0:T(8,128)S(1)} %fusion.9), custom_call_target="Cholesky" | custom-call | tf_op jit(solution)/shard_map/jit(cholesky)/cholesky | solution.py:44
  133.6 2.4 %custom-call.8 = f32[1,32,32]{1,2,0:T(8,128)S(1)} custom-call(f32[1,32,32]{2,1,0:T(8,128)S(1)} %fusion.4), custom_call_target="InvertDiagBlocksLowerTriangular" | custom-call | tf_op jit(solution)/shard_map/triangular_solve/custom-call.0 | solution.py:45
  137.7 2.9 %cholesky.81 = f32[32,32]{1,0:T(8,128)S(1)} custom-call(f32[32,32]{1,0:T(8,128)S(1)} %fusion.7), custom_call_target="Cholesky" | custom-call | tf_op jit(solution)/shard_map/jit(cholesky)/cholesky | solution.py:44
  141.9 2.4 %custom-call.9 = f32[1,32,32]{1,2,0:T(8,128)S(1)} custom-call(f32[1,32,32]{2,1,0:T(8,128)S(1)} %fusion.5), custom_call_target="InvertDiagBlocksLowerTriangular" | custom-call | tf_op jit(solution)/shard_map/triangular_solve/custom-call.0 | solution.py:45
  146.9 4.7 %all-to-all-start.3 = ((bf16[8,32,2048]{2,1,0:T(8,128)(2,1)}), bf16[8,32,2048]{2,1,0:T(8,128)(2,1)S(1)}, u32[]{:S(2)}, u32[]{:S(2)}) async-start(bf16[8,32,2048]{2,1,0:T(8,128)(2,1)} %broadcast_in_dim.5), calls=%async_computation.3 | async-start | bytes 2097152 | tf_op jit(solution)/shard_map/all_to_all | solution.py:100
  151.6 2.5 %convert.1 = f32[8,8,128,128]{3,2,1,0:T(8,128)} convert(bf16[8,8,128,128]{3,2,1,0:T(8,128)(2,1)S(1)} %bitcast.102) | non-fusion elementwise | flops 1048576 | bytes 6291456
  154.0 12.5 %all-to-all-done.3 = bf16[8,32,2048]{2,1,0:T(8,128)(2,1)S(1)} async-done(((bf16[8,32,2048]{2,1,0:T(8,128)(2,1)}), bf16[8,32,2048]{2,1,0:T(8,128)(2,1)S(1)}, u32[]{:S(2)}, u32[]{:S(2)}) %all-to-all-start.3) | async-done | bytes 1048608 | tf_op jit(solution)/shard_map/all_to_all | solution.py:100
  167.7 1.9 %copy-done.2 = f32[8,8,128,128]{3,2,1,0:T(8,128)S(1)} copy-done((f32[8,8,128,128]{3,2,1,0:T(8,128)S(1)}, f32[8,8,128,128]{3,2,1,0:T(8,128)}, u32[]{:S(2)}) %copy-start.2) | copy-done | bytes 4194328
  169.6 3.8 %fusion = bf16[64,16384]{1,0:T(8,128)(2,1)} fusion(f32[64,16384]{1,0:T(8,128)S(1)} %bitcast.103, f32[8,8,128,128]{3,2,1,0:T(8,128)S(1)} %copy-done.2), kind=kLoop, calls=%fused_computation.1 | loop fusion | flops 2097152 | bytes 10485760 | tf_op jit(solution)/shard_map/convert_element_type | solution.py:105
  (71 shorter events, 17.2 us)
Async XLA Ops:
  0.6 119.0 %copy-start = (f32[512,32]{0,1:T(8,128)S(1)}, f32[512,32]{0,1:T(8,128)}, u32[]{:S(2)}) copy-start(f32[512,32]{0,1:T(8,128)} %param.10) | copy-start | bytes 196612
  0.6 3.6 %copy-start.5 = (s32[64,128,9]{1,0,2:T(8,128)S(1)}, s32[64,128,9]{1,0,2:T(8,128)}, u32[]{:S(2)}) copy-start(s32[64,128,9]{1,0,2:T(8,128)} %param.9) | copy-start | bytes 884740
  93.8 18.9 %all-to-all-start.2 = ((f32[128,1,1152]{2,1,0:T(1,128)}), f32[128,1,1152]{2,1,0:T(1,128)S(1)}, u32[]{:S(2)}, u32[]{:S(2)}) async-start(f32[128,1,1152]{2,1,0:T(1,128)} %broadcast_in_dim.4), calls=%async_computation.2 | async-start | bytes 1179648 | tf_op jit(solution)/shard_map/all_to_all | solution.py:55
  114.3 0.8 copy-start.4
  116.5 1.3 copy-start.3
  145.8 5.8 %copy-start.1 = (bf16[64,128,128]{2,1,0:T(8,128)(2,1)S(1)}, bf16[64,128,128]{2,1,0:T(8,128)(2,1)}, u32[]{:S(2)}) copy-start(bf16[64,128,128]{2,1,0:T(8,128)(2,1)} %shard_map.59) | copy-start | bytes 6291460
  146.9 19.7 %all-to-all-start.3 = ((bf16[8,32,2048]{2,1,0:T(8,128)(2,1)}), bf16[8,32,2048]{2,1,0:T(8,128)(2,1)S(1)}, u32[]{:S(2)}, u32[]{:S(2)}) async-start(bf16[8,32,2048]{2,1,0:T(8,128)(2,1)} %broadcast_in_dim.5), calls=%async_computation.3 | async-start | bytes 2097152 | tf_op jit(solution)/shard_map/all_to_all | solution.py:100
  167.4 2.2 %copy-start.2 = (f32[8,8,128,128]{3,2,1,0:T(8,128)S(1)}, f32[8,8,128,128]{3,2,1,0:T(8,128)}, u32[]{:S(2)}) copy-start(f32[8,8,128,128]{3,2,1,0:T(8,128)} %convert.1) | copy-start | bytes 12582916

commit v4 on v3

--- a/solution.py
+++ b/solution.py
@@ -7,7 +7,7 @@
 BLK = 128
 ITERS = 3
 AXES = ("chan", "pix")
-CT = 4
+CT = 8
 
 def smooth_kernel(pat_ref, sky_ref, beam_ref, out_ref):
     taps = beam_ref.shape[1]
@@ -23,19 +23,19 @@
         lhs = jnp.concatenate([src[k * nblk:(k + 1) * nblk] for k in range(taps)], axis=1)
         rhs = jnp.concatenate([beam_ref[c, k] for k in range(taps)], axis=1)
         out = lax.dot_general(lhs, rhs, (((1,), (1,)), ((), ())), preferred_element_type=jnp.float32)
-        out_ref[c] = out.astype(out_ref.dtype)
+        out_ref[:, c] = out.astype(out_ref.dtype).reshape(out_ref.shape[0], out_ref.shape[2], out_ref.shape[3])
 
-def smooth(sky3, beam, pattern):
+def smooth(sky3, beam, pattern, parts):
     chans, nblk, blk = sky3.shape
     taps = beam.shape[1]
     return pl.pallas_call(
         smooth_kernel,
-        out_shape=jax.ShapeDtypeStruct((chans, nblk, blk), jnp.bfloat16),
+        out_shape=jax.ShapeDtypeStruct((parts, chans, nblk // parts, blk), jnp.bfloat16),
         grid=(chans // CT,),
         in_specs=[pl.BlockSpec((CT, nblk, taps), lambda i: (i, 0, 0)),
                   pl.BlockSpec((CT, nblk, blk), lambda i: (i, 0, 0)),
                   pl.BlockSpec((CT, taps, blk, blk), lambda i: (i, 0, 0, 0))],
-        out_specs=pl.BlockSpec((CT, nblk, blk), lambda i: (i, 0, 0)),
+        out_specs=pl.BlockSpec((parts, CT, nblk // parts, blk), lambda i: (0, i, 0, 0)),
     )(pattern, sky3, beam)
 
 
@@ -83,10 +83,9 @@
     pix_group = sky_cube.shape[1]
     block_count = pix_group // BLK
     blocks = sky_cube.reshape(chans, block_count, BLK)
-    smoothed = smooth(blocks, beam_blocks, pattern)
-    smoothed = smoothed.reshape(chans, pix_group)
-    by_pixel = lax.all_to_all(smoothed, "chan", split_axis=1, concat_axis=0, tiled=True)
     n_chan = lax.axis_size("chan")
+    chunks = smooth(blocks, beam_blocks, pattern, n_chan).reshape(n_chan, chans, pix_group // n_chan)
+    by_pixel = lax.all_to_all(chunks, "chan", 0, 0, tiled=True).reshape(n_chan * chans, pix_group // n_chan)
     all_pixels = pix_group * lax.axis_size("pix")
     basis = start_modes
     partial_value = jnp.dot(by_pixel, by_pixel.T, preferred_element_type=jnp.float32)
@@ -100,9 +99,9 @@
     gathered = lax.all_to_all(spread, "chan", 0, 0, tiled=False)
     me = lax.axis_index("chan")
     my_modes = lax.dynamic_slice_in_dim(modes_low, me * chans, chans, axis=0)
-    removed = jnp.einsum("cm,jmp->cjp", my_modes, gathered, preferred_element_type=jnp.float32)
-    removed = removed.reshape(chans, pix_group)
-    cleaned = (smoothed.astype(jnp.float32) - removed).astype(jnp.bfloat16)
+    removed = jnp.einsum("cm,jmp->jcp", my_modes, gathered, preferred_element_type=jnp.float32)
+    cleaned = (chunks.astype(jnp.float32) - removed).astype(jnp.bfloat16)
+    cleaned = cleaned.transpose(1, 0, 2).reshape(chans, pix_group)
     return (cleaned, basis)
 
 

time: 174 us -> 174 us (level)
  other arithmetic: 30.1 us -> 23.9 us
  local copies, waits for them, and re-layouts: 19.4 us -> 23.3 us
  waiting for transfers between devices: 26.7 us -> 29.2 us
  Pallas kernels: 24.1 us -> 22.2 us
    reshape x1 -> x2, local copies, waits for them, and re-layouts: 0.27 us -> 4.28 us  [the longest x1 2.82 us: local(): smooth(blocks, beam_blocks, pattern, n_chan)]
    all_to_all x2 -> x0, local copies, waits for them, and re-layouts: 3.97 us -> none  [local(): lax.all_to_all(smoothed, 'chan', split_axis=1, concat_axis=0, tiled=True)]
    convert_element_type x1 -> x0, other arithmetic: 3.76 us -> none  [local(): cleaned = (smoothed.astype(jnp.float32) - removed).astype(jnp.bfloat16)]
    squeeze x4, local copies, waits for them, and re-layouts: 0.16 us -> 3.5 us  [symmetric_sum(): summed[i, :, width:]]
    unnamed x21 -> x17, local copies, waits for them, and re-layouts: 9.93 us -> 6.83 us
    squeeze x3, local copies, waits for them, and re-layouts: 0.03 us -> 2.71 us  [symmetric_sum(): summed[i, :, :width]]
    all_to_all x1, waiting for transfers between devices: 12.5 us -> 15 us  [local(): gathered = lax.all_to_all(spread, 'chan', 0, 0, tiled=False)]
    unnamed x1 -> x0, other arithmetic: 2.45 us -> none
  transfers between devices with their start and end apart: 2 -> 2, of which waited for: 2 -> 2; matrix products, arithmetic and copies ran while one was open for 1% -> 0% of each run, Pallas kernels for 0% -> 0%
where the time goes in v4:
time: 174 us; the launch traced here: 173 us
  blocking collectives  54.8 us (31%)
  waiting for transfers between devices  29.2 us (17%)
  other arithmetic  23.9 us (14%)
  local copies, waits for them, and re-layouts  23.3 us (13%)
  Pallas kernels  22.2 us (13%)
  matrix products  9.51 us (5%)
  starting transfers between devices  9.38 us (5%)
    all_to_all x1, blocking collectives, local(): lax.all_to_all(chunks, 'chan', 0, 0, tiled=True)  31.9 us
    all_to_all x1, blocking collectives, sum_all(): got = lax.all_to_all(pieces, AXES, 0, 0, tiled=False)  22.9 us
    pallas_call x1, Pallas kernels, smooth(): pl.pallas_call(smooth_kernel, out_shape=jax.ShapeDtypeStruct((parts, chan...  22.2 us
    all_to_all x1, waiting for transfers between devices, local(): gathered = lax.all_to_all(spread, 'chan', 0, 0, tiled=False)  15 us
    all_to_all x1, waiting for transfers between devices, sum_all(): return lax.all_to_all(spread, AXES, 0, 0, tiled=False)  14.2 us
    another operation x9, other arithmetic, orthonormal(): factor = jnp.linalg.cholesky(square)  10.8 us
    another operation x6, other arithmetic, orthonormal(): lax.linalg.triangular_solve(factor, images, left_side=False, lower=True,...  9.26 us
    unnamed x17, local copies, waits for them, and re-layouts  6.83 us
  transfers between devices with their start and end apart: 2, of which 2 were waited for; matrix products, arithmetic and copies ran while one was open for 0% of the time, Pallas kernels for 0%

profile of v4, /device:TPU:1, one launch (start us, length us, event | category | flops | bytes accessed | tf_op | source)
XLA Modules:
  0.0 173.1 jit_solution(12107911850473922665)
XLA Ops:
  0.7 3.7 %copy.17.pat_ref = s32[64,128,9]{2,1,0:T(8,128)} copy(s32[64,128,9]{1,0,2:T(8,128)} %param.9) | data formatting | bytes 589824 | tf_op args[2]
  4.3 1.9 %copy.25 = bf16[8,8,128,128]{3,2,1,0:T(8,128)(2,1)} copy(bf16[8,8,128,128]{3,1,2,0:T(8,128)(2,1)S(1)} %bitcast.106) | data formatting | bytes 4194304
  6.2 22.2 %shard_map.59 = bf16[8,64,16,128]{3,2,1,0:T(8,128)(2,1)} custom-call(s32[64,128,9]{2,1,0:T(8,128)} %copy.17.pat_ref, bf16[64,128,128]{2,1,0:T(8,128)(2,1)} %bitcast.105, bf16[64,9,128,128]{3,2,1,0:T(8,128)(2,1)} %beam_ref.1), custom_call_target="tpu_custom_call" | custom-call | tf_op jit(solution)/shard_map/pallas_call | solution.py:31
  28.4 2.8 %reshape.43 = bf16[8,64,2048]{2,1,0:T(8,128)(2,1)S(1)} reshape(bf16[8,64,16,128]{3,2,1,0:T(8,128)(2,1)} %shard_map.59) | data formatting | bytes 4194304 | tf_op jit(solution)/shard_map/reshape | solution.py:87
  31.2 31.9 %all_to_all.26 = bf16[8,64,2048]{2,1,0:T(8,128)(2,1)S(1)} all-to-all(bf16[8,64,2048]{2,1,0:T(8,128)(2,1)S(1)} %reshape.43), channel_id=1, replica_groups=mesh['chan'=8,'pix'=16] {'chan'}, dimensions={0} | all-to-all | bytes 4194304 | tf_op jit(solution)/shard_map/all_to_all | solution.py:88
  63.2 1.3 fusion.24
  65.8 22.9 %all_to_all.27 = f32[128,1,1152]{2,1,0:T(1,128)S(1)} all-to-all(f32[128,1,1152]{2,1,0:T(1,128)S(1)} %all_to_all.21), channel_id=1, replica_groups=mesh['chan'=8,'pix'=16] {'chan','pix'}, dimensions={0} | all-to-all | bytes 1179648 | tf_op jit(solution)/shard_map/all_to_all | solution.py:52
  89.1 1.1 broadcast_in_dim.4
  90.2 4.7 %all-to-all-start.2 = ((f32[128,1,1152]{2,1,0:T(1,128)}), f32[128,1,1152]{2,1,0:T(1,128)S(1)}, u32[]{:S(2)}, u32[]{:S(2)}) async-start(f32[128,1,1152]{2,1,0:T(1,128)} %broadcast_in_dim.4), calls=%async_computation.2 | async-start | bytes 1179648 | tf_op jit(solution)/shard_map/all_to_all | solution.py:55
  94.9 14.2 %all-to-all-done.2 = f32[128,1,1152]{2,1,0:T(1,128)S(1)} async-done(((f32[128,1,1152]{2,1,0:T(1,128)}), f32[128,1,1152]{2,1,0:T(1,128)S(1)}, u32[]{:S(2)}, u32[]{:S(2)}) %all-to-all-start.2) | async-done | bytes 589856 | tf_op jit(solution)/shard_map/all_to_all | solution.py:55
  109.1 1.4 reduce.5
  119.0 1.4 copy.19
  120.4 1.8 %fusion.2 = f32[512,512]{1,0:T(8,128)S(1)} fusion(f32[512,512]{1,0:T(8,128)} %copy-done.2, f32[512,512]{0,1:T(8,128)} %copy.19, s32[512]{0:T(512)S(1)} %get-tuple-element.10, s32[512]{0:T(512)S(1)} %get-tuple-element.11, pred[512]{0:T(512)(128)(4,1)S(1)} %fusion.21), kind=kLoop, calls=%fused_computation.8 | loop fusion | flops 1310720 | bytes 3150336 | tf_op jit(solution)/shard_map/mul | solution.py:78
  123.6 2.9 %cholesky.59 = f32[32,32]{1,0:T(8,128)S(1)} custom-call(f32[32,32]{1,0:T(8,128)S(1)} %fusion.12), custom_call_target="Cholesky" | custom-call | tf_op jit(solution)/shard_map/jit(cholesky)/cholesky | solution.py:44
  127.9 2.4 %custom-call.7 = f32[1,32,32]{1,2,0:T(8,128)S(1)} custom-call(f32[1,32,32]{2,1,0:T(8,128)S(1)} %fusion.4), custom_call_target="InvertDiagBlocksLowerTriangular" | custom-call | tf_op jit(solution)/shard_map/triangular_solve/custom-call.0 | solution.py:45
  131.9 2.9 %cholesky.70 = f32[32,32]{1,0:T(8,128)S(1)} custom-call(f32[32,32]{1,0:T(8,128)S(1)} %fusion.10), custom_call_target="Cholesky" | custom-call | tf_op jit(solution)/shard_map/jit(cholesky)/cholesky | solution.py:44
  136.2 2.4 %custom-call.8 = f32[1,32,32]{1,2,0:T(8,128)S(1)} custom-call(f32[1,32,32]{2,1,0:T(8,128)S(1)} %fusion.5), custom_call_target="InvertDiagBlocksLowerTriangular" | custom-call | tf_op jit(solution)/shard_map/triangular_solve/custom-call.0 | solution.py:45
  140.3 2.9 %cholesky.81 = f32[32,32]{1,0:T(8,128)S(1)} custom-call(f32[32,32]{1,0:T(8,128)S(1)} %fusion.8), custom_call_target="Cholesky" | custom-call | tf_op jit(solution)/shard_map/jit(cholesky)/cholesky | solution.py:44
  144.5 2.4 %custom-call.9 = f32[1,32,32]{1,2,0:T(8,128)S(1)} custom-call(f32[1,32,32]{2,1,0:T(8,128)S(1)} %fusion.6), custom_call_target="InvertDiagBlocksLowerTriangular" | custom-call | tf_op jit(solution)/shard_map/triangular_solve/custom-call.0 | solution.py:45
  147.9 2.0 %convolution_convert_fusion = bf16[32,2048]{1,0:T(8,128)(2,1)S(1)} fusion(bf16[512,32]{0,1:T(8,128)(2,1)S(1)} %get-tuple-element.4, bf16[512,2048]{1,0:T(8,128)(2,1)} %bitcast.104), kind=kOutput, calls=%fused_computation.3 | convolution fusion | flops 67174400 | bytes 2260992 | tf_op jit(solution)/shard_map/dot_general | solution.py:97
  149.9 1.1 broadcast_in_dim.5
  151.0 4.7 %all-to-all-start.3 = ((bf16[8,32,2048]{2,1,0:T(8,128)(2,1)}), bf16[8,32,2048]{2,1,0:T(8,128)(2,1)S(1)}, u32[]{:S(2)}, u32[]{:S(2)}) async-start(bf16[8,32,2048]{2,1,0:T(8,128)(2,1)} %broadcast_in_dim.5), calls=%async_computation.3 | async-start | bytes 2097152 | tf_op jit(solution)/shard_map/all_to_all | solution.py:99
  155.7 15.0 %all-to-all-done.3 = bf16[8,32,2048]{2,1,0:T(8,128)(2,1)S(1)} async-done(((bf16[8,32,2048]{2,1,0:T(8,128)(2,1)}), bf16[8,32,2048]{2,1,0:T(8,128)(2,1)S(1)}, u32[]{:S(2)}, u32[]{:S(2)}) %all-to-all-start.3) | async-done | bytes 1048608 | tf_op jit(solution)/shard_map/all_to_all | solution.py:99
  171.7 1.5 copy.24
  (64 shorter events, 20.6 us)
Async XLA Ops:
  0.6 121.6 %copy-start = (f32[512,32]{0,1:T(8,128)S(1)}, f32[512,32]{0,1:T(8,128)}, u32[]{:S(2)}) copy-start(f32[512,32]{0,1:T(8,128)} %param.10) | copy-start | bytes 196612
  0.6 3.7 %copy-start.3 = (bf16[64,16384]{1,0:T(8,128)(2,1)S(1)}, bf16[64,16384]{1,0:T(8,128)(2,1)}, u32[]{:S(2)}) copy-start(bf16[64,16384]{1,0:T(8,128)(2,1)} %param.7) | copy-start | bytes 6291460
  63.2 1.3 copy-start.1
  90.2 18.9 %all-to-all-start.2 = ((f32[128,1,1152]{2,1,0:T(1,128)}), f32[128,1,1152]{2,1,0:T(1,128)S(1)}, u32[]{:S(2)}, u32[]{:S(2)}) async-start(f32[128,1,1152]{2,1,0:T(1,128)} %broadcast_in_dim.4), calls=%async_computation.2 | async-start | bytes 1179648 | tf_op jit(solution)/shard_map/all_to_all | solution.py:55
  119.0 1.4 copy-start.2
  151.0 19.7 %all-to-all-start.3 = ((bf16[8,32,2048]{2,1,0:T(8,128)(2,1)}), bf16[8,32,2048]{2,1,0:T(8,128)(2,1)S(1)}, u32[]{:S(2)}, u32[]{:S(2)}) async-start(bf16[8,32,2048]{2,1,0:T(8,128)(2,1)} %broadcast_in_dim.5), calls=%async_computation.3 | async-start | bytes 2097152 | tf_op jit(solution)/shard_map/all_to_all | solution.py:99

commit v5 on v4

--- a/solution.py
+++ b/solution.py
@@ -12,11 +12,14 @@
 def smooth_kernel(pat_ref, sky_ref, beam_ref, out_ref):
     taps = beam_ref.shape[1]
     nblk = sky_ref.shape[1]
-    lane = lax.broadcasted_iota(jnp.int32, (nblk, nblk), 1)
+    lane = lax.broadcasted_iota(jnp.int32, (nblk, nblk), 1).astype(jnp.float32)
+    row = lax.broadcasted_iota(jnp.int32, (nblk, nblk), 0)
+    eye = jnp.where(row == lax.broadcasted_iota(jnp.int32, (nblk, nblk), 1), 1.0, 0.0).astype(jnp.bfloat16)
     one = jnp.ones((nblk, nblk), jnp.float32)
     zero = jnp.zeros((nblk, nblk), jnp.float32)
     for c in range(sky_ref.shape[0]):
-        p = pat_ref[c]
+        p = pat_ref[:, c, :].astype(jnp.float32).astype(jnp.bfloat16)
+        p = lax.dot_general(eye, p, (((1,), (1,)), ((), ())), preferred_element_type=jnp.float32)
         sel = jnp.concatenate(
             [jnp.where(p[:, k:k + 1] == lane, one, zero).astype(jnp.bfloat16) for k in range(taps)], axis=0)
         src = jnp.dot(sel, sky_ref[c], preferred_element_type=jnp.float32).astype(jnp.bfloat16)
@@ -28,15 +31,16 @@
 def smooth(sky3, beam, pattern, parts):
     chans, nblk, blk = sky3.shape
     taps = beam.shape[1]
+    pat_t = jnp.transpose(pattern, (2, 0, 1))
     return pl.pallas_call(
         smooth_kernel,
         out_shape=jax.ShapeDtypeStruct((parts, chans, nblk // parts, blk), jnp.bfloat16),
         grid=(chans // CT,),
-        in_specs=[pl.BlockSpec((CT, nblk, taps), lambda i: (i, 0, 0)),
+        in_specs=[pl.BlockSpec((taps, CT, nblk), lambda i: (0, i, 0)),
                   pl.BlockSpec((CT, nblk, blk), lambda i: (i, 0, 0)),
                   pl.BlockSpec((CT, taps, blk, blk), lambda i: (i, 0, 0, 0))],
         out_specs=pl.BlockSpec((parts, CT, nblk // parts, blk), lambda i: (0, i, 0, 0)),
-    )(pattern, sky3, beam)
+    )(pat_t, sky3, beam)
 
 
 def orthonormal(images):
@@ -66,12 +70,16 @@
     packed = jnp.stack(rows)
     n = lax.axis_size(AXES)
     summed = sum_all(packed.reshape(n, -1)).reshape(packed.shape)
-    upper = [None] * nb
-    for i in range(nb // 2):
-        k = nb - 1 - i
-        width = (nb - i) * bs
-        upper[i] = jnp.concatenate([jnp.zeros((bs, i * bs), jnp.float32), summed[i, :, :width]], axis=1)
-        upper[k] = jnp.concatenate([jnp.zeros((bs, k * bs), jnp.float32), summed[i, :, width:]], axis=1)
+    lead = (nb // 2 - 1) * bs
+    padded = jnp.pad(summed, ((0, 0), (0, 0), (lead, 0)))
+    width = padded.shape[2]
+    upper = []
+    for r in range(nb):
+        if r < nb // 2:
+            start = lead - r * bs
+            upper.append(padded[r, :, start:start + size])
+        else:
+            upper.append(padded[nb - 1 - r, :, width - size:])
     half = jnp.concatenate(upper, axis=0)
     blk = lax.broadcasted_iota(jnp.int32, (size, size), 0) // bs
     blk_t = lax.broadcasted_iota(jnp.int32, (size, size), 1) // bs
@@ -84,24 +92,26 @@
     block_count = pix_group // BLK
     blocks = sky_cube.reshape(chans, block_count, BLK)
     n_chan = lax.axis_size("chan")
-    chunks = smooth(blocks, beam_blocks, pattern, n_chan).reshape(n_chan, chans, pix_group // n_chan)
-    by_pixel = lax.all_to_all(chunks, "chan", 0, 0, tiled=True).reshape(n_chan * chans, pix_group // n_chan)
+    chunks = smooth(blocks, beam_blocks, pattern, n_chan)
+    by_pixel = lax.all_to_all(chunks, "chan", 0, 0, tiled=True)
+    by_pixel = by_pixel.reshape((n_chan * chans,) + by_pixel.shape[2:])
     all_pixels = pix_group * lax.axis_size("pix")
     basis = start_modes
-    partial_value = jnp.dot(by_pixel, by_pixel.T, preferred_element_type=jnp.float32)
+    partial_value = lax.dot_general(
+        by_pixel, by_pixel, (((1, 2), (1, 2)), ((), ())), preferred_element_type=jnp.float32)
     gram = symmetric_sum(partial_value, n_chan, 1.0 / all_pixels)
     for sweep in range(ITERS):
         images = jnp.dot(gram, basis, precision=lax.Precision.HIGHEST)
         basis = orthonormal(images)
     modes_low = basis.astype(jnp.bfloat16)
-    coeffs = jnp.dot(modes_low.T, by_pixel, preferred_element_type=jnp.float32).astype(jnp.bfloat16)
+    coeffs = jnp.einsum("cm,cbi->mbi", modes_low, by_pixel, preferred_element_type=jnp.float32).astype(jnp.bfloat16)
     spread = jnp.broadcast_to(coeffs[None], (n_chan,) + coeffs.shape)
     gathered = lax.all_to_all(spread, "chan", 0, 0, tiled=False)
     me = lax.axis_index("chan")
     my_modes = lax.dynamic_slice_in_dim(modes_low, me * chans, chans, axis=0)
-    removed = jnp.einsum("cm,jmp->jcp", my_modes, gathered, preferred_element_type=jnp.float32)
-    cleaned = (chunks.astype(jnp.float32) - removed).astype(jnp.bfloat16)
-    cleaned = cleaned.transpose(1, 0, 2).reshape(chans, pix_group)
+    removed = jnp.einsum("cm,jmbi->cjbi", my_modes, gathered, preferred_element_type=jnp.float32)
+    cleaned = (chunks.transpose(1, 0, 2, 3).astype(jnp.float32) - removed).astype(jnp.bfloat16)
+    cleaned = cleaned.reshape(chans, pix_group)
     return (cleaned, basis)
 
 

time: 174 us -> 182 us (1.046)
  Pallas kernels: 22.2 us -> 34.1 us
  local copies, waits for them, and re-layouts: 23.3 us -> 19 us
  other arithmetic: 23.9 us -> 26.7 us
    pallas_call x1, Pallas kernels: 22.2 us -> 34.1 us  [smooth(): pl.pallas_call(smooth_kernel, out_shape=jax.ShapeDtypeStruct((parts, chan...]
    squeeze x7 -> x0, local copies, waits for them, and re-layouts: 6.21 us -> none  [the longest x4 3.5 us: symmetric_sum(): summed[i, :, width:]]
    unnamed x17 -> x13, local copies, waits for them, and re-layouts: 6.83 us -> 11.4 us
    reshape x2 -> x0, local copies, waits for them, and re-layouts: 4.28 us -> none  [the longest x1 2.82 us: local(): smooth(blocks, beam_blocks, pattern, n_chan)]
    convert_element_type x0 -> x1, other arithmetic: none -> 2.8 us  [local(): (chunks.transpose(1, 0, 2, 3).astype(jnp.float32) - removed).astype(jnp.b...]
    concatenate x2, local copies, waits for them, and re-layouts: 1.45 us -> 3.3 us  [symmetric_sum(): half = jnp.concatenate(upper, axis=0)]
where the time goes in v5:
time: 182 us
  blocking collectives  55 us (30%)
  Pallas kernels  34.1 us (19%)
  waiting for transfers between devices  29.2 us (16%)
  other arithmetic  26.7 us (15%)
  local copies, waits for them, and re-layouts  19 us (10%)
  starting transfers between devices  9.38 us (5%)
  matrix products  7.83 us (4%)
    pallas_call x1, Pallas kernels, smooth(): pl.pallas_call(smooth_kernel, out_shape=jax.ShapeDtypeStruct((parts, chan...  34.1 us
    all_to_all x1, blocking collectives, local(): by_pixel = lax.all_to_all(chunks, 'chan', 0, 0, tiled=True)  32.1 us
    all_to_all x1, blocking collectives, sum_all(): got = lax.all_to_all(pieces, AXES, 0, 0, tiled=False)  22.9 us
    all_to_all x1, waiting for transfers between devices, local(): gathered = lax.all_to_all(spread, 'chan', 0, 0, tiled=False)  15 us
    all_to_all x1, waiting for transfers between devices, sum_all(): return lax.all_to_all(spread, AXES, 0, 0, tiled=False)  14.2 us
    unnamed x13, local copies, waits for them, and re-layouts  11.4 us
    another operation x9, other arithmetic, orthonormal(): factor = jnp.linalg.cholesky(square)  10.8 us
    another operation x6, other arithmetic, orthonormal(): lax.linalg.triangular_solve(factor, images, left_side=False, lower=True,...  9.26 us
  transfers between devices with their start and end apart: 2, of which 2 were waited for; matrix products, arithmetic and copies ran while one was open for 0% of the time, Pallas kernels for 0%

profile of v5, /device:TPU:1, one launch (start us, length us, event | category | flops | bytes accessed | tf_op | source)
XLA Modules:
  0.0 182.1 jit_solution(3072860910070116684)
XLA Ops:
  0.6 3.5 %copy.32 = bf16[8,8,128,128]{3,2,1,0:T(8,128)(2,1)} copy(bf16[8,8,128,128]{3,1,2,0:T(8,128)(2,1)} %bitcast.122) | data formatting | bytes 4194304
  4.2 34.1 %shard_map.59 = bf16[8,64,16,128]{3,2,1,0:T(8,128)(2,1)} custom-call(s32[9,64,128]{2,1,0:T(8,128)} %bitcast.124, bf16[64,128,128]{2,1,0:T(8,128)(2,1)} %bitcast.118, bf16[64,9,128,128]{3,2,1,0:T(8,128)(2,1)} %beam_ref.1), custom_call_target="tpu_custom_call" | custom-call | tf_op jit(solution)/shard_map/pallas_call | solution.py:35
  38.2 32.1 %all_to_all.26 = bf16[8,64,16,128]{3,2,1,0:T(8,128)(2,1)S(1)} all-to-all(bf16[8,64,16,128]{3,2,1,0:T(8,128)(2,1)} %shard_map.59), channel_id=1, replica_groups=mesh['chan'=8,'pix'=16] {'chan'}, dimensions={0} | all-to-all | bytes 4194304 | tf_op jit(solution)/shard_map/all_to_all | solution.py:96
  70.4 1.3 fusion.5
  73.0 22.9 %all_to_all.27 = f32[128,1,1152]{2,1,0:T(1,128)S(1)} all-to-all(f32[128,1,1152]{2,1,0:T(1,128)S(1)} %all_to_all.21), channel_id=1, replica_groups=mesh['chan'=8,'pix'=16] {'chan','pix'}, dimensions={0} | all-to-all | bytes 1179648 | tf_op jit(solution)/shard_map/all_to_all | solution.py:56
  96.3 1.1 broadcast_in_dim.4
  97.4 4.7 %all-to-all-start.2 = ((f32[128,1,1152]{2,1,0:T(1,128)}), f32[128,1,1152]{2,1,0:T(1,128)S(1)}, u32[]{:S(2)}, u32[]{:S(2)}) async-start(f32[128,1,1152]{2,1,0:T(1,128)} %broadcast_in_dim.4), calls=%async_computation.2 | async-start | bytes 1179648 | tf_op jit(solution)/shard_map/all_to_all | solution.py:59
  102.1 14.2 %all-to-all-done.2 = f32[128,1,1152]{2,1,0:T(1,128)S(1)} async-done(((f32[128,1,1152]{2,1,0:T(1,128)}), f32[128,1,1152]{2,1,0:T(1,128)S(1)}, u32[]{:S(2)}, u32[]{:S(2)}) %all-to-all-start.2) | async-done | bytes 589856 | tf_op jit(solution)/shard_map/all_to_all | solution.py:59
  116.3 1.4 reduce.5
  123.7 2.5 %copy.24 = f32[512,512]{0,1:T(8,128)} copy(f32[512,512]{1,0:T(8,128)} %fusion.18) | data formatting | bytes 2097152 | tf_op jit(solution)/shard_map/concatenate | solution.py:83
  126.3 1.8 fusion.11
  128.1 1.1 fusion.45
  129.5 2.9 %cholesky.59 = f32[32,32]{1,0:T(8,128)S(1)} custom-call(f32[32,32]{1,0:T(8,128)S(1)} %fusion.32), custom_call_target="Cholesky" | custom-call | tf_op jit(solution)/shard_map/jit(cholesky)/cholesky | solution.py:48
  133.7 2.4 %custom-call.7 = f32[1,32,32]{1,2,0:T(8,128)S(1)} custom-call(f32[1,32,32]{2,1,0:T(8,128)S(1)} %fusion.24), custom_call_target="InvertDiagBlocksLowerTriangular" | custom-call | tf_op jit(solution)/shard_map/triangular_solve/custom-call.0 | solution.py:49
  137.8 2.9 %cholesky.70 = f32[32,32]{1,0:T(8,128)S(1)} custom-call(f32[32,32]{1,0:T(8,128)S(1)} %fusion.30), custom_call_target="Cholesky" | custom-call | tf_op jit(solution)/shard_map/jit(cholesky)/cholesky | solution.py:48
  142.1 2.4 %custom-call.8 = f32[1,32,32]{1,2,0:T(8,128)S(1)} custom-call(f32[1,32,32]{2,1,0:T(8,128)S(1)} %fusion.25), custom_call_target="InvertDiagBlocksLowerTriangular" | custom-call | tf_op jit(solution)/shard_map/triangular_solve/custom-call.0 | solution.py:49
  144.8 1.1 fusion.49
  146.1 2.9 %cholesky.81 = f32[32,32]{1,0:T(8,128)S(1)} custom-call(f32[32,32]{1,0:T(8,128)S(1)} %fusion.28), custom_call_target="Cholesky" | custom-call | tf_op jit(solution)/shard_map/jit(cholesky)/cholesky | solution.py:48
  150.4 2.4 %custom-call.9 = f32[1,32,32]{1,2,0:T(8,128)S(1)} custom-call(f32[1,32,32]{2,1,0:T(8,128)S(1)} %fusion.26), custom_call_target="InvertDiagBlocksLowerTriangular" | custom-call | tf_op jit(solution)/shard_map/triangular_solve/custom-call.0 | solution.py:49
  154.2 1.2 broadcast_in_dim.6
  155.4 4.7 %all-to-all-start.3 = ((bf16[8,32,16,128]{3,1,2,0:T(8,128)(2,1)}), bf16[8,32,16,128]{3,1,2,0:T(8,128)(2,1)S(1)}, u32[]{:S(2)}, u32[]{:S(2)}) async-start(bf16[8,32,16,128]{3,1,2,0:T(8,128)(2,1)} %broadcast_in_dim.6), calls=%async_computation.3 | async-start | bytes 2097152 | tf_op jit(solution)/shard_map/all_to_all | solution.py:109
  160.1 15.0 %all-to-all-done.3 = bf16[8,32,16,128]{3,1,2,0:T(8,128)(2,1)S(1)} async-done(((bf16[8,32,16,128]{3,1,2,0:T(8,128)(2,1)}), bf16[8,32,16,128]{3,1,2,0:T(8,128)(2,1)S(1)}, u32[]{:S(2)}, u32[]{:S(2)}) %all-to-all-start.3) | async-done | bytes 1048608 | tf_op jit(solution)/shard_map/all_to_all | solution.py:109
  175.9 2.8 %fusion = bf16[64,8,16,128]{3,2,0,1:T(8,128)(2,1)S(1)} fusion(f32[64,8,16,128]{3,0,2,1:T(8,128)S(1)} %fusion.37, bf16[8,64,16,128]{3,2,1,0:T(8,128)(2,1)S(1)} %copy-done.1), kind=kLoop, calls=%fused_computation.1 | loop fusion | flops 3145728 | bytes 8388608 | tf_op jit(solution)/shard_map/convert_element_type | solution.py:113
  179.3 2.8 %copy.44 = bf16[8,8,128,128]{3,1,2,0:T(8,128)(2,1)} copy(bf16[8,8,128,128]{3,2,1,0:T(8,128)(2,1)S(1)} %bitcast.121) | data formatting | bytes 4194304
  (53 shorter events, 16.9 us)
Async XLA Ops:
  0.6 127.5 %copy-start = (f32[512,32]{0,1:T(8,128)S(1)}, f32[512,32]{0,1:T(8,128)}, u32[]{:S(2)}) copy-start(f32[512,32]{0,1:T(8,128)} %param.10) | copy-start | bytes 196612
  97.4 18.9 %all-to-all-start.2 = ((f32[128,1,1152]{2,1,0:T(1,128)}), f32[128,1,1152]{2,1,0:T(1,128)S(1)}, u32[]{:S(2)}, u32[]{:S(2)}) async-start(f32[128,1,1152]{2,1,0:T(1,128)} %broadcast_in_dim.4), calls=%async_computation.2 | async-start | bytes 1179648 | tf_op jit(solution)/shard_map/all_to_all | solution.py:59
  155.4 19.7 %all-to-all-start.3 = ((bf16[8,32,16,128]{3,1,2,0:T(8,128)(2,1)}), bf16[8,32,16,128]{3,1,2,0:T(8,128)(2,1)S(1)}, u32[]{:S(2)}, u32[]{:S(2)}) async-start(bf16[8,32,16,128]{3,1,2,0:T(8,128)(2,1)} %broadcast_in_dim.6), calls=%async_computation.3 | async-start | bytes 2097152 | tf_op jit(solution)/shard_map/all_to_all | solution.py:109
  160.1 15.8 %copy-start.1 = (bf16[8,64,16,128]{3,2,1,0:T(8,128)(2,1)S(1)}, bf16[8,64,16,128]{3,2,1,0:T(8,128)(2,1)}, u32[]{:S(2)}) copy-start(bf16[8,64,16,128]{3,2,1,0:T(8,128)(2,1)} %shard_map.59) | copy-start | bytes 6291460

commit v6 on v5

--- a/solution.py
+++ b/solution.py
@@ -17,11 +17,13 @@
     eye = jnp.where(row == lax.broadcasted_iota(jnp.int32, (nblk, nblk), 1), 1.0, 0.0).astype(jnp.bfloat16)
     one = jnp.ones((nblk, nblk), jnp.float32)
     zero = jnp.zeros((nblk, nblk), jnp.float32)
-    for c in range(sky_ref.shape[0]):
-        p = pat_ref[:, c, :].astype(jnp.float32).astype(jnp.bfloat16)
-        p = lax.dot_general(eye, p, (((1,), (1,)), ((), ())), preferred_element_type=jnp.float32)
+    ct = sky_ref.shape[0]
+    pat = pat_ref[...].reshape(taps * ct, nblk).astype(jnp.float32).astype(jnp.bfloat16)
+    pat = lax.dot_general(eye, pat, (((1,), (1,)), ((), ())), preferred_element_type=jnp.float32)
+    for c in range(ct):
         sel = jnp.concatenate(
-            [jnp.where(p[:, k:k + 1] == lane, one, zero).astype(jnp.bfloat16) for k in range(taps)], axis=0)
+            [jnp.where(pat[:, k * ct + c:k * ct + c + 1] == lane, one, zero).astype(jnp.bfloat16)
+             for k in range(taps)], axis=0)
         src = jnp.dot(sel, sky_ref[c], preferred_element_type=jnp.float32).astype(jnp.bfloat16)
         lhs = jnp.concatenate([src[k * nblk:(k + 1) * nblk] for k in range(taps)], axis=1)
         rhs = jnp.concatenate([beam_ref[c, k] for k in range(taps)], axis=1)

time: 182 us -> 171 us (0.940)
  Pallas kernels: 34.1 us -> 22.3 us
    pallas_call x1, Pallas kernels: 34.1 us -> 22.3 us  [smooth(): pl.pallas_call(smooth_kernel, out_shape=jax.ShapeDtypeStruct((parts, chan...]
where the time goes in v6:
time: 171 us; the launch traced here: 170 us
  blocking collectives  55 us (32%)
  waiting for transfers between devices  29.2 us (17%)
  other arithmetic  26.7 us (16%)
  Pallas kernels  22.3 us (13%)
  local copies, waits for them, and re-layouts  19 us (11%)
  starting transfers between devices  9.38 us (5%)
  matrix products  7.82 us (5%)
    all_to_all x1, blocking collectives, local(): by_pixel = lax.all_to_all(chunks, 'chan', 0, 0, tiled=True)  32.1 us
    all_to_all x1, blocking collectives, sum_all(): got = lax.all_to_all(pieces, AXES, 0, 0, tiled=False)  22.9 us
    pallas_call x1, Pallas kernels, smooth(): pl.pallas_call(smooth_kernel, out_shape=jax.ShapeDtypeStruct((parts, chan...  22.3 us
    all_to_all x1, waiting for transfers between devices, local(): gathered = lax.all_to_all(spread, 'chan', 0, 0, tiled=False)  15 us
    all_to_all x1, waiting for transfers between devices, sum_all(): return lax.all_to_all(spread, AXES, 0, 0, tiled=False)  14.2 us
    unnamed x13, local copies, waits for them, and re-layouts  11.4 us
    another operation x9, other arithmetic, orthonormal(): factor = jnp.linalg.cholesky(square)  10.8 us
    another operation x6, other arithmetic, orthonormal(): lax.linalg.triangular_solve(factor, images, left_side=False, lower=True,...  9.26 us
  transfers between devices with their start and end apart: 2, of which 2 were waited for; matrix products, arithmetic and copies ran while one was open for 0% of the time, Pallas kernels for 0%

profile of v6, /device:TPU:1, one launch (start us, length us, event | category | flops | bytes accessed | tf_op | source)
XLA Modules:
  0.0 170.3 jit_solution(1609392706739244875)
XLA Ops:
  0.6 3.5 %copy.32 = bf16[8,8,128,128]{3,2,1,0:T(8,128)(2,1)} copy(bf16[8,8,128,128]{3,1,2,0:T(8,128)(2,1)} %bitcast.122) | data formatting | bytes 4194304
  4.2 22.3 %shard_map.59 = bf16[8,64,16,128]{3,2,1,0:T(8,128)(2,1)} custom-call(s32[9,64,128]{2,1,0:T(8,128)} %bitcast.124, bf16[64,128,128]{2,1,0:T(8,128)(2,1)} %bitcast.118, bf16[64,9,128,128]{3,2,1,0:T(8,128)(2,1)} %beam_ref.1), custom_call_target="tpu_custom_call" | custom-call | tf_op jit(solution)/shard_map/pallas_call | solution.py:37
  26.4 32.1 %all_to_all.26 = bf16[8,64,16,128]{3,2,1,0:T(8,128)(2,1)S(1)} all-to-all(bf16[8,64,16,128]{3,2,1,0:T(8,128)(2,1)} %shard_map.59), channel_id=1, replica_groups=mesh['chan'=8,'pix'=16] {'chan'}, dimensions={0} | all-to-all | bytes 4194304 | tf_op jit(solution)/shard_map/all_to_all | solution.py:98
  58.6 1.3 fusion.5
  61.2 22.9 %all_to_all.27 = f32[128,1,1152]{2,1,0:T(1,128)S(1)} all-to-all(f32[128,1,1152]{2,1,0:T(1,128)S(1)} %all_to_all.21), channel_id=1, replica_groups=mesh['chan'=8,'pix'=16] {'chan','pix'}, dimensions={0} | all-to-all | bytes 1179648 | tf_op jit(solution)/shard_map/all_to_all | solution.py:58
  84.5 1.1 broadcast_in_dim.4
  85.6 4.7 %all-to-all-start.2 = ((f32[128,1,1152]{2,1,0:T(1,128)}), f32[128,1,1152]{2,1,0:T(1,128)S(1)}, u32[]{:S(2)}, u32[]{:S(2)}) async-start(f32[128,1,1152]{2,1,0:T(1,128)} %broadcast_in_dim.4), calls=%async_computation.2 | async-start | bytes 1179648 | tf_op jit(solution)/shard_map/all_to_all | solution.py:61
  90.3 14.2 %all-to-all-done.2 = f32[128,1,1152]{2,1,0:T(1,128)S(1)} async-done(((f32[128,1,1152]{2,1,0:T(1,128)}), f32[128,1,1152]{2,1,0:T(1,128)S(1)}, u32[]{:S(2)}, u32[]{:S(2)}) %all-to-all-start.2) | async-done | bytes 589856 | tf_op jit(solution)/shard_map/all_to_all | solution.py:61
  104.5 1.4 reduce.5
  111.9 2.5 %copy.24 = f32[512,512]{0,1:T(8,128)} copy(f32[512,512]{1,0:T(8,128)} %fusion.18) | data formatting | bytes 2097152 | tf_op jit(solution)/shard_map/concatenate | solution.py:85
  114.5 1.8 %fusion.11 = f32[512,512]{1,0:T(8,128)S(1)} fusion(f32[512,512]{1,0:T(8,128)} %fusion.18, f32[512,512]{0,1:T(8,128)} %copy.24, s32[512]{0:T(512)S(1)} %get-tuple-element.10, s32[512]{0:T(512)S(1)} %get-tuple-element.11, pred[512]{0:T(512)(128)(4,1)S(1)} %fusion.42), kind=kLoop, calls=%fused_computation.13 | loop fusion | flops 1310720 | bytes 3150336 | tf_op jit(solution)/shard_map/mul | solution.py:88
  116.3 1.1 fusion.45
  117.7 2.9 %cholesky.59 = f32[32,32]{1,0:T(8,128)S(1)} custom-call(f32[32,32]{1,0:T(8,128)S(1)} %fusion.32), custom_call_target="Cholesky" | custom-call | tf_op jit(solution)/shard_map/jit(cholesky)/cholesky | solution.py:50
  121.9 2.4 %custom-call.7 = f32[1,32,32]{1,2,0:T(8,128)S(1)} custom-call(f32[1,32,32]{2,1,0:T(8,128)S(1)} %fusion.24), custom_call_target="InvertDiagBlocksLowerTriangular" | custom-call | tf_op jit(solution)/shard_map/triangular_solve/custom-call.0 | solution.py:51
  124.7 1.1 fusion.47
  126.0 2.9 %cholesky.70 = f32[32,32]{1,0:T(8,128)S(1)} custom-call(f32[32,32]{1,0:T(8,128)S(1)} %fusion.30), custom_call_target="Cholesky" | custom-call | tf_op jit(solution)/shard_map/jit(cholesky)/cholesky | solution.py:50
  130.3 2.4 %custom-call.8 = f32[1,32,32]{1,2,0:T(8,128)S(1)} custom-call(f32[1,32,32]{2,1,0:T(8,128)S(1)} %fusion.25), custom_call_target="InvertDiagBlocksLowerTriangular" | custom-call | tf_op jit(solution)/shard_map/triangular_solve/custom-call.0 | solution.py:51
  134.4 2.9 %cholesky.81 = f32[32,32]{1,0:T(8,128)S(1)} custom-call(f32[32,32]{1,0:T(8,128)S(1)} %fusion.28), custom_call_target="Cholesky" | custom-call | tf_op jit(solution)/shard_map/jit(cholesky)/cholesky | solution.py:50
  138.6 2.4 %custom-call.9 = f32[1,32,32]{1,2,0:T(8,128)S(1)} custom-call(f32[1,32,32]{2,1,0:T(8,128)S(1)} %fusion.26), custom_call_target="InvertDiagBlocksLowerTriangular" | custom-call | tf_op jit(solution)/shard_map/triangular_solve/custom-call.0 | solution.py:51
  142.4 1.2 broadcast_in_dim.6
  143.6 4.7 %all-to-all-start.3 = ((bf16[8,32,16,128]{3,1,2,0:T(8,128)(2,1)}), bf16[8,32,16,128]{3,1,2,0:T(8,128)(2,1)S(1)}, u32[]{:S(2)}, u32[]{:S(2)}) async-start(bf16[8,32,16,128]{3,1,2,0:T(8,128)(2,1)} %broadcast_in_dim.6), calls=%async_computation.3 | async-start | bytes 2097152 | tf_op jit(solution)/shard_map/all_to_all | solution.py:111
  148.3 15.0 %all-to-all-done.3 = bf16[8,32,16,128]{3,1,2,0:T(8,128)(2,1)S(1)} async-done(((bf16[8,32,16,128]{3,1,2,0:T(8,128)(2,1)}), bf16[8,32,16,128]{3,1,2,0:T(8,128)(2,1)S(1)}, u32[]{:S(2)}, u32[]{:S(2)}) %all-to-all-start.3) | async-done | bytes 1048608 | tf_op jit(solution)/shard_map/all_to_all | solution.py:111
  164.1 2.8 %fusion = bf16[64,8,16,128]{3,2,0,1:T(8,128)(2,1)S(1)} fusion(f32[64,8,16,128]{3,0,2,1:T(8,128)S(1)} %fusion.37, bf16[8,64,16,128]{3,2,1,0:T(8,128)(2,1)S(1)} %copy-done.1), kind=kLoop, calls=%fused_computation.1 | loop fusion | flops 3145728 | bytes 8388608 | tf_op jit(solution)/shard_map/convert_element_type | solution.py:115
  167.5 2.8 %copy.44 = bf16[8,8,128,128]{3,1,2,0:T(8,128)(2,1)} copy(bf16[8,8,128,128]{3,2,1,0:T(8,128)(2,1)S(1)} %bitcast.121) | data formatting | bytes 4194304
  (53 shorter events, 16.9 us)
Async XLA Ops:
  0.6 115.7 %copy-start = (f32[512,32]{0,1:T(8,128)S(1)}, f32[512,32]{0,1:T(8,128)}, u32[]{:S(2)}) copy-start(f32[512,32]{0,1:T(8,128)} %param.10) | copy-start | bytes 196612
  85.6 18.9 %all-to-all-start.2 = ((f32[128,1,1152]{2,1,0:T(1,128)}), f32[128,1,1152]{2,1,0:T(1,128)S(1)}, u32[]{:S(2)}, u32[]{:S(2)}) async-start(f32[128,1,1152]{2,1,0:T(1,128)} %broadcast_in_dim.4), calls=%async_computation.2 | async-start | bytes 1179648 | tf_op jit(solution)/shard_map/all_to_all | solution.py:61
  143.6 19.7 %all-to-all-start.3 = ((bf16[8,32,16,128]{3,1,2,0:T(8,128)(2,1)}), bf16[8,32,16,128]{3,1,2,0:T(8,128)(2,1)S(1)}, u32[]{:S(2)}, u32[]{:S(2)}) async-start(bf16[8,32,16,128]{3,1,2,0:T(8,128)(2,1)} %broadcast_in_dim.6), calls=%async_computation.3 | async-start | bytes 2097152 | tf_op jit(solution)/shard_map/all_to_all | solution.py:111
  148.3 15.8 %copy-start.1 = (bf16[8,64,16,128]{3,2,1,0:T(8,128)(2,1)S(1)}, bf16[8,64,16,128]{3,2,1,0:T(8,128)(2,1)}, u32[]{:S(2)}) copy-start(bf16[8,64,16,128]{3,2,1,0:T(8,128)(2,1)} %shard_map.59) | copy-start | bytes 6291460

commit v7 on v6

--- a/solution.py
+++ b/solution.py
@@ -2,6 +2,7 @@
 import jax.numpy as jnp
 from jax import lax
 from jax.sharding import PartitionSpec as P
+import functools
 from jax.experimental import pallas as pl
 
 BLK = 128
@@ -45,12 +46,43 @@
     )(pat_t, sky3, beam)
 
 
-def orthonormal(images):
-    square = jnp.dot(images.T, images, precision=lax.Precision.HIGHEST)
-    factor = jnp.linalg.cholesky(square)
-    return lax.linalg.triangular_solve(
-        factor, images, left_side=False, lower=True, transpose_a=True
-    )
+HI = lax.Precision.HIGHEST
+
+def sweep_kernel(g_ref, b_ref, o_ref, *, iters):
+    g = g_ref[...]
+    bt = b_ref[...]
+    m = bt.shape[0]
+    rows = lax.broadcasted_iota(jnp.int32, (m, m), 0)
+    cols = lax.broadcasted_iota(jnp.int32, (m, m), 1)
+    for _ in range(iters):
+        it = jnp.dot(bt, g, precision=HI, preferred_element_type=jnp.float32)
+        a = lax.dot_general(it, it, (((1,), (1,)), ((), ())), precision=HI,
+                            preferred_element_type=jnp.float32)
+        low = jnp.zeros((m, m), jnp.float32)
+        for j in range(m):
+            d = jnp.sqrt(a[j:j + 1, j:j + 1])
+            col = jnp.where(rows[:, j:j + 1] >= j, a[:, j:j + 1] / d, 0.0)
+            row = jnp.where(cols[j:j + 1, :] >= j, a[j:j + 1, :] / d, 0.0)
+            low = jnp.where(cols == j, col, low)
+            a = a - col * row
+        bad = jnp.isnan(jnp.sum(low, keepdims=True))
+        low = jnp.where(bad, jnp.nan, low)
+        rest = jnp.where(rows == cols, 1.0, 0.0).astype(jnp.float32)
+        inv = jnp.zeros((m, m), jnp.float32)
+        for i in range(m):
+            r = rest[i:i + 1, :] / low[i:i + 1, i:i + 1]
+            inv = jnp.where(rows == i, r, inv)
+            rest = rest - low[:, i:i + 1] * r
+        bt = jnp.dot(inv, it, precision=HI, preferred_element_type=jnp.float32)
+    o_ref[...] = bt
+
+def sweeps(gram, basis, iters):
+    bt = basis.T
+    out = pl.pallas_call(
+        functools.partial(sweep_kernel, iters=iters),
+        out_shape=jax.ShapeDtypeStruct(bt.shape, jnp.float32),
+    )(gram, bt)
+    return out.T
 
 
 def sum_all(pieces):
@@ -102,9 +134,7 @@
     partial_value = lax.dot_general(
         by_pixel, by_pixel, (((1, 2), (1, 2)), ((), ())), preferred_element_type=jnp.float32)
     gram = symmetric_sum(partial_value, n_chan, 1.0 / all_pixels)
-    for sweep in range(ITERS):
-        images = jnp.dot(gram, basis, precision=lax.Precision.HIGHEST)
-        basis = orthonormal(images)
+    basis = sweeps(gram, basis, ITERS)
     modes_low = basis.astype(jnp.bfloat16)
     coeffs = jnp.einsum("cm,cbi->mbi", modes_low, by_pixel, preferred_element_type=jnp.float32).astype(jnp.bfloat16)
     spread = jnp.broadcast_to(coeffs[None], (n_chan,) + coeffs.shape)

time: 171 us -> 160 us (0.936)
  other arithmetic: 26.7 us -> 8.13 us
  Pallas kernels: 22.3 us -> 37.2 us
  matrix products: 7.82 us -> 2.57 us
  local copies, waits for them, and re-layouts: 19 us -> 17.1 us
    another operation x15 -> x0, other arithmetic: 20 us -> none  [the longest x9 10.8 us: orthonormal(): factor = jnp.linalg.cholesky(square)]
    pallas_call x0 -> x1, Pallas kernels: none -> 14.9 us  [sweeps(): pl.pallas_call(functools.partial(sweep_kernel, iters=iters), out_shape=ja...]
    unnamed x13 -> x4, local copies, waits for them, and re-layouts: 11.4 us -> 6.25 us
    dot_general x6 -> x0, matrix products: 3.79 us -> none  [the longest x3 3.21 us: local(): images = jnp.dot(gram, basis, precision=lax.Precision.HIGHEST)]
    reshape x1 -> x2, local copies, waits for them, and re-layouts: 0.16 us -> 2.46 us  [symmetric_sum(): summed = sum_all(packed.reshape(n, -1)).reshape(packed.shape)]
where the time goes in v7:
time: 160 us; the launch traced here: 159 us
  blocking collectives  55 us (34%)
  Pallas kernels  37.2 us (23%)
  waiting for transfers between devices  29.2 us (18%)
  local copies, waits for them, and re-layouts  17.1 us (11%)
  starting transfers between devices  9.39 us (6%)
  other arithmetic  8.13 us (5%)
  matrix products  2.57 us (2%)
    all_to_all x1, blocking collectives, local(): by_pixel = lax.all_to_all(chunks, 'chan', 0, 0, tiled=True)  32.1 us
    all_to_all x1, blocking collectives, sum_all(): got = lax.all_to_all(pieces, AXES, 0, 0, tiled=False)  22.9 us
    pallas_call x1, Pallas kernels, smooth(): pl.pallas_call(smooth_kernel, out_shape=jax.ShapeDtypeStruct((parts, chan...  22.3 us
    all_to_all x1, waiting for transfers between devices, local(): gathered = lax.all_to_all(spread, 'chan', 0, 0, tiled=False)  15 us
    pallas_call x1, Pallas kernels, sweeps(): pl.pallas_call(functools.partial(sweep_kernel, iters=iters), out_shape=ja...  14.9 us
    all_to_all x1, waiting for transfers between devices, sum_all(): return lax.all_to_all(spread, AXES, 0, 0, tiled=False)  14.2 us
    unnamed x4, local copies, waits for them, and re-layouts  6.25 us
    all_to_all x1, starting transfers between devices, local(): gathered = lax.all_to_all(spread, 'chan', 0, 0, tiled=False)  4.71 us
  transfers between devices with their start and end apart: 2, of which 2 were waited for; matrix products, arithmetic and copies ran while one was open for 0% of the time, Pallas kernels for 0%

profile of v7, /device:TPU:1, one launch (start us, length us, event | category | flops | bytes accessed | tf_op | source)
XLA Modules:
  0.0 159.3 jit_solution(9640820460578055627)
XLA Ops:
  0.6 3.5 %copy.35 = bf16[8,8,128,128]{3,2,1,0:T(8,128)(2,1)} copy(bf16[8,8,128,128]{3,1,2,0:T(8,128)(2,1)} %bitcast.59) | data formatting | bytes 4194304
  4.1 22.3 %shard_map.59 = bf16[8,64,16,128]{3,2,1,0:T(8,128)(2,1)} custom-call(s32[9,64,128]{2,1,0:T(8,128)} %bitcast.61, bf16[64,128,128]{2,1,0:T(8,128)(2,1)} %bitcast.55, bf16[64,9,128,128]{3,2,1,0:T(8,128)(2,1)} %beam_ref.1), custom_call_target="tpu_custom_call" | custom-call | tf_op jit(solution)/shard_map/pallas_call | solution.py:38
  26.4 32.1 %all_to_all.26 = bf16[8,64,16,128]{3,2,1,0:T(8,128)(2,1)S(1)} all-to-all(bf16[8,64,16,128]{3,2,1,0:T(8,128)(2,1)} %shard_map.59), channel_id=1, replica_groups=mesh['chan'=8,'pix'=16] {'chan'}, dimensions={0} | all-to-all | bytes 4194304 | tf_op jit(solution)/shard_map/all_to_all | solution.py:130
  58.5 1.3 fusion.5
  60.5 0.7 all_to_all.21
  61.2 22.9 %all_to_all.27 = f32[128,1,1152]{2,1,0:T(1,128)S(1)} all-to-all(f32[128,1,1152]{2,1,0:T(1,128)S(1)} %all_to_all.21), channel_id=1, replica_groups=mesh['chan'=8,'pix'=16] {'chan','pix'}, dimensions={0} | all-to-all | bytes 1179648 | tf_op jit(solution)/shard_map/all_to_all | solution.py:90
  84.4 1.1 broadcast_in_dim.4
  85.6 4.7 %all-to-all-start.2 = ((f32[128,1,1152]{2,1,0:T(1,128)}), f32[128,1,1152]{2,1,0:T(1,128)S(1)}, u32[]{:S(2)}, u32[]{:S(2)}) async-start(f32[128,1,1152]{2,1,0:T(1,128)} %broadcast_in_dim.4), calls=%async_computation.2 | async-start | bytes 1179648 | tf_op jit(solution)/shard_map/all_to_all | solution.py:93
  90.3 14.2 %all-to-all-done.2 = f32[128,1,1152]{2,1,0:T(1,128)S(1)} async-done(((f32[128,1,1152]{2,1,0:T(1,128)}), f32[128,1,1152]{2,1,0:T(1,128)S(1)}, u32[]{:S(2)}, u32[]{:S(2)}) %all-to-all-start.2) | async-done | bytes 589856 | tf_op jit(solution)/shard_map/all_to_all | solution.py:93
  104.5 1.4 reduce.1
  105.9 1.0 reshape.30
  106.9 1.4 copy.24
  108.3 1.3 slice_bitcast_fusion
  109.6 1.8 %concatenate.19 = f32[512,512]{0,1:T(8,128)S(1)} concatenate(f32[64,512]{0,1:T(8,128)} %get-tuple-element.9, f32[64,512]{0,1:T(8,128)} %get-tuple-element.8, f32[64,512]{0,1:T(8,128)} %get-tuple-element.3, f32[64,512]{0,1:T(8,128)} %get-tuple-element.4, f32[64,512]{0,1:T(8,128)} %get-tuple-element.7, f32[64,512]{0,1:T(8,128)} %get-tuple-element.6, f32[64,512]{0,1:T(8,128)} %get-tuple-element.5, ...), dimensions={0} | concatenate | bytes 2097152 | tf_op jit(solution)/shard_map/concatenate | solution.py:117
  111.4 1.3 copy.30
  112.8 2.5 %fusion.11.g_ref = f32[512,512]{1,0:T(8,128)} fusion(f32[512,512]{1,0:T(8,128)} %copy.30, f32[512,512]{0,1:T(8,128)S(1)} %concatenate.19, s32[512]{0:T(512)S(1)} %get-tuple-element.14, s32[512]{0:T(512)S(1)} %get-tuple-element.15, pred[512]{0:T(512)(128)(4,1)S(1)} %fusion.21), kind=kLoop, calls=%fused_computation.13 | loop fusion | flops 1310720 | bytes 3150336 | tf_op jit(solution)/shard_map/mul | solution.py:120
  115.2 14.9 %shard_map.60 = f32[32,512]{1,0:T(8,128)} custom-call(f32[512,512]{1,0:T(8,128)} %fusion.11.g_ref, f32[32,512]{1,0:T(8,128)} %bitcast.63), custom_call_target="tpu_custom_call" | custom-call | tf_op jit(solution)/shard_map/pallas_call | solution.py:81
  130.1 0.8 bitcast_convert_fusion
  131.4 1.2 broadcast_in_dim.5
  132.6 4.7 %all-to-all-start.3 = ((bf16[8,32,16,128]{3,1,2,0:T(8,128)(2,1)}), bf16[8,32,16,128]{3,1,2,0:T(8,128)(2,1)S(1)}, u32[]{:S(2)}, u32[]{:S(2)}) async-start(bf16[8,32,16,128]{3,1,2,0:T(8,128)(2,1)} %broadcast_in_dim.5), calls=%async_computation.3 | async-start | bytes 2097152 | tf_op jit(solution)/shard_map/all_to_all | solution.py:141
  137.3 15.0 %all-to-all-done.3 = bf16[8,32,16,128]{3,1,2,0:T(8,128)(2,1)S(1)} async-done(((bf16[8,32,16,128]{3,1,2,0:T(8,128)(2,1)}), bf16[8,32,16,128]{3,1,2,0:T(8,128)(2,1)S(1)}, u32[]{:S(2)}, u32[]{:S(2)}) %all-to-all-start.3) | async-done | bytes 1048608 | tf_op jit(solution)/shard_map/all_to_all | solution.py:141
  152.3 0.8 fusion.16
  153.1 2.8 %fusion = bf16[64,8,16,128]{3,2,0,1:T(8,128)(2,1)S(1)} fusion(f32[64,8,16,128]{3,0,2,1:T(8,128)S(1)} %fusion.16, bf16[8,64,16,128]{3,2,1,0:T(8,128)(2,1)S(1)} %copy-done), kind=kLoop, calls=%fused_computation.1 | loop fusion | flops 3145728 | bytes 8388608 | tf_op jit(solution)/shard_map/convert_element_type | solution.py:145
  156.5 2.8 %copy.47 = bf16[8,8,128,128]{3,1,2,0:T(8,128)(2,1)} copy(bf16[8,8,128,128]{3,2,1,0:T(8,128)(2,1)S(1)} %bitcast.58) | data formatting | bytes 4194304
  (18 shorter events, 2.1 us)
Async XLA Ops:
  85.6 18.9 %all-to-all-start.2 = ((f32[128,1,1152]{2,1,0:T(1,128)}), f32[128,1,1152]{2,1,0:T(1,128)S(1)}, u32[]{:S(2)}, u32[]{:S(2)}) async-start(f32[128,1,1152]{2,1,0:T(1,128)} %broadcast_in_dim.4), calls=%async_computation.2 | async-start | bytes 1179648 | tf_op jit(solution)/shard_map/all_to_all | solution.py:93
  132.6 19.7 %all-to-all-start.3 = ((bf16[8,32,16,128]{3,1,2,0:T(8,128)(2,1)}), bf16[8,32,16,128]{3,1,2,0:T(8,128)(2,1)S(1)}, u32[]{:S(2)}, u32[]{:S(2)}) async-start(bf16[8,32,16,128]{3,1,2,0:T(8,128)(2,1)} %broadcast_in_dim.5), calls=%async_computation.3 | async-start | bytes 2097152 | tf_op jit(solution)/shard_map/all_to_all | solution.py:141
  137.3 15.8 %copy-start = (bf16[8,64,16,128]{3,2,1,0:T(8,128)(2,1)S(1)}, bf16[8,64,16,128]{3,2,1,0:T(8,128)(2,1)}, u32[]{:S(2)}) copy-start(bf16[8,64,16,128]{3,2,1,0:T(8,128)(2,1)} %shard_map.59) | copy-start | bytes 6291460

commit v8 on v7

--- a/solution.py
+++ b/solution.py
@@ -48,8 +48,34 @@
 
 HI = lax.Precision.HIGHEST
 
-def sweep_kernel(g_ref, b_ref, o_ref, *, iters):
-    g = g_ref[...]
+def build_gram(x, nb, bs, scale):
+    n, w = x.shape
+    pairs = nb // 2
+    per = n // pairs
+    span = (nb + 1) * bs
+    q = w // span
+    size = nb * bs
+    mats = []
+    for i in range(pairs):
+        xi = x[i * per:(i + 1) * per]
+        mats.append(jnp.concatenate([xi[:, h * span:(h + 1) * span] for h in range(q)], axis=0))
+    rows = []
+    for r in range(nb):
+        if r < pairs:
+            data = mats[r][:, :(nb - r) * bs]
+            if r:
+                data = jnp.concatenate([jnp.zeros((bs, r * bs), jnp.float32), data], axis=1)
+            rows.append(data)
+        else:
+            rows.append(mats[nb - 1 - r][:, span - size:])
+    half = jnp.concatenate(rows, axis=0)
+    blk = lax.broadcasted_iota(jnp.int32, (size, size), 0) // bs
+    blk_t = lax.broadcasted_iota(jnp.int32, (size, size), 1) // bs
+    return jnp.where(blk <= blk_t, half, half.T) * scale
+
+
+def sweep_kernel(g_ref, b_ref, o_ref, *, iters, nb, bs, scale):
+    g = build_gram(g_ref[...], nb, bs, scale)
     bt = b_ref[...]
     m = bt.shape[0]
     rows = lax.broadcasted_iota(jnp.int32, (m, m), 0)
@@ -76,12 +102,12 @@
         bt = jnp.dot(inv, it, precision=HI, preferred_element_type=jnp.float32)
     o_ref[...] = bt
 
-def sweeps(gram, basis, iters):
+def sweeps(packed, basis, iters, nb, bs, scale):
     bt = basis.T
     out = pl.pallas_call(
-        functools.partial(sweep_kernel, iters=iters),
+        functools.partial(sweep_kernel, iters=iters, nb=nb, bs=bs, scale=scale),
         out_shape=jax.ShapeDtypeStruct(bt.shape, jnp.float32),
-    )(gram, bt)
+    )(packed, bt)
     return out.T
 
 
@@ -93,31 +119,19 @@
     return lax.all_to_all(spread, AXES, 0, 0, tiled=False)
 
 
-def symmetric_sum(partial, nb, scale):
+def pack_gram(partial, nb, n):
     size = partial.shape[0]
     bs = size // nb
-    rows = []
-    for i in range(nb // 2):
+    pairs = nb // 2
+    q = bs * pairs // n
+    out = []
+    for i in range(pairs):
         k = nb - 1 - i
-        rows.append(jnp.concatenate(
-            [partial[i * bs:(i + 1) * bs, i * bs:], partial[k * bs:(k + 1) * bs, k * bs:]], axis=1))
-    packed = jnp.stack(rows)
-    n = lax.axis_size(AXES)
-    summed = sum_all(packed.reshape(n, -1)).reshape(packed.shape)
-    lead = (nb // 2 - 1) * bs
-    padded = jnp.pad(summed, ((0, 0), (0, 0), (lead, 0)))
-    width = padded.shape[2]
-    upper = []
-    for r in range(nb):
-        if r < nb // 2:
-            start = lead - r * bs
-            upper.append(padded[r, :, start:start + size])
-        else:
-            upper.append(padded[nb - 1 - r, :, width - size:])
-    half = jnp.concatenate(upper, axis=0)
-    blk = lax.broadcasted_iota(jnp.int32, (size, size), 0) // bs
-    blk_t = lax.broadcasted_iota(jnp.int32, (size, size), 1) // bs
-    return jnp.where(blk <= blk_t, half, half.T) * scale
+        m = jnp.concatenate(
+            [partial[i * bs:(i + 1) * bs, i * bs:], partial[k * bs:(k + 1) * bs, k * bs:]], axis=1)
+        rows = bs // q
+        out.append(jnp.concatenate([m[h * rows:(h + 1) * rows] for h in range(q)], axis=1))
+    return jnp.concatenate(out, axis=0)
 
 
 def local(sky_cube, beam_blocks, pattern, start_modes):
@@ -133,8 +147,11 @@
     basis = start_modes
     partial_value = lax.dot_general(
         by_pixel, by_pixel, (((1, 2), (1, 2)), ((), ())), preferred_element_type=jnp.float32)
-    gram = symmetric_sum(partial_value, n_chan, 1.0 / all_pixels)
-    basis = sweeps(gram, basis, ITERS)
+    nb = 4
+    n_dev = lax.axis_size(AXES)
+    packed = sum_all(pack_gram(partial_value, nb, n_dev))
+    packed = packed.reshape(n_dev, -1)
+    basis = sweeps(packed, basis, ITERS, nb, partial_value.shape[0] // nb, 1.0 / all_pixels)
     modes_low = basis.astype(jnp.bfloat16)
     coeffs = jnp.einsum("cm,cbi->mbi", modes_low, by_pixel, preferred_element_type=jnp.float32).astype(jnp.bfloat16)
     spread = jnp.broadcast_to(coeffs[None], (n_chan,) + coeffs.shape)

time: 160 us -> 149 us (0.931)
  blocking collectives: 55 us -> 74.7 us
  waiting for transfers between devices: 29.2 us -> 15 us
  local copies, waits for them, and re-layouts: 17.1 us -> 9.81 us
  starting transfers between devices: 9.39 us -> 4.81 us
  other arithmetic: 8.13 us -> 4.34 us
    all_to_all x0 -> x1, blocking collectives: none -> 19.1 us  [sum_all(): return lax.all_to_all(spread, AXES, 0, 0, tiled=False)]
    all_to_all x1 -> x0, waiting for transfers between devices: 14.2 us -> none  [sum_all(): return lax.all_to_all(spread, AXES, 0, 0, tiled=False)]
    all_to_all x1 -> x0, starting transfers between devices: 4.67 us -> none  [sum_all(): return lax.all_to_all(spread, AXES, 0, 0, tiled=False)]
    concatenate x2 -> x0, local copies, waits for them, and re-layouts: 3.16 us -> none  [symmetric_sum(): half = jnp.concatenate(upper, axis=0)]
    mul x1 -> x0, other arithmetic: 2.47 us -> none  [symmetric_sum(): return jnp.where(blk <= blk_t, half, half.T) * scale]
    reshape x2 -> x0, local copies, waits for them, and re-layouts: 2.46 us -> none  [symmetric_sum(): summed = sum_all(packed.reshape(n, -1)).reshape(packed.shape)]
    unnamed x4 -> x5, local copies, waits for them, and re-layouts: 6.25 us -> 7.13 us
  transfers between devices with their start and end apart: 2 -> 1, of which waited for: 2 -> 1; matrix products, arithmetic and copies ran while one was open for 0% -> 0% of each run, Pallas kernels for 0% -> 0%
where the time goes in v8:
time: 149 us
  blocking collectives  74.7 us (50%)
  Pallas kernels  37 us (25%)
  waiting for transfers between devices  15 us (10%)
  local copies, waits for them, and re-layouts  9.81 us (7%)
  starting transfers between devices  4.81 us (3%)
  other arithmetic  4.34 us (3%)
  matrix products  2.57 us (2%)
    all_to_all x1, blocking collectives, local(): by_pixel = lax.all_to_all(chunks, 'chan', 0, 0, tiled=True)  32.1 us
    all_to_all x1, blocking collectives, sum_all(): got = lax.all_to_all(pieces, AXES, 0, 0, tiled=False)  23.5 us
    pallas_call x1, Pallas kernels, smooth(): pl.pallas_call(smooth_kernel, out_shape=jax.ShapeDtypeStruct((parts, chan...  22.3 us
    all_to_all x1, blocking collectives, sum_all(): return lax.all_to_all(spread, AXES, 0, 0, tiled=False)  19.1 us
    all_to_all x1, waiting for transfers between devices, local(): gathered = lax.all_to_all(spread, 'chan', 0, 0, tiled=False)  15 us
    pallas_call x1, Pallas kernels, sweeps(): pl.pallas_call(functools.partial(sweep_kernel, iters=iters, nb=nb, bs=bs,...  14.8 us
    unnamed x5, local copies, waits for them, and re-layouts  7.13 us
    all_to_all x1, starting transfers between devices, local(): gathered = lax.all_to_all(spread, 'chan', 0, 0, tiled=False)  4.81 us
  transfers between devices with their start and end apart: 1, of which 1 were waited for; matrix products, arithmetic and copies ran while one was open for 0% of the time, Pallas kernels for 0%

profile of v8, /device:TPU:1, one launch (start us, length us, event | category | flops | bytes accessed | tf_op | source)
XLA Modules:
  0.0 149.0 jit_solution(8438702776200291616)
XLA Ops:
  0.6 3.5 %copy.21 = bf16[8,8,128,128]{3,2,1,0:T(8,128)(2,1)} copy(bf16[8,8,128,128]{3,1,2,0:T(8,128)(2,1)} %bitcast.37) | data formatting | bytes 4194304
  4.1 22.3 %shard_map.59 = bf16[8,64,16,128]{3,2,1,0:T(8,128)(2,1)} custom-call(s32[9,64,128]{2,1,0:T(8,128)} %bitcast.39, bf16[64,128,128]{2,1,0:T(8,128)(2,1)} %bitcast.32, bf16[64,9,128,128]{3,2,1,0:T(8,128)(2,1)} %beam_ref.1), custom_call_target="tpu_custom_call" | custom-call | tf_op jit(solution)/shard_map/pallas_call | solution.py:38
  26.4 32.1 %all_to_all.27 = bf16[8,64,16,128]{3,2,1,0:T(8,128)(2,1)S(1)} all-to-all(bf16[8,64,16,128]{3,2,1,0:T(8,128)(2,1)} %shard_map.59), channel_id=1, replica_groups=mesh['chan'=8,'pix'=16] {'chan'}, dimensions={0} | all-to-all | bytes 4194304 | tf_op jit(solution)/shard_map/all_to_all | solution.py:144
  58.5 1.3 fusion.5
  60.0 0.2 fusion.13
  60.2 0.5 copy.15
  60.7 23.5 %all_to_all.28 = f32[128,1,1280]{2,1,0:T(1,128)S(1)} all-to-all(f32[128,1,1280]{2,1,0:T(1,128)S(1)} %copy.15), channel_id=1, replica_groups=mesh['chan'=8,'pix'=16] {'chan','pix'}, dimensions={0} | all-to-all | bytes 1310720 | tf_op jit(solution)/shard_map/all_to_all | solution.py:116
  84.2 0.4 reduce_sum.9
  84.6 0.3 broadcast_in_dim.4
  85.0 19.1 %all_to_all.29 = f32[128,1,1280]{2,1,0:T(1,128)S(1)} all-to-all(f32[128,1,1280]{2,1,0:T(1,128)S(1)} %broadcast_in_dim.4), channel_id=1, replica_groups=mesh['chan'=8,'pix'=16] {'chan','pix'}, dimensions={0} | all-to-all | bytes 1310720 | tf_op jit(solution)/shard_map/all_to_all | solution.py:119
  104.1 0.9 copy.35
  104.9 14.8 %shard_map.60 = f32[32,512]{1,0:T(8,128)} custom-call(f32[128,1280]{1,0:T(8,128)} %bitcast.36, f32[32,512]{1,0:T(8,128)} %bitcast.41), custom_call_target="tpu_custom_call" | custom-call | tf_op jit(solution)/shard_map/pallas_call | solution.py:107
  119.7 0.8 bitcast_convert_fusion
  120.5 0.5 fusion.8
  121.0 1.2 broadcast_in_dim.5
  122.2 4.8 %all-to-all-start.3 = ((bf16[8,32,16,128]{3,1,2,0:T(8,128)(2,1)}), bf16[8,32,16,128]{3,1,2,0:T(8,128)(2,1)S(1)}, u32[]{:S(2)}, u32[]{:S(2)}) async-start(bf16[8,32,16,128]{3,1,2,0:T(8,128)(2,1)} %broadcast_in_dim.5), calls=%async_computation.3 | async-start | bytes 2097152 | tf_op jit(solution)/shard_map/all_to_all | solution.py:158
  127.0 0.0 copy-start
  127.0 15.0 %all-to-all-done.3 = bf16[8,32,16,128]{3,1,2,0:T(8,128)(2,1)S(1)} async-done(((bf16[8,32,16,128]{3,1,2,0:T(8,128)(2,1)}), bf16[8,32,16,128]{3,1,2,0:T(8,128)(2,1)S(1)}, u32[]{:S(2)}, u32[]{:S(2)}) %all-to-all-start.3) | async-done | bytes 1048608 | tf_op jit(solution)/shard_map/all_to_all | solution.py:158
  142.0 0.8 fusion.16
  142.8 0.0 copy-done
  142.8 2.8 %fusion = bf16[64,8,16,128]{3,2,0,1:T(8,128)(2,1)S(1)} fusion(f32[64,8,16,128]{3,0,2,1:T(8,128)S(1)} %fusion.16, bf16[8,64,16,128]{3,2,1,0:T(8,128)(2,1)S(1)} %copy-done), kind=kLoop, calls=%fused_computation.1 | loop fusion | flops 3145728 | bytes 8388608 | tf_op jit(solution)/shard_map/convert_element_type | solution.py:162
  145.6 0.6 copy.18
  146.2 2.8 %copy.34 = bf16[8,8,128,128]{3,1,2,0:T(8,128)(2,1)} copy(bf16[8,8,128,128]{3,2,1,0:T(8,128)(2,1)S(1)} %bitcast.35) | data formatting | bytes 4194304
  (5 shorter events, 0.1 us)
Async XLA Ops:
  122.2 19.8 %all-to-all-start.3 = ((bf16[8,32,16,128]{3,1,2,0:T(8,128)(2,1)}), bf16[8,32,16,128]{3,1,2,0:T(8,128)(2,1)S(1)}, u32[]{:S(2)}, u32[]{:S(2)}) async-start(bf16[8,32,16,128]{3,1,2,0:T(8,128)(2,1)} %broadcast_in_dim.5), calls=%async_computation.3 | async-start | bytes 2097152 | tf_op jit(solution)/shard_map/all_to_all | solution.py:158
  127.0 15.8 %copy-start = (bf16[8,64,16,128]{3,2,1,0:T(8,128)(2,1)S(1)}, bf16[8,64,16,128]{3,2,1,0:T(8,128)(2,1)}, u32[]{:S(2)}) copy-start(bf16[8,64,16,128]{3,2,1,0:T(8,128)(2,1)} %shard_map.59) | copy-start | bytes 6291460

commit v9 on v8

--- a/solution.py
+++ b/solution.py
@@ -31,17 +31,16 @@
         out = lax.dot_general(lhs, rhs, (((1,), (1,)), ((), ())), preferred_element_type=jnp.float32)
         out_ref[:, c] = out.astype(out_ref.dtype).reshape(out_ref.shape[0], out_ref.shape[2], out_ref.shape[3])
 
-def smooth(sky3, beam, pattern, parts):
+def smooth(sky3, beam, pat_t, parts, first, steps):
     chans, nblk, blk = sky3.shape
     taps = beam.shape[1]
-    pat_t = jnp.transpose(pattern, (2, 0, 1))
     return pl.pallas_call(
         smooth_kernel,
-        out_shape=jax.ShapeDtypeStruct((parts, chans, nblk // parts, blk), jnp.bfloat16),
-        grid=(chans // CT,),
-        in_specs=[pl.BlockSpec((taps, CT, nblk), lambda i: (0, i, 0)),
-                  pl.BlockSpec((CT, nblk, blk), lambda i: (i, 0, 0)),
-                  pl.BlockSpec((CT, taps, blk, blk), lambda i: (i, 0, 0, 0))],
+        out_shape=jax.ShapeDtypeStruct((parts, steps * CT, nblk // parts, blk), jnp.bfloat16),
+        grid=(steps,),
+        in_specs=[pl.BlockSpec((taps, CT, nblk), lambda i: (0, i + first, 0)),
+                  pl.BlockSpec((CT, nblk, blk), lambda i: (i + first, 0, 0)),
+                  pl.BlockSpec((CT, taps, blk, blk), lambda i: (i + first, 0, 0, 0))],
         out_specs=pl.BlockSpec((parts, CT, nblk // parts, blk), lambda i: (0, i, 0, 0)),
     )(pat_t, sky3, beam)
 
@@ -140,8 +139,16 @@
     block_count = pix_group // BLK
     blocks = sky_cube.reshape(chans, block_count, BLK)
     n_chan = lax.axis_size("chan")
-    chunks = smooth(blocks, beam_blocks, pattern, n_chan)
-    by_pixel = lax.all_to_all(chunks, "chan", 0, 0, tiled=True)
+    halves = []
+    got = []
+    pat_t = jnp.transpose(pattern, (2, 0, 1))
+    steps = chans // CT // 2
+    for part in range(2):
+        c_part = smooth(blocks, beam_blocks, pat_t, n_chan, part * steps, steps)
+        halves.append(c_part)
+        got.append(lax.all_to_all(c_part, "chan", 0, 0, tiled=True))
+    chunks = jnp.concatenate(halves, axis=1)
+    by_pixel = jnp.concatenate(got, axis=1)
     by_pixel = by_pixel.reshape((n_chan * chans,) + by_pixel.shape[2:])
     all_pixels = pix_group * lax.axis_size("pix")
     basis = start_modes

time: 149 us -> 148 us (level)
  blocking collectives: 74.7 us -> 61.9 us
  starting transfers between devices: 4.81 us -> 10.8 us
  Pallas kernels: 37 us -> 39.6 us
  waiting for transfers between devices: 15 us -> 17.5 us
    all_to_all x1, blocking collectives: 32.1 us -> 19.4 us  [local(): got.append(lax.all_to_all(c_part, 'chan', 0, 0, tiled=True))]
    all_to_all x0 -> x1, starting transfers between devices: none -> 5.96 us  [local(): got.append(lax.all_to_all(c_part, 'chan', 0, 0, tiled=True))]
    pallas_call x1 -> x2, Pallas kernels: 22.3 us -> 24.8 us  [smooth(): pl.pallas_call(smooth_kernel, out_shape=jax.ShapeDtypeStruct((parts, step...]
    all_to_all x0 -> x1, waiting for transfers between devices: none -> 2.54 us  [local(): got.append(lax.all_to_all(c_part, 'chan', 0, 0, tiled=True))]
    unnamed x5 -> x7, local copies, waits for them, and re-layouts: 7.13 us -> 7.13 us
  transfers between devices with their start and end apart: 1 -> 2, of which waited for: 1 -> 2; matrix products, arithmetic and copies ran while one was open for 0% -> 0% of each run, Pallas kernels for 0% -> 8%
where the time goes in v9:
time: 148 us; the launch traced here: 147 us
  blocking collectives  61.9 us (42%)
  Pallas kernels  39.6 us (27%)
  waiting for transfers between devices  17.5 us (12%)
  starting transfers between devices  10.8 us (7%)
  local copies, waits for them, and re-layouts  9.81 us (7%)
  other arithmetic  4.56 us (3%)
  matrix products  2.57 us (2%)
    pallas_call x2, Pallas kernels, smooth(): pl.pallas_call(smooth_kernel, out_shape=jax.ShapeDtypeStruct((parts, step...  24.8 us
    all_to_all x1, blocking collectives, sum_all(): got = lax.all_to_all(pieces, AXES, 0, 0, tiled=False)  23.5 us
    all_to_all x1, blocking collectives, local(): got.append(lax.all_to_all(c_part, 'chan', 0, 0, tiled=True))  19.4 us
    all_to_all x1, blocking collectives, sum_all(): return lax.all_to_all(spread, AXES, 0, 0, tiled=False)  19.1 us
    all_to_all x1, waiting for transfers between devices, local(): gathered = lax.all_to_all(spread, 'chan', 0, 0, tiled=False)  15 us
    pallas_call x1, Pallas kernels, sweeps(): pl.pallas_call(functools.partial(sweep_kernel, iters=iters, nb=nb, bs=bs,...  14.8 us
    unnamed x7, local copies, waits for them, and re-layouts  7.13 us
    all_to_all x1, starting transfers between devices, local(): got.append(lax.all_to_all(c_part, 'chan', 0, 0, tiled=True))  5.96 us
  transfers between devices with their start and end apart: 2, of which 2 were waited for; matrix products, arithmetic and copies ran while one was open for 0% of the time, Pallas kernels for 8%

profile of v9, /device:TPU:1, one launch (start us, length us, event | category | flops | bytes accessed | tf_op | source)
XLA Modules:
  0.0 147.5 jit_solution(15326155999284036416)
XLA Ops:
  0.6 3.5 %copy.21 = bf16[8,8,128,128]{3,2,1,0:T(8,128)(2,1)} copy(bf16[8,8,128,128]{3,1,2,0:T(8,128)(2,1)} %bitcast.38) | data formatting | bytes 4194304
  4.1 12.4 %shard_map.59 = bf16[8,32,16,128]{3,2,1,0:T(8,128)(2,1)} custom-call(s32[9,64,128]{2,1,0:T(8,128)} %bitcast.40, bf16[64,128,128]{2,1,0:T(8,128)(2,1)} %bitcast.32, bf16[64,9,128,128]{3,2,1,0:T(8,128)(2,1)} %beam_ref.3), custom_call_target="tpu_custom_call" | custom-call | tf_op jit(solution)/shard_map/pallas_call | solution.py:37
  16.5 6.0 %all-to-all-start = ((bf16[8,32,16,128]{3,2,1,0:T(8,128)(2,1)}), bf16[8,32,16,128]{3,2,1,0:T(8,128)(2,1)S(1)}, u32[]{:S(2)}, u32[]{:S(2)}) async-start(bf16[8,32,16,128]{3,2,1,0:T(8,128)(2,1)} %shard_map.59), calls=%async_computation | async-start | bytes 2097152 | tf_op jit(solution)/shard_map/all_to_all | solution.py:149
  22.5 12.4 %shard_map.60 = bf16[8,32,16,128]{3,2,1,0:T(8,128)(2,1)} custom-call(s32[9,64,128]{2,1,0:T(8,128)} %bitcast.41, bf16[64,128,128]{2,1,0:T(8,128)(2,1)} %bitcast.33, bf16[64,9,128,128]{3,2,1,0:T(8,128)(2,1)} %beam_ref.3), custom_call_target="tpu_custom_call" | custom-call | tf_op jit(solution)/shard_map/pallas_call | solution.py:37
  34.9 2.5 %all-to-all-done = bf16[8,32,16,128]{3,2,1,0:T(8,128)(2,1)S(1)} async-done(((bf16[8,32,16,128]{3,2,1,0:T(8,128)(2,1)}), bf16[8,32,16,128]{3,2,1,0:T(8,128)(2,1)S(1)}, u32[]{:S(2)}, u32[]{:S(2)}) %all-to-all-start) | async-done | bytes 1048608 | tf_op jit(solution)/shard_map/all_to_all | solution.py:149
  37.4 19.4 %all_to_all.32 = bf16[8,32,16,128]{3,2,1,0:T(8,128)(2,1)S(1)} all-to-all(bf16[8,32,16,128]{3,2,1,0:T(8,128)(2,1)} %shard_map.60), channel_id=1, replica_groups=mesh['chan'=8,'pix'=16] {'chan'}, dimensions={0} | all-to-all | bytes 2097152 | tf_op jit(solution)/shard_map/all_to_all | solution.py:149
  57.0 1.3 fusion.5
  58.5 0.2 fusion.13
  58.7 0.5 copy.15
  59.2 23.5 %all_to_all.33 = f32[128,1,1280]{2,1,0:T(1,128)S(1)} all-to-all(f32[128,1,1280]{2,1,0:T(1,128)S(1)} %copy.15), channel_id=1, replica_groups=mesh['chan'=8,'pix'=16] {'chan','pix'}, dimensions={0} | all-to-all | bytes 1310720 | tf_op jit(solution)/shard_map/all_to_all | solution.py:115
  82.7 0.4 reduce_sum.9
  83.1 0.3 broadcast_in_dim.4
  83.4 19.1 %all_to_all.34 = f32[128,1,1280]{2,1,0:T(1,128)S(1)} all-to-all(f32[128,1,1280]{2,1,0:T(1,128)S(1)} %broadcast_in_dim.4), channel_id=1, replica_groups=mesh['chan'=8,'pix'=16] {'chan','pix'}, dimensions={0} | all-to-all | bytes 1310720 | tf_op jit(solution)/shard_map/all_to_all | solution.py:118
  102.5 0.9 copy.35
  103.4 14.8 %shard_map.61 = f32[32,512]{1,0:T(8,128)} custom-call(f32[128,1280]{1,0:T(8,128)} %bitcast.37, f32[32,512]{1,0:T(8,128)} %bitcast.43), custom_call_target="tpu_custom_call" | custom-call | tf_op jit(solution)/shard_map/pallas_call | solution.py:106
  118.2 0.8 bitcast_convert_fusion
  119.0 0.5 fusion.8
  119.5 1.2 broadcast_in_dim.5
  120.6 4.8 %all-to-all-start.4 = ((bf16[8,32,16,128]{3,1,2,0:T(8,128)(2,1)}), bf16[8,32,16,128]{3,1,2,0:T(8,128)(2,1)S(1)}, u32[]{:S(2)}, u32[]{:S(2)}) async-start(bf16[8,32,16,128]{3,1,2,0:T(8,128)(2,1)} %broadcast_in_dim.5), calls=%async_computation.4 | async-start | bytes 2097152 | tf_op jit(solution)/shard_map/all_to_all | solution.py:165
  125.4 15.0 %all-to-all-done.4 = bf16[8,32,16,128]{3,1,2,0:T(8,128)(2,1)S(1)} async-done(((bf16[8,32,16,128]{3,1,2,0:T(8,128)(2,1)}), bf16[8,32,16,128]{3,1,2,0:T(8,128)(2,1)S(1)}, u32[]{:S(2)}, u32[]{:S(2)}) %all-to-all-start.4) | async-done | bytes 1048608 | tf_op jit(solution)/shard_map/all_to_all | solution.py:165
  140.4 0.8 fusion.16
  141.3 2.8 %fusion = bf16[64,8,16,128]{3,2,0,1:T(8,128)(2,1)S(1)} fusion(f32[64,8,16,128]{3,0,2,1:T(8,128)S(1)} %fusion.16, bf16[8,32,16,128]{3,2,1,0:T(8,128)(2,1)S(1)} %copy-done.1, bf16[8,32,16,128]{3,2,1,0:T(8,128)(2,1)S(1)} %copy-done), kind=kLoop, calls=%fused_computation.1 | loop fusion | flops 4194304 | bytes 8388608 | tf_op jit(solution)/shard_map/convert_element_type | solution.py:169
  144.1 0.6 copy.18
  144.7 2.8 %copy.34 = bf16[8,8,128,128]{3,1,2,0:T(8,128)(2,1)} copy(bf16[8,8,128,128]{3,2,1,0:T(8,128)(2,1)S(1)} %bitcast.36) | data formatting | bytes 4194304
  (10 shorter events, 0.3 us)
Async XLA Ops:
  16.5 20.9 %all-to-all-start = ((bf16[8,32,16,128]{3,2,1,0:T(8,128)(2,1)}), bf16[8,32,16,128]{3,2,1,0:T(8,128)(2,1)S(1)}, u32[]{:S(2)}, u32[]{:S(2)}) async-start(bf16[8,32,16,128]{3,2,1,0:T(8,128)(2,1)} %shard_map.59), calls=%async_computation | async-start | bytes 2097152 | tf_op jit(solution)/shard_map/all_to_all | solution.py:149
  120.6 19.8 %all-to-all-start.4 = ((bf16[8,32,16,128]{3,1,2,0:T(8,128)(2,1)}), bf16[8,32,16,128]{3,1,2,0:T(8,128)(2,1)S(1)}, u32[]{:S(2)}, u32[]{:S(2)}) async-start(bf16[8,32,16,128]{3,1,2,0:T(8,128)(2,1)} %broadcast_in_dim.5), calls=%async_computation.4 | async-start | bytes 2097152 | tf_op jit(solution)/shard_map/all_to_all | solution.py:165
  125.4 15.8 %copy-start = (bf16[8,32,16,128]{3,2,1,0:T(8,128)(2,1)S(1)}, bf16[8,32,16,128]{3,2,1,0:T(8,128)(2,1)}, u32[]{:S(2)}) copy-start(bf16[8,32,16,128]{3,2,1,0:T(8,128)(2,1)} %shard_map.59) | copy-start | bytes 3145732
  125.4 15.8 %copy-start.1 = (bf16[8,32,16,128]{3,2,1,0:T(8,128)(2,1)S(1)}, bf16[8,32,16,128]{3,2,1,0:T(8,128)(2,1)}, u32[]{:S(2)}) copy-start(bf16[8,32,16,128]{3,2,1,0:T(8,128)(2,1)} %shard_map.60) | copy-start | bytes 3145732

commit v10 on v9

--- a/solution.py
+++ b/solution.py
@@ -13,22 +13,20 @@
 def smooth_kernel(pat_ref, sky_ref, beam_ref, out_ref):
     taps = beam_ref.shape[1]
     nblk = sky_ref.shape[1]
-    lane = lax.broadcasted_iota(jnp.int32, (nblk, nblk), 1).astype(jnp.float32)
-    row = lax.broadcasted_iota(jnp.int32, (nblk, nblk), 0)
-    eye = jnp.where(row == lax.broadcasted_iota(jnp.int32, (nblk, nblk), 1), 1.0, 0.0).astype(jnp.bfloat16)
+    ct = sky_ref.shape[0]
+    sub = lax.broadcasted_iota(jnp.int32, (nblk, nblk), 0)
     one = jnp.ones((nblk, nblk), jnp.float32)
     zero = jnp.zeros((nblk, nblk), jnp.float32)
-    ct = sky_ref.shape[0]
-    pat = pat_ref[...].reshape(taps * ct, nblk).astype(jnp.float32).astype(jnp.bfloat16)
-    pat = lax.dot_general(eye, pat, (((1,), (1,)), ((), ())), preferred_element_type=jnp.float32)
+    pat = pat_ref[...]
     for c in range(ct):
-        sel = jnp.concatenate(
-            [jnp.where(pat[:, k * ct + c:k * ct + c + 1] == lane, one, zero).astype(jnp.bfloat16)
-             for k in range(taps)], axis=0)
-        src = jnp.dot(sel, sky_ref[c], preferred_element_type=jnp.float32).astype(jnp.bfloat16)
-        lhs = jnp.concatenate([src[k * nblk:(k + 1) * nblk] for k in range(taps)], axis=1)
+        selt = jnp.concatenate(
+            [jnp.where(pat[k, c:c + 1, :] == sub, one, zero).astype(jnp.bfloat16) for k in range(taps)], axis=1)
+        srct = lax.dot_general(sky_ref[c], selt, (((0,), (0,)), ((), ())),
+                               preferred_element_type=jnp.float32).astype(jnp.bfloat16)
+        stacked = jnp.concatenate([srct[:, k * nblk:(k + 1) * nblk] for k in range(taps)], axis=0)
         rhs = jnp.concatenate([beam_ref[c, k] for k in range(taps)], axis=1)
-        out = lax.dot_general(lhs, rhs, (((1,), (1,)), ((), ())), preferred_element_type=jnp.float32)
+        outt = jnp.dot(rhs, stacked, preferred_element_type=jnp.float32)
+        out = outt.T
         out_ref[:, c] = out.astype(out_ref.dtype).reshape(out_ref.shape[0], out_ref.shape[2], out_ref.shape[3])
 
 def smooth(sky3, beam, pat_t, parts, first, steps):
@@ -83,21 +81,18 @@
         it = jnp.dot(bt, g, precision=HI, preferred_element_type=jnp.float32)
         a = lax.dot_general(it, it, (((1,), (1,)), ((), ())), precision=HI,
                             preferred_element_type=jnp.float32)
-        low = jnp.zeros((m, m), jnp.float32)
+        rest = jnp.where(rows == cols, 1.0, 0.0).astype(jnp.float32)
+        inv = jnp.zeros((m, m), jnp.float32)
         for j in range(m):
             d = jnp.sqrt(a[j:j + 1, j:j + 1])
             col = jnp.where(rows[:, j:j + 1] >= j, a[:, j:j + 1] / d, 0.0)
             row = jnp.where(cols[j:j + 1, :] >= j, a[j:j + 1, :] / d, 0.0)
-            low = jnp.where(cols == j, col, low)
             a = a - col * row
-        bad = jnp.isnan(jnp.sum(low, keepdims=True))
-        low = jnp.where(bad, jnp.nan, low)
-        rest = jnp.where(rows == cols, 1.0, 0.0).astype(jnp.float32)
-        inv = jnp.zeros((m, m), jnp.float32)
-        for i in range(m):
-            r = rest[i:i + 1, :] / low[i:i + 1, i:i + 1]
-            inv = jnp.where(rows == i, r, inv)
-            rest = rest - low[:, i:i + 1] * r
+            r = rest[j:j + 1, :] / d
+            inv = jnp.where(rows == j, r, inv)
+            rest = rest - col * r
+        bad = jnp.isnan(jnp.sum(inv, keepdims=True))
+        inv = jnp.where(bad, jnp.nan, inv)
         bt = jnp.dot(inv, it, precision=HI, preferred_element_type=jnp.float32)
     o_ref[...] = bt
 

time: 148 us -> 146 us (0.986)
  Pallas kernels: 39.6 us -> 36.9 us
    pallas_call x2, Pallas kernels: 24.8 us -> 22.8 us  [smooth(): pl.pallas_call(smooth_kernel, out_shape=jax.ShapeDtypeStruct((parts, step...]
where the time goes in v10:
time: 146 us
  blocking collectives  61.9 us (42%)
  Pallas kernels  36.9 us (25%)
  waiting for transfers between devices  18.6 us (13%)
  starting transfers between devices  10.8 us (7%)
  local copies, waits for them, and re-layouts  9.81 us (7%)
  other arithmetic  4.56 us (3%)
  matrix products  2.56 us (2%)
    all_to_all x1, blocking collectives, sum_all(): got = lax.all_to_all(pieces, AXES, 0, 0, tiled=False)  23.5 us
    pallas_call x2, Pallas kernels, smooth(): pl.pallas_call(smooth_kernel, out_shape=jax.ShapeDtypeStruct((parts, step...  22.8 us
    all_to_all x1, blocking collectives, local(): got.append(lax.all_to_all(c_part, 'chan', 0, 0, tiled=True))  19.4 us
    all_to_all x1, blocking collectives, sum_all(): return lax.all_to_all(spread, AXES, 0, 0, tiled=False)  19.1 us
    all_to_all x1, waiting for transfers between devices, local(): gathered = lax.all_to_all(spread, 'chan', 0, 0, tiled=False)  15 us
    pallas_call x1, Pallas kernels, sweeps(): pl.pallas_call(functools.partial(sweep_kernel, iters=iters, nb=nb, bs=bs,...  14.1 us
    unnamed x7, local copies, waits for them, and re-layouts  7.13 us
    all_to_all x1, starting transfers between devices, local(): got.append(lax.all_to_all(c_part, 'chan', 0, 0, tiled=True))  5.96 us
  transfers between devices with their start and end apart: 2, of which 2 were waited for; matrix products, arithmetic and copies ran while one was open for 0% of the time, Pallas kernels for 8%

profile of v10, /device:TPU:1, one launch (start us, length us, event | category | flops | bytes accessed | tf_op | source)
XLA Modules:
  0.0 145.8 jit_solution(8235433145677699304)
XLA Ops:
  0.6 3.5 %copy.21 = bf16[8,8,128,128]{3,2,1,0:T(8,128)(2,1)} copy(bf16[8,8,128,128]{3,1,2,0:T(8,128)(2,1)} %bitcast.38) | data formatting | bytes 4194304
  4.1 11.4 %shard_map.59 = bf16[8,32,16,128]{3,2,1,0:T(8,128)(2,1)} custom-call(s32[9,64,128]{2,1,0:T(8,128)} %bitcast.40, bf16[64,128,128]{2,1,0:T(8,128)(2,1)} %bitcast.32, bf16[64,9,128,128]{3,2,1,0:T(8,128)(2,1)} %beam_ref.3), custom_call_target="tpu_custom_call" | custom-call | tf_op jit(solution)/shard_map/pallas_call | solution.py:35
  15.5 6.0 %all-to-all-start = ((bf16[8,32,16,128]{3,2,1,0:T(8,128)(2,1)}), bf16[8,32,16,128]{3,2,1,0:T(8,128)(2,1)S(1)}, u32[]{:S(2)}, u32[]{:S(2)}) async-start(bf16[8,32,16,128]{3,2,1,0:T(8,128)(2,1)} %shard_map.59), calls=%async_computation | async-start | bytes 2097152 | tf_op jit(solution)/shard_map/all_to_all | solution.py:144
  21.5 11.4 %shard_map.60 = bf16[8,32,16,128]{3,2,1,0:T(8,128)(2,1)} custom-call(s32[9,64,128]{2,1,0:T(8,128)} %bitcast.41, bf16[64,128,128]{2,1,0:T(8,128)(2,1)} %bitcast.33, bf16[64,9,128,128]{3,2,1,0:T(8,128)(2,1)} %beam_ref.3), custom_call_target="tpu_custom_call" | custom-call | tf_op jit(solution)/shard_map/pallas_call | solution.py:35
  32.9 3.6 %all-to-all-done = bf16[8,32,16,128]{3,2,1,0:T(8,128)(2,1)S(1)} async-done(((bf16[8,32,16,128]{3,2,1,0:T(8,128)(2,1)}), bf16[8,32,16,128]{3,2,1,0:T(8,128)(2,1)S(1)}, u32[]{:S(2)}, u32[]{:S(2)}) %all-to-all-start) | async-done | bytes 1048608 | tf_op jit(solution)/shard_map/all_to_all | solution.py:144
  36.4 19.4 %all_to_all.32 = bf16[8,32,16,128]{3,2,1,0:T(8,128)(2,1)S(1)} all-to-all(bf16[8,32,16,128]{3,2,1,0:T(8,128)(2,1)} %shard_map.60), channel_id=1, replica_groups=mesh['chan'=8,'pix'=16] {'chan'}, dimensions={0} | all-to-all | bytes 2097152 | tf_op jit(solution)/shard_map/all_to_all | solution.py:144
  56.0 1.3 fusion.5
  57.5 0.2 fusion.13
  57.7 0.5 copy.15
  58.2 23.5 %all_to_all.33 = f32[128,1,1280]{2,1,0:T(1,128)S(1)} all-to-all(f32[128,1,1280]{2,1,0:T(1,128)S(1)} %copy.15), channel_id=1, replica_groups=mesh['chan'=8,'pix'=16] {'chan','pix'}, dimensions={0} | all-to-all | bytes 1310720 | tf_op jit(solution)/shard_map/all_to_all | solution.py:110
  81.7 0.4 reduce_sum.9
  82.1 0.3 broadcast_in_dim.4
  82.4 19.1 %all_to_all.34 = f32[128,1,1280]{2,1,0:T(1,128)S(1)} all-to-all(f32[128,1,1280]{2,1,0:T(1,128)S(1)} %broadcast_in_dim.4), channel_id=1, replica_groups=mesh['chan'=8,'pix'=16] {'chan','pix'}, dimensions={0} | all-to-all | bytes 1310720 | tf_op jit(solution)/shard_map/all_to_all | solution.py:113
  101.5 0.9 copy.35
  102.4 14.1 %shard_map.61 = f32[32,512]{1,0:T(8,128)} custom-call(f32[128,1280]{1,0:T(8,128)} %bitcast.37, f32[32,512]{1,0:T(8,128)} %bitcast.43), custom_call_target="tpu_custom_call" | custom-call | tf_op jit(solution)/shard_map/pallas_call | solution.py:101
  116.5 0.8 bitcast_convert_fusion
  117.4 0.5 fusion.8
  117.8 1.2 broadcast_in_dim.5
  119.0 4.8 %all-to-all-start.4 = ((bf16[8,32,16,128]{3,1,2,0:T(8,128)(2,1)}), bf16[8,32,16,128]{3,1,2,0:T(8,128)(2,1)S(1)}, u32[]{:S(2)}, u32[]{:S(2)}) async-start(bf16[8,32,16,128]{3,1,2,0:T(8,128)(2,1)} %broadcast_in_dim.5), calls=%async_computation.4 | async-start | bytes 2097152 | tf_op jit(solution)/shard_map/all_to_all | solution.py:160
  123.8 15.0 %all-to-all-done.4 = bf16[8,32,16,128]{3,1,2,0:T(8,128)(2,1)S(1)} async-done(((bf16[8,32,16,128]{3,1,2,0:T(8,128)(2,1)}), bf16[8,32,16,128]{3,1,2,0:T(8,128)(2,1)S(1)}, u32[]{:S(2)}, u32[]{:S(2)}) %all-to-all-start.4) | async-done | bytes 1048608 | tf_op jit(solution)/shard_map/all_to_all | solution.py:160
  138.8 0.8 fusion.16
  139.6 2.8 %fusion = bf16[64,8,16,128]{3,2,0,1:T(8,128)(2,1)S(1)} fusion(f32[64,8,16,128]{3,0,2,1:T(8,128)S(1)} %fusion.16, bf16[8,32,16,128]{3,2,1,0:T(8,128)(2,1)S(1)} %copy-done.1, bf16[8,32,16,128]{3,2,1,0:T(8,128)(2,1)S(1)} %copy-done), kind=kLoop, calls=%fused_computation.1 | loop fusion | flops 4194304 | bytes 8388608 | tf_op jit(solution)/shard_map/convert_element_type | solution.py:164
  142.5 0.6 copy.18
  143.1 2.8 %copy.34 = bf16[8,8,128,128]{3,1,2,0:T(8,128)(2,1)} copy(bf16[8,8,128,128]{3,2,1,0:T(8,128)(2,1)S(1)} %bitcast.36) | data formatting | bytes 4194304
  (10 shorter events, 0.3 us)
Async XLA Ops:
  15.5 20.9 %all-to-all-start = ((bf16[8,32,16,128]{3,2,1,0:T(8,128)(2,1)}), bf16[8,32,16,128]{3,2,1,0:T(8,128)(2,1)S(1)}, u32[]{:S(2)}, u32[]{:S(2)}) async-start(bf16[8,32,16,128]{3,2,1,0:T(8,128)(2,1)} %shard_map.59), calls=%async_computation | async-start | bytes 2097152 | tf_op jit(solution)/shard_map/all_to_all | solution.py:144
  119.0 19.8 %all-to-all-start.4 = ((bf16[8,32,16,128]{3,1,2,0:T(8,128)(2,1)}), bf16[8,32,16,128]{3,1,2,0:T(8,128)(2,1)S(1)}, u32[]{:S(2)}, u32[]{:S(2)}) async-start(bf16[8,32,16,128]{3,1,2,0:T(8,128)(2,1)} %broadcast_in_dim.5), calls=%async_computation.4 | async-start | bytes 2097152 | tf_op jit(solution)/shard_map/all_to_all | solution.py:160
  123.8 15.8 %copy-start = (bf16[8,32,16,128]{3,2,1,0:T(8,128)(2,1)S(1)}, bf16[8,32,16,128]{3,2,1,0:T(8,128)(2,1)}, u32[]{:S(2)}) copy-start(bf16[8,32,16,128]{3,2,1,0:T(8,128)(2,1)} %shard_map.59) | copy-start | bytes 3145732
  123.8 15.8 %copy-start.1 = (bf16[8,32,16,128]{3,2,1,0:T(8,128)(2,1)S(1)}, bf16[8,32,16,128]{3,2,1,0:T(8,128)(2,1)}, u32[]{:S(2)}) copy-start(bf16[8,32,16,128]{3,2,1,0:T(8,128)(2,1)} %shard_map.60) | copy-start | bytes 3145732

commit v11 on v10

--- a/solution.py
+++ b/solution.py
@@ -156,13 +156,20 @@
     basis = sweeps(packed, basis, ITERS, nb, partial_value.shape[0] // nb, 1.0 / all_pixels)
     modes_low = basis.astype(jnp.bfloat16)
     coeffs = jnp.einsum("cm,cbi->mbi", modes_low, by_pixel, preferred_element_type=jnp.float32).astype(jnp.bfloat16)
-    spread = jnp.broadcast_to(coeffs[None], (n_chan,) + coeffs.shape)
-    gathered = lax.all_to_all(spread, "chan", 0, 0, tiled=False)
     me = lax.axis_index("chan")
     my_modes = lax.dynamic_slice_in_dim(modes_low, me * chans, chans, axis=0)
-    removed = jnp.einsum("cm,jmbi->cjbi", my_modes, gathered, preferred_element_type=jnp.float32)
-    cleaned = (chunks.transpose(1, 0, 2, 3).astype(jnp.float32) - removed).astype(jnp.bfloat16)
-    cleaned = cleaned.reshape(chans, pix_group)
+    width = pix_group // n_chan
+    cleaned = jnp.zeros((chans, pix_group), jnp.bfloat16)
+    for shift in range(n_chan):
+        if shift:
+            part = lax.ppermute(coeffs, "chan", [(i, (i + shift) % n_chan) for i in range(n_chan)])
+        else:
+            part = coeffs
+        src = (me - shift) % n_chan
+        removed = jnp.einsum("cm,mbi->cbi", my_modes, part, preferred_element_type=jnp.float32)
+        mine = lax.dynamic_index_in_dim(chunks, src, axis=0, keepdims=False)
+        slab = (mine.astype(jnp.float32) - removed).astype(jnp.bfloat16).reshape(chans, width)
+        cleaned = lax.dynamic_update_slice_in_dim(cleaned, slab, src * width, axis=1)
     return (cleaned, basis)
 
 

time: 146 us -> 148 us (1.014)
  blocking collectives: 61.9 us -> 42.8 us
  starting transfers between devices: 10.8 us -> 21.9 us
  waiting for transfers between devices: 18.6 us -> 28 us
  local copies, waits for them, and re-layouts: 9.81 us -> 8.02 us
  matrix products: 2.56 us -> 4.32 us
    all_to_all x1 -> x0, blocking collectives: 19.1 us -> none  [sum_all(): return lax.all_to_all(spread, AXES, 0, 0, tiled=False)]
    ppermute x0 -> x7, starting transfers between devices: none -> 11.2 us  [local(): lax.ppermute(coeffs, 'chan', [(i, (i + shift) % n_chan) for i in range(n_...]
    ppermute x0 -> x7, waiting for transfers between devices: none -> 9.81 us  [local(): lax.ppermute(coeffs, 'chan', [(i, (i + shift) % n_chan) for i in range(n_...]
    dot_general x1 -> x8, matrix products: 0.8 us -> 2.55 us  [local(): jnp.einsum('cm,mbi->cbi', my_modes, part, preferred_element_type=jnp.floa...]
    unnamed x7 -> x8, local copies, waits for them, and re-layouts: 7.13 us -> 5.69 us
  transfers between devices with their start and end apart: 2 -> 9, of which waited for: 2 -> 5; matrix products, arithmetic and copies ran while one was open for 0% -> 3% of each run, Pallas kernels for 8% -> 8%
where the time goes in v11:
time: 148 us; the launch traced here: 147 us
  blocking collectives  42.8 us (29%)
  Pallas kernels  36.9 us (25%)
  waiting for transfers between devices  28 us (19%)
  starting transfers between devices  21.9 us (15%)
  local copies, waits for them, and re-layouts  8.02 us (5%)
  other arithmetic  4.34 us (3%)
  matrix products  4.32 us (3%)
    all_to_all x1, blocking collectives, sum_all(): got = lax.all_to_all(pieces, AXES, 0, 0, tiled=False)  23.5 us
    pallas_call x2, Pallas kernels, smooth(): pl.pallas_call(smooth_kernel, out_shape=jax.ShapeDtypeStruct((parts, step...  22.8 us
    all_to_all x1, blocking collectives, local(): got.append(lax.all_to_all(c_part, 'chan', 0, 0, tiled=True))  19.4 us
    all_to_all x1, waiting for transfers between devices, sum_all(): return lax.all_to_all(spread, AXES, 0, 0, tiled=False)  14.6 us
    pallas_call x1, Pallas kernels, sweeps(): pl.pallas_call(functools.partial(sweep_kernel, iters=iters, nb=nb, bs=bs,...  14.1 us
    ppermute x7, starting transfers between devices, local(): lax.ppermute(coeffs, 'chan', [(i, (i + shift) % n_chan) for i in range(n_...  11.2 us
    ppermute x7, waiting for transfers between devices, local(): lax.ppermute(coeffs, 'chan', [(i, (i + shift) % n_chan) for i in range(n_...  9.81 us
    all_to_all x1, starting transfers between devices, local(): got.append(lax.all_to_all(c_part, 'chan', 0, 0, tiled=True))  5.96 us
  transfers between devices with their start and end apart: 9, of which 5 were waited for; matrix products, arithmetic and copies ran while one was open for 3% of the time, Pallas kernels for 8%

profile of v11, /device:TPU:1, one launch (start us, length us, event | category | flops | bytes accessed | tf_op | source)
XLA Modules:
  0.0 147.4 jit_solution(16982866222462058307)
XLA Ops:
  0.6 3.5 %copy.30 = bf16[8,8,128,128]{3,2,1,0:T(8,128)(2,1)} copy(bf16[8,8,128,128]{3,1,2,0:T(8,128)(2,1)} %bitcast.95) | data formatting | bytes 4194304
  4.1 11.4 %shard_map.59 = bf16[8,32,16,128]{3,2,1,0:T(8,128)(2,1)} custom-call(s32[9,64,128]{2,1,0:T(8,128)} %bitcast.96, bf16[64,128,128]{2,1,0:T(8,128)(2,1)} %bitcast.90, bf16[64,9,128,128]{3,2,1,0:T(8,128)(2,1)} %beam_ref.3), custom_call_target="tpu_custom_call" | custom-call | tf_op jit(solution)/shard_map/pallas_call | solution.py:35
  15.5 6.0 %all-to-all-start = ((bf16[8,32,16,128]{3,2,1,0:T(8,128)(2,1)}), bf16[8,32,16,128]{3,2,1,0:T(8,128)(2,1)S(1)}, u32[]{:S(2)}, u32[]{:S(2)}) async-start(bf16[8,32,16,128]{3,2,1,0:T(8,128)(2,1)} %shard_map.59), calls=%async_computation | async-start | bytes 2097152 | tf_op jit(solution)/shard_map/all_to_all | solution.py:144
  21.5 11.4 %shard_map.60 = bf16[8,32,16,128]{3,2,1,0:T(8,128)(2,1)} custom-call(s32[9,64,128]{2,1,0:T(8,128)} %bitcast.97, bf16[64,128,128]{2,1,0:T(8,128)(2,1)} %bitcast.91, bf16[64,9,128,128]{3,2,1,0:T(8,128)(2,1)} %beam_ref.3), custom_call_target="tpu_custom_call" | custom-call | tf_op jit(solution)/shard_map/pallas_call | solution.py:35
  32.9 3.6 %all-to-all-done = bf16[8,32,16,128]{3,2,1,0:T(8,128)(2,1)S(1)} async-done(((bf16[8,32,16,128]{3,2,1,0:T(8,128)(2,1)}), bf16[8,32,16,128]{3,2,1,0:T(8,128)(2,1)S(1)}, u32[]{:S(2)}, u32[]{:S(2)}) %all-to-all-start) | async-done | bytes 1048608 | tf_op jit(solution)/shard_map/all_to_all | solution.py:144
  36.4 19.4 %all_to_all.27 = bf16[8,32,16,128]{3,2,1,0:T(8,128)(2,1)S(1)} all-to-all(bf16[8,32,16,128]{3,2,1,0:T(8,128)(2,1)} %shard_map.60), channel_id=1, replica_groups=mesh['chan'=8,'pix'=16] {'chan'}, dimensions={0} | all-to-all | bytes 2097152 | tf_op jit(solution)/shard_map/all_to_all | solution.py:144
  56.0 1.3 fusion.4
  58.2 23.5 %all_to_all.28 = f32[128,1,1280]{2,1,0:T(1,128)S(1)} all-to-all(f32[128,1,1280]{2,1,0:T(1,128)S(1)} %copy.19), channel_id=1, replica_groups=mesh['chan'=8,'pix'=16] {'chan','pix'}, dimensions={0} | all-to-all | bytes 1310720 | tf_op jit(solution)/shard_map/all_to_all | solution.py:110
  82.1 1.2 broadcast_in_dim.10
  83.3 4.8 %all-to-all-start.3 = ((f32[128,1,1280]{2,1,0:T(1,128)}), f32[128,1,1280]{2,1,0:T(1,128)S(1)}, u32[]{:S(2)}, u32[]{:S(2)}) async-start(f32[128,1,1280]{2,1,0:T(1,128)} %broadcast_in_dim.10), calls=%async_computation.3 | async-start | bytes 1310720 | tf_op jit(solution)/shard_map/all_to_all | solution.py:113
  88.2 14.6 %all-to-all-done.3 = f32[128,1,1280]{2,1,0:T(1,128)S(1)} async-done(((f32[128,1,1280]{2,1,0:T(1,128)}), f32[128,1,1280]{2,1,0:T(1,128)S(1)}, u32[]{:S(2)}, u32[]{:S(2)}) %all-to-all-start.3) | async-done | bytes 655392 | tf_op jit(solution)/shard_map/all_to_all | solution.py:113
  103.7 14.1 %shard_map.61 = f32[32,512]{1,0:T(8,128)} custom-call(f32[128,1280]{1,0:T(8,128)} %bitcast.94, f32[32,512]{1,0:T(8,128)} %bitcast.107), custom_call_target="tpu_custom_call" | custom-call | tf_op jit(solution)/shard_map/pallas_call | solution.py:101
  119.2 2.1 %collective-permute-start.4 = (bf16[32,16,128]{2,0,1:T(8,128)(2,1)S(1)}, bf16[32,16,128]{2,0,1:T(8,128)(2,1)S(1)}, u32[]{:S(2)}, u32[]{:S(2)}) collective-permute-start(bf16[32,16,128]{2,0,1:T(8,128)(2,1)S(1)} %fusion.7), channel_id=1, source_target_pairs={{0,80},{16,96},{32,112},{48,0},{64,16},{80,32},{96,48},{112,64},{1... | collective-permute-start | bytes 393224 | tf_op jit(solution)/shard_map/ppermute | solution.py:165
  121.3 1.3 collective-permute-start.3
  122.6 1.2 collective-permute-start.2
  123.8 1.7 %collective-permute-start.5 = (bf16[32,16,128]{2,0,1:T(8,128)(2,1)S(1)}, bf16[32,16,128]{2,0,1:T(8,128)(2,1)S(1)}, u32[]{:S(2)}, u32[]{:S(2)}) collective-permute-start(bf16[32,16,128]{2,0,1:T(8,128)(2,1)S(1)} %fusion.7), channel_id=1, source_target_pairs={{0,96},{16,112},{32,0},{48,16},{64,32},{80,48},{96,64},{112,80},{1... | collective-permute-start | bytes 393224 | tf_op jit(solution)/shard_map/ppermute | solution.py:165
  125.8 7.2 %collective-permute-done.1 = bf16[32,16,128]{2,0,1:T(8,128)(2,1)S(1)} collective-permute-done((bf16[32,16,128]{2,0,1:T(8,128)(2,1)S(1)}, bf16[32,16,128]{2,0,1:T(8,128)(2,1)S(1)}, u32[]{:S(2)}, u32[]{:S(2)}) %collective-permute-start.1) | collective-permute-done | bytes 131104 | tf_op jit(solution)/shard_map/ppermute | solution.py:165
  133.1 1.0 collective-permute-start
  134.4 1.6 %collective-permute-done = bf16[32,16,128]{2,0,1:T(8,128)(2,1)S(1)} collective-permute-done((bf16[32,16,128]{2,0,1:T(8,128)(2,1)S(1)}, bf16[32,16,128]{2,0,1:T(8,128)(2,1)S(1)}, u32[]{:S(2)}, u32[]{:S(2)}) %collective-permute-start) | collective-permute-done | bytes 131104 | tf_op jit(solution)/shard_map/ppermute | solution.py:165
  136.0 3.8 %collective-permute-start.6 = (bf16[32,16,128]{2,0,1:T(8,128)(2,1)S(1)}, bf16[32,16,128]{2,0,1:T(8,128)(2,1)S(1)}, u32[]{:S(2)}, u32[]{:S(2)}) collective-permute-start(bf16[32,16,128]{2,0,1:T(8,128)(2,1)S(1)} %fusion.7), channel_id=1, source_target_pairs={{0,112},{16,0},{32,16},{48,32},{64,48},{80,64},{96,80},{112,96},{1... | collective-permute-start | bytes 393224 | tf_op jit(solution)/shard_map/ppermute | solution.py:165
  140.2 0.9 collective-permute-done.6
  141.4 1.3 fusion.14
  144.4 1.3 fusion.15
  146.1 1.3 copy-done.2
  (39 shorter events, 6.8 us)
Async XLA Ops:
  15.5 20.9 %all-to-all-start = ((bf16[8,32,16,128]{3,2,1,0:T(8,128)(2,1)}), bf16[8,32,16,128]{3,2,1,0:T(8,128)(2,1)S(1)}, u32[]{:S(2)}, u32[]{:S(2)}) async-start(bf16[8,32,16,128]{3,2,1,0:T(8,128)(2,1)} %shard_map.59), calls=%async_computation | async-start | bytes 2097152 | tf_op jit(solution)/shard_map/all_to_all | solution.py:144
  83.3 19.6 %all-to-all-start.3 = ((f32[128,1,1280]{2,1,0:T(1,128)}), f32[128,1,1280]{2,1,0:T(1,128)S(1)}, u32[]{:S(2)}, u32[]{:S(2)}) async-start(f32[128,1,1280]{2,1,0:T(1,128)} %broadcast_in_dim.10), calls=%async_computation.3 | async-start | bytes 1310720 | tf_op jit(solution)/shard_map/all_to_all | solution.py:113
  118.7 22.7 %copy-start = (bf16[8,32,16,128]{3,2,1,0:T(8,128)(2,1)S(1)}, bf16[8,32,16,128]{3,2,1,0:T(8,128)(2,1)}, u32[]{:S(2)}) copy-start(bf16[8,32,16,128]{3,2,1,0:T(8,128)(2,1)} %shard_map.59) | copy-start | bytes 3145732
  118.7 22.8 %copy-start.1 = (bf16[8,32,16,128]{3,2,1,0:T(8,128)(2,1)S(1)}, bf16[8,32,16,128]{3,2,1,0:T(8,128)(2,1)}, u32[]{:S(2)}) copy-start(bf16[8,32,16,128]{3,2,1,0:T(8,128)(2,1)} %shard_map.60) | copy-start | bytes 3145732
  119.2 23.9 %collective-permute-start.4 = (bf16[32,16,128]{2,0,1:T(8,128)(2,1)S(1)}, bf16[32,16,128]{2,0,1:T(8,128)(2,1)S(1)}, u32[]{:S(2)}, u32[]{:S(2)}) collective-permute-start(bf16[32,16,128]{2,0,1:T(8,128)(2,1)S(1)} %fusion.7), channel_id=1, source_target_pairs={{0,80},{16,96},{32,112},{48,0},{64,16},{80,32},{96,48},{112,64},{1... | collective-permute-start | bytes 393224 | tf_op jit(solution)/shard_map/ppermute | solution.py:165
  121.3 22.1 %collective-permute-start.3 = (bf16[32,16,128]{2,0,1:T(8,128)(2,1)S(1)}, bf16[32,16,128]{2,0,1:T(8,128)(2,1)S(1)}, u32[]{:S(2)}, u32[]{:S(2)}) collective-permute-start(bf16[32,16,128]{2,0,1:T(8,128)(2,1)S(1)} %fusion.7), channel_id=1, source_target_pairs={{0,64},{16,80},{32,96},{48,112},{64,0},{80,16},{96,32},{112,48},{1... | collective-permute-start | bytes 393224 | tf_op jit(solution)/shard_map/ppermute | solution.py:165
  122.6 21.2 %collective-permute-start.2 = (bf16[32,16,128]{2,0,1:T(8,128)(2,1)S(1)}, bf16[32,16,128]{2,0,1:T(8,128)(2,1)S(1)}, u32[]{:S(2)}, u32[]{:S(2)}) collective-permute-start(bf16[32,16,128]{2,0,1:T(8,128)(2,1)S(1)} %fusion.7), channel_id=1, source_target_pairs={{0,48},{16,64},{32,80},{48,96},{64,112},{80,0},{96,16},{112,32},{1... | collective-permute-start | bytes 393224 | tf_op jit(solution)/shard_map/ppermute | solution.py:165
  123.8 20.3 %collective-permute-start.5 = (bf16[32,16,128]{2,0,1:T(8,128)(2,1)S(1)}, bf16[32,16,128]{2,0,1:T(8,128)(2,1)S(1)}, u32[]{:S(2)}, u32[]{:S(2)}) collective-permute-start(bf16[32,16,128]{2,0,1:T(8,128)(2,1)S(1)} %fusion.7), channel_id=1, source_target_pairs={{0,96},{16,112},{32,0},{48,16},{64,32},{80,48},{96,64},{112,80},{1... | collective-permute-start | bytes 393224 | tf_op jit(solution)/shard_map/ppermute | solution.py:165
  125.5 7.6 %collective-permute-start.1 = (bf16[32,16,128]{2,0,1:T(8,128)(2,1)S(1)}, bf16[32,16,128]{2,0,1:T(8,128)(2,1)S(1)}, u32[]{:S(2)}, u32[]{:S(2)}) collective-permute-start(bf16[32,16,128]{2,0,1:T(8,128)(2,1)S(1)} %fusion.7), channel_id=1, source_target_pairs={{0,32},{16,48},{32,64},{48,80},{64,96},{80,112},{96,0},{112,16},{1... | collective-permute-start | bytes 393224 | tf_op jit(solution)/shard_map/ppermute | solution.py:165
  133.1 2.9 %collective-permute-start = (bf16[32,16,128]{2,0,1:T(8,128)(2,1)S(1)}, bf16[32,16,128]{2,0,1:T(8,128)(2,1)S(1)}, u32[]{:S(2)}, u32[]{:S(2)}) collective-permute-start(bf16[32,16,128]{2,0,1:T(8,128)(2,1)S(1)} %fusion.7), channel_id=1, source_target_pairs={{0,16},{16,32},{32,48},{48,64},{64,80},{80,96},{96,112},{112,0},{1... | collective-permute-start | bytes 393224 | tf_op jit(solution)/shard_map/ppermute | solution.py:165
  136.0 5.1 %collective-permute-start.6 = (bf16[32,16,128]{2,0,1:T(8,128)(2,1)S(1)}, bf16[32,16,128]{2,0,1:T(8,128)(2,1)S(1)}, u32[]{:S(2)}, u32[]{:S(2)}) collective-permute-start(bf16[32,16,128]{2,0,1:T(8,128)(2,1)S(1)} %fusion.7), channel_id=1, source_target_pairs={{0,112},{16,0},{32,16},{48,32},{64,48},{80,64},{96,80},{112,96},{1... | collective-permute-start | bytes 393224 | tf_op jit(solution)/shard_map/ppermute | solution.py:165
  146.1 1.3 copy-start.2

commit v12 on v10

--- a/solution.py
+++ b/solution.py
@@ -137,9 +137,10 @@
     halves = []
     got = []
     pat_t = jnp.transpose(pattern, (2, 0, 1))
-    steps = chans // CT // 2
-    for part in range(2):
-        c_part = smooth(blocks, beam_blocks, pat_t, n_chan, part * steps, steps)
+    total = chans // CT
+    first = (3 * total) // 8
+    for lo, steps in ((0, first), (first, total - first)):
+        c_part = smooth(blocks, beam_blocks, pat_t, n_chan, lo, steps)
         halves.append(c_part)
         got.append(lax.all_to_all(c_part, "chan", 0, 0, tiled=True))
     chunks = jnp.concatenate(halves, axis=1)

time: 146 us -> 146 us (level)
  waiting for transfers between devices: 18.6 us -> 15 us
  blocking collectives: 61.9 us -> 65 us
    all_to_all x1, waiting for transfers between devices: 3.59 us -> 0.01 us  [local(): got.append(lax.all_to_all(c_part, 'chan', 0, 0, tiled=True))]
    all_to_all x1, blocking collectives: 19.4 us -> 22.6 us  [local(): got.append(lax.all_to_all(c_part, 'chan', 0, 0, tiled=True))]
  transfers between devices with their start and end apart: 2 -> 2, of which waited for: 2 -> 1; matrix products, arithmetic and copies ran while one was open for 0% -> 0% of each run, Pallas kernels for 8% -> 9%
where the time goes in v12:
time: 146 us; the launch traced here: 145 us
  blocking collectives  65 us (45%)
  Pallas kernels  36.9 us (25%)
  waiting for transfers between devices  15 us (10%)
  starting transfers between devices  10.8 us (7%)
  local copies, waits for them, and re-layouts  9.81 us (7%)
  other arithmetic  4.56 us (3%)
  matrix products  2.56 us (2%)
    all_to_all x1, blocking collectives, sum_all(): got = lax.all_to_all(pieces, AXES, 0, 0, tiled=False)  23.4 us
    pallas_call x2, Pallas kernels, smooth(): pl.pallas_call(smooth_kernel, out_shape=jax.ShapeDtypeStruct((parts, step...  22.8 us
    all_to_all x1, blocking collectives, local(): got.append(lax.all_to_all(c_part, 'chan', 0, 0, tiled=True))  22.6 us
    all_to_all x1, blocking collectives, sum_all(): return lax.all_to_all(spread, AXES, 0, 0, tiled=False)  19.1 us
    all_to_all x1, waiting for transfers between devices, local(): gathered = lax.all_to_all(spread, 'chan', 0, 0, tiled=False)  15 us
    pallas_call x1, Pallas kernels, sweeps(): pl.pallas_call(functools.partial(sweep_kernel, iters=iters, nb=nb, bs=bs,...  14.1 us
    unnamed x7, local copies, waits for them, and re-layouts  7.13 us
    all_to_all x1, starting transfers between devices, local(): got.append(lax.all_to_all(c_part, 'chan', 0, 0, tiled=True))  5.96 us
  transfers between devices with their start and end apart: 2, of which 1 were waited for; matrix products, arithmetic and copies ran while one was open for 0% of the time, Pallas kernels for 9%

profile of v12, /device:TPU:1, one launch (start us, length us, event | category | flops | bytes accessed | tf_op | source)
XLA Modules:
  0.0 145.4 jit_solution(6981038421537669927)
XLA Ops:
  0.6 3.5 %copy.21 = bf16[8,8,128,128]{3,2,1,0:T(8,128)(2,1)} copy(bf16[8,8,128,128]{3,1,2,0:T(8,128)(2,1)} %bitcast.38) | data formatting | bytes 4194304
  4.1 9.2 %shard_map.59 = bf16[8,24,16,128]{3,2,1,0:T(8,128)(2,1)} custom-call(s32[9,64,128]{2,1,0:T(8,128)} %bitcast.40, bf16[64,128,128]{2,1,0:T(8,128)(2,1)} %bitcast.32, bf16[64,9,128,128]{3,2,1,0:T(8,128)(2,1)} %beam_ref.3), custom_call_target="tpu_custom_call" | custom-call | tf_op jit(solution)/shard_map/pallas_call | solution.py:35
  13.3 6.0 %all-to-all-start = ((bf16[8,24,16,128]{3,2,1,0:T(8,128)(2,1)}), bf16[8,24,16,128]{3,2,1,0:T(8,128)(2,1)S(1)}, u32[]{:S(2)}, u32[]{:S(2)}) async-start(bf16[8,24,16,128]{3,2,1,0:T(8,128)(2,1)} %shard_map.59), calls=%async_computation | async-start | bytes 1572864 | tf_op jit(solution)/shard_map/all_to_all | solution.py:145
  19.2 13.6 %shard_map.60 = bf16[8,40,16,128]{3,2,1,0:T(8,128)(2,1)} custom-call(s32[9,64,128]{2,1,0:T(8,128)} %bitcast.41, bf16[64,128,128]{2,1,0:T(8,128)(2,1)} %bitcast.33, bf16[64,9,128,128]{3,2,1,0:T(8,128)(2,1)} %beam_ref.3), custom_call_target="tpu_custom_call" | custom-call | tf_op jit(solution)/shard_map/pallas_call | solution.py:35
  32.9 22.6 %all_to_all.32 = bf16[8,40,16,128]{3,2,1,0:T(8,128)(2,1)S(1)} all-to-all(bf16[8,40,16,128]{3,2,1,0:T(8,128)(2,1)} %shard_map.60), channel_id=1, replica_groups=mesh['chan'=8,'pix'=16] {'chan'}, dimensions={0} | all-to-all | bytes 2621440 | tf_op jit(solution)/shard_map/all_to_all | solution.py:145
  55.4 0.2 pad_maximum_fusion
  55.6 1.3 fusion.5
  57.1 0.2 fusion.13
  57.3 0.5 copy.15
  57.9 23.4 %all_to_all.33 = f32[128,1,1280]{2,1,0:T(1,128)S(1)} all-to-all(f32[128,1,1280]{2,1,0:T(1,128)S(1)} %copy.15), channel_id=1, replica_groups=mesh['chan'=8,'pix'=16] {'chan','pix'}, dimensions={0} | all-to-all | bytes 1310720 | tf_op jit(solution)/shard_map/all_to_all | solution.py:110
  81.3 0.4 reduce_sum.9
  81.7 0.3 broadcast_in_dim.4
  82.0 19.1 %all_to_all.34 = f32[128,1,1280]{2,1,0:T(1,128)S(1)} all-to-all(f32[128,1,1280]{2,1,0:T(1,128)S(1)} %broadcast_in_dim.4), channel_id=1, replica_groups=mesh['chan'=8,'pix'=16] {'chan','pix'}, dimensions={0} | all-to-all | bytes 1310720 | tf_op jit(solution)/shard_map/all_to_all | solution.py:113
  101.1 0.9 copy.35
  102.0 14.1 %shard_map.61 = f32[32,512]{1,0:T(8,128)} custom-call(f32[128,1280]{1,0:T(8,128)} %bitcast.37, f32[32,512]{1,0:T(8,128)} %bitcast.43), custom_call_target="tpu_custom_call" | custom-call | tf_op jit(solution)/shard_map/pallas_call | solution.py:101
  116.1 0.8 bitcast_convert_fusion
  116.9 0.5 fusion.8
  117.4 1.2 broadcast_in_dim.5
  118.6 4.8 %all-to-all-start.4 = ((bf16[8,32,16,128]{3,1,2,0:T(8,128)(2,1)}), bf16[8,32,16,128]{3,1,2,0:T(8,128)(2,1)S(1)}, u32[]{:S(2)}, u32[]{:S(2)}) async-start(bf16[8,32,16,128]{3,1,2,0:T(8,128)(2,1)} %broadcast_in_dim.5), calls=%async_computation.4 | async-start | bytes 2097152 | tf_op jit(solution)/shard_map/all_to_all | solution.py:161
  123.4 15.0 %all-to-all-done.4 = bf16[8,32,16,128]{3,1,2,0:T(8,128)(2,1)S(1)} async-done(((bf16[8,32,16,128]{3,1,2,0:T(8,128)(2,1)}), bf16[8,32,16,128]{3,1,2,0:T(8,128)(2,1)S(1)}, u32[]{:S(2)}, u32[]{:S(2)}) %all-to-all-start.4) | async-done | bytes 1048608 | tf_op jit(solution)/shard_map/all_to_all | solution.py:161
  138.4 0.8 fusion.16
  139.2 2.8 %fusion = bf16[64,8,16,128]{3,2,0,1:T(8,128)(2,1)S(1)} fusion(f32[64,8,16,128]{3,0,2,1:T(8,128)S(1)} %fusion.16, bf16[8,40,16,128]{3,2,1,0:T(8,128)(2,1)S(1)} %copy-done, bf16[8,24,16,128]{3,2,1,0:T(8,128)(2,1)S(1)} %copy-done.1), kind=kLoop, calls=%fused_computation.1 | loop fusion | flops 4194304 | bytes 8388608 | tf_op jit(solution)/shard_map/convert_element_type | solution.py:165
  142.0 0.6 copy.18
  142.6 2.8 %copy.34 = bf16[8,8,128,128]{3,1,2,0:T(8,128)(2,1)} copy(bf16[8,8,128,128]{3,2,1,0:T(8,128)(2,1)S(1)} %bitcast.36) | data formatting | bytes 4194304
  (10 shorter events, 0.1 us)
Async XLA Ops:
  13.3 19.6 %all-to-all-start = ((bf16[8,24,16,128]{3,2,1,0:T(8,128)(2,1)}), bf16[8,24,16,128]{3,2,1,0:T(8,128)(2,1)S(1)}, u32[]{:S(2)}, u32[]{:S(2)}) async-start(bf16[8,24,16,128]{3,2,1,0:T(8,128)(2,1)} %shard_map.59), calls=%async_computation | async-start | bytes 1572864 | tf_op jit(solution)/shard_map/all_to_all | solution.py:145
  118.6 19.8 %all-to-all-start.4 = ((bf16[8,32,16,128]{3,1,2,0:T(8,128)(2,1)}), bf16[8,32,16,128]{3,1,2,0:T(8,128)(2,1)S(1)}, u32[]{:S(2)}, u32[]{:S(2)}) async-start(bf16[8,32,16,128]{3,1,2,0:T(8,128)(2,1)} %broadcast_in_dim.5), calls=%async_computation.4 | async-start | bytes 2097152 | tf_op jit(solution)/shard_map/all_to_all | solution.py:161
  123.4 15.8 %copy-start = (bf16[8,40,16,128]{3,2,1,0:T(8,128)(2,1)S(1)}, bf16[8,40,16,128]{3,2,1,0:T(8,128)(2,1)}, u32[]{:S(2)}) copy-start(bf16[8,40,16,128]{3,2,1,0:T(8,128)(2,1)} %shard_map.60) | copy-start | bytes 3932164
  123.4 15.8 %copy-start.1 = (bf16[8,24,16,128]{3,2,1,0:T(8,128)(2,1)S(1)}, bf16[8,24,16,128]{3,2,1,0:T(8,128)(2,1)}, u32[]{:S(2)}) copy-start(bf16[8,24,16,128]{3,2,1,0:T(8,128)(2,1)} %shard_map.59) | copy-start | bytes 2359300

commit v13 on v10

--- a/solution.py
+++ b/solution.py
@@ -37,7 +37,7 @@
         out_shape=jax.ShapeDtypeStruct((parts, steps * CT, nblk // parts, blk), jnp.bfloat16),
         grid=(steps,),
         in_specs=[pl.BlockSpec((taps, CT, nblk), lambda i: (0, i + first, 0)),
-                  pl.BlockSpec((CT, nblk, blk), lambda i: (i + first, 0, 0)),
+                  pl.BlockSpec((CT, nblk, blk), lambda i: (i, 0, 0)),
                   pl.BlockSpec((CT, taps, blk, blk), lambda i: (i + first, 0, 0, 0))],
         out_specs=pl.BlockSpec((parts, CT, nblk // parts, blk), lambda i: (0, i, 0, 0)),
     )(pat_t, sky3, beam)
@@ -132,14 +132,15 @@
     chans = sky_cube.shape[0]
     pix_group = sky_cube.shape[1]
     block_count = pix_group // BLK
-    blocks = sky_cube.reshape(chans, block_count, BLK)
     n_chan = lax.axis_size("chan")
     halves = []
     got = []
     pat_t = jnp.transpose(pattern, (2, 0, 1))
     steps = chans // CT // 2
     for part in range(2):
-        c_part = smooth(blocks, beam_blocks, pat_t, n_chan, part * steps, steps)
+        lo = part * steps * CT
+        own = sky_cube[lo:lo + steps * CT].reshape(steps * CT, block_count, BLK)
+        c_part = smooth(own, beam_blocks, pat_t, n_chan, part * steps, steps)
         halves.append(c_part)
         got.append(lax.all_to_all(c_part, "chan", 0, 0, tiled=True))
     chunks = jnp.concatenate(halves, axis=1)

time: 146 us -> 146 us (level)
  waiting for transfers between devices: 18.6 us -> 17.1 us
    all_to_all x1, waiting for transfers between devices: 3.59 us -> 2.1 us  [local(): got.append(lax.all_to_all(c_part, 'chan', 0, 0, tiled=True))]
    unnamed x7 -> x9, local copies, waits for them, and re-layouts: 7.13 us -> 7.73 us
  transfers between devices with their start and end apart: 2 -> 2, of which waited for: 2 -> 2; matrix products, arithmetic and copies ran while one was open for 0% -> 1% of each run, Pallas kernels for 8% -> 8%
where the time goes in v13:
time: 146 us; the launch traced here: 145 us
  blocking collectives  61.9 us (42%)
  Pallas kernels  37.2 us (25%)
  waiting for transfers between devices  17.1 us (12%)
  starting transfers between devices  10.8 us (7%)
  local copies, waits for them, and re-layouts  10.4 us (7%)
  other arithmetic  4.56 us (3%)
  matrix products  2.57 us (2%)
    all_to_all x1, blocking collectives, sum_all(): got = lax.all_to_all(pieces, AXES, 0, 0, tiled=False)  23.5 us
    pallas_call x2, Pallas kernels, smooth(): pl.pallas_call(smooth_kernel, out_shape=jax.ShapeDtypeStruct((parts, step...  23 us
    all_to_all x1, blocking collectives, local(): got.append(lax.all_to_all(c_part, 'chan', 0, 0, tiled=True))  19.4 us
    all_to_all x1, blocking collectives, sum_all(): return lax.all_to_all(spread, AXES, 0, 0, tiled=False)  19.1 us
    all_to_all x1, waiting for transfers between devices, local(): gathered = lax.all_to_all(spread, 'chan', 0, 0, tiled=False)  15 us
    pallas_call x1, Pallas kernels, sweeps(): pl.pallas_call(functools.partial(sweep_kernel, iters=iters, nb=nb, bs=bs,...  14.1 us
    unnamed x9, local copies, waits for them, and re-layouts  7.73 us
    all_to_all x1, starting transfers between devices, local(): got.append(lax.all_to_all(c_part, 'chan', 0, 0, tiled=True))  5.96 us
  transfers between devices with their start and end apart: 2, of which 2 were waited for; matrix products, arithmetic and copies ran while one was open for 1% of the time, Pallas kernels for 8%

profile of v13, /device:TPU:1, one launch (start us, length us, event | category | flops | bytes accessed | tf_op | source)
XLA Modules:
  0.0 145.2 jit_solution(5777670707530797279)
XLA Ops:
  0.6 1.7 %slice_bitcast_fusion.1 = (bf16[4,8,128,128]{3,1,2,0:T(8,128)(2,1)S(1)}, bf16[4,8,128,128]{3,1,2,0:T(8,128)(2,1)S(1)}) fusion(bf16[64,16384]{1,0:T(8,128)(2,1)} %param.4), kind=kLoop, calls=%fused_computation.11 | loop fusion | bytes 4194304
  2.3 1.2 copy.21
  3.5 11.4 %shard_map.59 = bf16[8,32,16,128]{3,2,1,0:T(8,128)(2,1)} custom-call(s32[9,64,128]{2,1,0:T(8,128)} %bitcast.43, bf16[32,128,128]{2,1,0:T(8,128)(2,1)} %bitcast.39, bf16[64,9,128,128]{3,2,1,0:T(8,128)(2,1)} %beam_ref.3), custom_call_target="tpu_custom_call" | custom-call | tf_op jit(solution)/shard_map/pallas_call | solution.py:35
  14.9 6.0 %all-to-all-start = ((bf16[8,32,16,128]{3,2,1,0:T(8,128)(2,1)}), bf16[8,32,16,128]{3,2,1,0:T(8,128)(2,1)S(1)}, u32[]{:S(2)}, u32[]{:S(2)}) async-start(bf16[8,32,16,128]{3,2,1,0:T(8,128)(2,1)} %shard_map.59), calls=%async_computation | async-start | bytes 2097152 | tf_op jit(solution)/shard_map/all_to_all | solution.py:145
  20.9 1.2 copy.22
  22.1 11.7 %shard_map.60 = bf16[8,32,16,128]{3,2,1,0:T(8,128)(2,1)} custom-call(s32[9,64,128]{2,1,0:T(8,128)} %bitcast.44, bf16[32,128,128]{2,1,0:T(8,128)(2,1)} %bitcast.40, bf16[64,9,128,128]{3,2,1,0:T(8,128)(2,1)} %beam_ref.3), custom_call_target="tpu_custom_call" | custom-call | tf_op jit(solution)/shard_map/pallas_call | solution.py:35
  33.7 2.1 %all-to-all-done = bf16[8,32,16,128]{3,2,1,0:T(8,128)(2,1)S(1)} async-done(((bf16[8,32,16,128]{3,2,1,0:T(8,128)(2,1)}), bf16[8,32,16,128]{3,2,1,0:T(8,128)(2,1)S(1)}, u32[]{:S(2)}, u32[]{:S(2)}) %all-to-all-start) | async-done | bytes 1048608 | tf_op jit(solution)/shard_map/all_to_all | solution.py:145
  35.8 19.4 %all_to_all.32 = bf16[8,32,16,128]{3,2,1,0:T(8,128)(2,1)S(1)} all-to-all(bf16[8,32,16,128]{3,2,1,0:T(8,128)(2,1)} %shard_map.60), channel_id=1, replica_groups=mesh['chan'=8,'pix'=16] {'chan'}, dimensions={0} | all-to-all | bytes 2097152 | tf_op jit(solution)/shard_map/all_to_all | solution.py:145
  55.4 1.3 fusion.5
  57.1 0.5 copy.15
  57.6 23.5 %all_to_all.33 = f32[128,1,1280]{2,1,0:T(1,128)S(1)} all-to-all(f32[128,1,1280]{2,1,0:T(1,128)S(1)} %copy.15), channel_id=1, replica_groups=mesh['chan'=8,'pix'=16] {'chan','pix'}, dimensions={0} | all-to-all | bytes 1310720 | tf_op jit(solution)/shard_map/all_to_all | solution.py:110
  81.1 0.4 reduce_sum.9
  81.8 19.1 %all_to_all.34 = f32[128,1,1280]{2,1,0:T(1,128)S(1)} all-to-all(f32[128,1,1280]{2,1,0:T(1,128)S(1)} %broadcast_in_dim.4), channel_id=1, replica_groups=mesh['chan'=8,'pix'=16] {'chan','pix'}, dimensions={0} | all-to-all | bytes 1310720 | tf_op jit(solution)/shard_map/all_to_all | solution.py:113
  100.9 0.9 copy.36
  101.8 14.1 %shard_map.61 = f32[32,512]{1,0:T(8,128)} custom-call(f32[128,1280]{1,0:T(8,128)} %bitcast.41, f32[32,512]{1,0:T(8,128)} %bitcast.46), custom_call_target="tpu_custom_call" | custom-call | tf_op jit(solution)/shard_map/pallas_call | solution.py:101
  115.9 0.8 bitcast_convert_fusion
  116.8 0.5 fusion.8
  117.2 1.2 broadcast_in_dim.5
  118.4 4.8 %all-to-all-start.4 = ((bf16[8,32,16,128]{3,1,2,0:T(8,128)(2,1)}), bf16[8,32,16,128]{3,1,2,0:T(8,128)(2,1)S(1)}, u32[]{:S(2)}, u32[]{:S(2)}) async-start(bf16[8,32,16,128]{3,1,2,0:T(8,128)(2,1)} %broadcast_in_dim.5), calls=%async_computation.4 | async-start | bytes 2097152 | tf_op jit(solution)/shard_map/all_to_all | solution.py:161
  123.2 15.0 %all-to-all-done.4 = bf16[8,32,16,128]{3,1,2,0:T(8,128)(2,1)S(1)} async-done(((bf16[8,32,16,128]{3,1,2,0:T(8,128)(2,1)}), bf16[8,32,16,128]{3,1,2,0:T(8,128)(2,1)S(1)}, u32[]{:S(2)}, u32[]{:S(2)}) %all-to-all-start.4) | async-done | bytes 1048608 | tf_op jit(solution)/shard_map/all_to_all | solution.py:161
  138.2 0.8 fusion.16
  139.0 2.8 %fusion = bf16[64,8,16,128]{3,2,0,1:T(8,128)(2,1)S(1)} fusion(f32[64,8,16,128]{3,0,2,1:T(8,128)S(1)} %fusion.16, bf16[8,32,16,128]{3,2,1,0:T(8,128)(2,1)S(1)} %copy-done.1, bf16[8,32,16,128]{3,2,1,0:T(8,128)(2,1)S(1)} %copy-done), kind=kLoop, calls=%fused_computation.1 | loop fusion | flops 4194304 | bytes 8388608 | tf_op jit(solution)/shard_map/convert_element_type | solution.py:165
  141.8 0.6 copy.18
  142.5 2.8 %copy.35 = bf16[8,8,128,128]{3,1,2,0:T(8,128)(2,1)} copy(bf16[8,8,128,128]{3,2,1,0:T(8,128)(2,1)S(1)} %bitcast.38) | data formatting | bytes 4194304
  (12 shorter events, 0.9 us)
Async XLA Ops:
  14.9 20.9 %all-to-all-start = ((bf16[8,32,16,128]{3,2,1,0:T(8,128)(2,1)}), bf16[8,32,16,128]{3,2,1,0:T(8,128)(2,1)S(1)}, u32[]{:S(2)}, u32[]{:S(2)}) async-start(bf16[8,32,16,128]{3,2,1,0:T(8,128)(2,1)} %shard_map.59), calls=%async_computation | async-start | bytes 2097152 | tf_op jit(solution)/shard_map/all_to_all | solution.py:145
  118.4 19.8 %all-to-all-start.4 = ((bf16[8,32,16,128]{3,1,2,0:T(8,128)(2,1)}), bf16[8,32,16,128]{3,1,2,0:T(8,128)(2,1)S(1)}, u32[]{:S(2)}, u32[]{:S(2)}) async-start(bf16[8,32,16,128]{3,1,2,0:T(8,128)(2,1)} %broadcast_in_dim.5), calls=%async_computation.4 | async-start | bytes 2097152 | tf_op jit(solution)/shard_map/all_to_all | solution.py:161
  123.2 15.8 %copy-start = (bf16[8,32,16,128]{3,2,1,0:T(8,128)(2,1)S(1)}, bf16[8,32,16,128]{3,2,1,0:T(8,128)(2,1)}, u32[]{:S(2)}) copy-start(bf16[8,32,16,128]{3,2,1,0:T(8,128)(2,1)} %shard_map.59) | copy-start | bytes 3145732
  123.2 15.8 %copy-start.1 = (bf16[8,32,16,128]{3,2,1,0:T(8,128)(2,1)S(1)}, bf16[8,32,16,128]{3,2,1,0:T(8,128)(2,1)}, u32[]{:S(2)}) copy-start(bf16[8,32,16,128]{3,2,1,0:T(8,128)(2,1)} %shard_map.60) | copy-start | bytes 3145732

commit v14 on v13

--- a/solution.py
+++ b/solution.py
@@ -8,7 +8,7 @@
 BLK = 128
 ITERS = 3
 AXES = ("chan", "pix")
-CT = 8
+CT = 16
 
 def smooth_kernel(pat_ref, sky_ref, beam_ref, out_ref):
     taps = beam_ref.shape[1]

time: 146 us -> 146 us (level)
  no operation moved by 1% of the time
where the time goes in v14:
time: 146 us
  blocking collectives  61.9 us (42%)
  Pallas kernels  37.7 us (26%)
  waiting for transfers between devices  17 us (12%)
  starting transfers between devices  10.8 us (7%)
  local copies, waits for them, and re-layouts  10.4 us (7%)
  other arithmetic  4.56 us (3%)
  matrix products  2.57 us (2%)
    pallas_call x2, Pallas kernels, smooth(): pl.pallas_call(smooth_kernel, out_shape=jax.ShapeDtypeStruct((parts, step...  23.6 us
    all_to_all x1, blocking collectives, sum_all(): got = lax.all_to_all(pieces, AXES, 0, 0, tiled=False)  23.5 us
    all_to_all x1, blocking collectives, local(): got.append(lax.all_to_all(c_part, 'chan', 0, 0, tiled=True))  19.4 us
    all_to_all x1, blocking collectives, sum_all(): return lax.all_to_all(spread, AXES, 0, 0, tiled=False)  19.1 us
    all_to_all x1, waiting for transfers between devices, local(): gathered = lax.all_to_all(spread, 'chan', 0, 0, tiled=False)  15 us
    pallas_call x1, Pallas kernels, sweeps(): pl.pallas_call(functools.partial(sweep_kernel, iters=iters, nb=nb, bs=bs,...  14.1 us
    unnamed x9, local copies, waits for them, and re-layouts  7.73 us
    all_to_all x1, starting transfers between devices, local(): got.append(lax.all_to_all(c_part, 'chan', 0, 0, tiled=True))  5.96 us
  transfers between devices with their start and end apart: 2, of which 2 were waited for; matrix products, arithmetic and copies ran while one was open for 1% of the time, Pallas kernels for 8%

profile of v14, /device:TPU:1, one launch (start us, length us, event | category | flops | bytes accessed | tf_op | source)
XLA Modules:
  0.0 145.6 jit_solution(9317630539553662704)
XLA Ops:
  0.6 1.7 %slice_bitcast_fusion.1 = (bf16[4,8,128,128]{3,1,2,0:T(8,128)(2,1)S(1)}, bf16[4,8,128,128]{3,1,2,0:T(8,128)(2,1)S(1)}) fusion(bf16[64,16384]{1,0:T(8,128)(2,1)} %param.4), kind=kLoop, calls=%fused_computation.11 | loop fusion | bytes 4194304
  2.3 1.2 copy.21
  3.5 11.8 %shard_map.59 = bf16[8,32,16,128]{3,2,1,0:T(8,128)(2,1)} custom-call(s32[9,64,128]{2,1,0:T(8,128)} %bitcast.43, bf16[32,128,128]{2,1,0:T(8,128)(2,1)} %bitcast.39, bf16[64,9,128,128]{3,2,1,0:T(8,128)(2,1)} %beam_ref.3), custom_call_target="tpu_custom_call" | custom-call | tf_op jit(solution)/shard_map/pallas_call | solution.py:35
  15.3 6.0 %all-to-all-start = ((bf16[8,32,16,128]{3,2,1,0:T(8,128)(2,1)}), bf16[8,32,16,128]{3,2,1,0:T(8,128)(2,1)S(1)}, u32[]{:S(2)}, u32[]{:S(2)}) async-start(bf16[8,32,16,128]{3,2,1,0:T(8,128)(2,1)} %shard_map.59), calls=%async_computation | async-start | bytes 2097152 | tf_op jit(solution)/shard_map/all_to_all | solution.py:145
  21.2 1.2 copy.22
  22.4 11.8 %shard_map.60 = bf16[8,32,16,128]{3,2,1,0:T(8,128)(2,1)} custom-call(s32[9,64,128]{2,1,0:T(8,128)} %bitcast.44, bf16[32,128,128]{2,1,0:T(8,128)(2,1)} %bitcast.40, bf16[64,9,128,128]{3,2,1,0:T(8,128)(2,1)} %beam_ref.3), custom_call_target="tpu_custom_call" | custom-call | tf_op jit(solution)/shard_map/pallas_call | solution.py:35
  34.2 2.0 %all-to-all-done = bf16[8,32,16,128]{3,2,1,0:T(8,128)(2,1)S(1)} async-done(((bf16[8,32,16,128]{3,2,1,0:T(8,128)(2,1)}), bf16[8,32,16,128]{3,2,1,0:T(8,128)(2,1)S(1)}, u32[]{:S(2)}, u32[]{:S(2)}) %all-to-all-start) | async-done | bytes 1048608 | tf_op jit(solution)/shard_map/all_to_all | solution.py:145
  36.2 19.4 %all_to_all.32 = bf16[8,32,16,128]{3,2,1,0:T(8,128)(2,1)S(1)} all-to-all(bf16[8,32,16,128]{3,2,1,0:T(8,128)(2,1)} %shard_map.60), channel_id=1, replica_groups=mesh['chan'=8,'pix'=16] {'chan'}, dimensions={0} | all-to-all | bytes 2097152 | tf_op jit(solution)/shard_map/all_to_all | solution.py:145
  55.8 1.3 fusion.5
  57.5 0.5 copy.15
  58.0 23.5 %all_to_all.33 = f32[128,1,1280]{2,1,0:T(1,128)S(1)} all-to-all(f32[128,1,1280]{2,1,0:T(1,128)S(1)} %copy.15), channel_id=1, replica_groups=mesh['chan'=8,'pix'=16] {'chan','pix'}, dimensions={0} | all-to-all | bytes 1310720 | tf_op jit(solution)/shard_map/all_to_all | solution.py:110
  81.5 0.4 reduce_sum.9
  82.2 19.1 %all_to_all.34 = f32[128,1,1280]{2,1,0:T(1,128)S(1)} all-to-all(f32[128,1,1280]{2,1,0:T(1,128)S(1)} %broadcast_in_dim.4), channel_id=1, replica_groups=mesh['chan'=8,'pix'=16] {'chan','pix'}, dimensions={0} | all-to-all | bytes 1310720 | tf_op jit(solution)/shard_map/all_to_all | solution.py:113
  101.3 0.9 copy.36
  102.2 14.1 %shard_map.61 = f32[32,512]{1,0:T(8,128)} custom-call(f32[128,1280]{1,0:T(8,128)} %bitcast.41, f32[32,512]{1,0:T(8,128)} %bitcast.46), custom_call_target="tpu_custom_call" | custom-call | tf_op jit(solution)/shard_map/pallas_call | solution.py:101
  116.3 0.8 bitcast_convert_fusion
  117.2 0.5 fusion.8
  117.6 1.2 broadcast_in_dim.5
  118.8 4.8 %all-to-all-start.4 = ((bf16[8,32,16,128]{3,1,2,0:T(8,128)(2,1)}), bf16[8,32,16,128]{3,1,2,0:T(8,128)(2,1)S(1)}, u32[]{:S(2)}, u32[]{:S(2)}) async-start(bf16[8,32,16,128]{3,1,2,0:T(8,128)(2,1)} %broadcast_in_dim.5), calls=%async_computation.4 | async-start | bytes 2097152 | tf_op jit(solution)/shard_map/all_to_all | solution.py:161
  123.6 15.0 %all-to-all-done.4 = bf16[8,32,16,128]{3,1,2,0:T(8,128)(2,1)S(1)} async-done(((bf16[8,32,16,128]{3,1,2,0:T(8,128)(2,1)}), bf16[8,32,16,128]{3,1,2,0:T(8,128)(2,1)S(1)}, u32[]{:S(2)}, u32[]{:S(2)}) %all-to-all-start.4) | async-done | bytes 1048608 | tf_op jit(solution)/shard_map/all_to_all | solution.py:161
  138.6 0.8 fusion.16
  139.4 2.8 %fusion = bf16[64,8,16,128]{3,2,0,1:T(8,128)(2,1)S(1)} fusion(f32[64,8,16,128]{3,0,2,1:T(8,128)S(1)} %fusion.16, bf16[8,32,16,128]{3,2,1,0:T(8,128)(2,1)S(1)} %copy-done.1, bf16[8,32,16,128]{3,2,1,0:T(8,128)(2,1)S(1)} %copy-done), kind=kLoop, calls=%fused_computation.1 | loop fusion | flops 4194304 | bytes 8388608 | tf_op jit(solution)/shard_map/convert_element_type | solution.py:165
  142.3 0.6 copy.18
  142.9 2.8 %copy.35 = bf16[8,8,128,128]{3,1,2,0:T(8,128)(2,1)} copy(bf16[8,8,128,128]{3,2,1,0:T(8,128)(2,1)S(1)} %bitcast.38) | data formatting | bytes 4194304
  (12 shorter events, 0.9 us)
Async XLA Ops:
  15.3 20.9 %all-to-all-start = ((bf16[8,32,16,128]{3,2,1,0:T(8,128)(2,1)}), bf16[8,32,16,128]{3,2,1,0:T(8,128)(2,1)S(1)}, u32[]{:S(2)}, u32[]{:S(2)}) async-start(bf16[8,32,16,128]{3,2,1,0:T(8,128)(2,1)} %shard_map.59), calls=%async_computation | async-start | bytes 2097152 | tf_op jit(solution)/shard_map/all_to_all | solution.py:145
  118.8 19.8 %all-to-all-start.4 = ((bf16[8,32,16,128]{3,1,2,0:T(8,128)(2,1)}), bf16[8,32,16,128]{3,1,2,0:T(8,128)(2,1)S(1)}, u32[]{:S(2)}, u32[]{:S(2)}) async-start(bf16[8,32,16,128]{3,1,2,0:T(8,128)(2,1)} %broadcast_in_dim.5), calls=%async_computation.4 | async-start | bytes 2097152 | tf_op jit(solution)/shard_map/all_to_all | solution.py:161
  123.6 15.8 %copy-start = (bf16[8,32,16,128]{3,2,1,0:T(8,128)(2,1)S(1)}, bf16[8,32,16,128]{3,2,1,0:T(8,128)(2,1)}, u32[]{:S(2)}) copy-start(bf16[8,32,16,128]{3,2,1,0:T(8,128)(2,1)} %shard_map.59) | copy-start | bytes 3145732
  123.6 15.8 %copy-start.1 = (bf16[8,32,16,128]{3,2,1,0:T(8,128)(2,1)S(1)}, bf16[8,32,16,128]{3,2,1,0:T(8,128)(2,1)}, u32[]{:S(2)}) copy-start(bf16[8,32,16,128]{3,2,1,0:T(8,128)(2,1)} %shard_map.60) | copy-start | bytes 3145732

commit v15 on v13

--- a/solution.py
+++ b/solution.py
@@ -71,7 +71,7 @@
     return jnp.where(blk <= blk_t, half, half.T) * scale
 
 
-def sweep_kernel(g_ref, b_ref, o_ref, *, iters, nb, bs, scale):
+def sweep_kernel(g_ref, b_ref, o_ref, low_ref, *, iters, nb, bs, scale):
     g = build_gram(g_ref[...], nb, bs, scale)
     bt = b_ref[...]
     m = bt.shape[0]
@@ -95,14 +95,16 @@
         inv = jnp.where(bad, jnp.nan, inv)
         bt = jnp.dot(inv, it, precision=HI, preferred_element_type=jnp.float32)
     o_ref[...] = bt
+    low_ref[...] = bt.astype(low_ref.dtype)
 
 def sweeps(packed, basis, iters, nb, bs, scale):
     bt = basis.T
-    out = pl.pallas_call(
+    out, low = pl.pallas_call(
         functools.partial(sweep_kernel, iters=iters, nb=nb, bs=bs, scale=scale),
-        out_shape=jax.ShapeDtypeStruct(bt.shape, jnp.float32),
+        out_shape=(jax.ShapeDtypeStruct(bt.shape, jnp.float32),
+                   jax.ShapeDtypeStruct(bt.shape, jnp.bfloat16)),
     )(packed, bt)
-    return out.T
+    return out.T, low
 
 
 def sum_all(pieces):
@@ -154,14 +156,13 @@
     n_dev = lax.axis_size(AXES)
     packed = sum_all(pack_gram(partial_value, nb, n_dev))
     packed = packed.reshape(n_dev, -1)
-    basis = sweeps(packed, basis, ITERS, nb, partial_value.shape[0] // nb, 1.0 / all_pixels)
-    modes_low = basis.astype(jnp.bfloat16)
-    coeffs = jnp.einsum("cm,cbi->mbi", modes_low, by_pixel, preferred_element_type=jnp.float32).astype(jnp.bfloat16)
+    basis, modes_t = sweeps(packed, basis, ITERS, nb, partial_value.shape[0] // nb, 1.0 / all_pixels)
+    coeffs = jnp.einsum("mc,cbi->mbi", modes_t, by_pixel, preferred_element_type=jnp.float32).astype(jnp.bfloat16)
     spread = jnp.broadcast_to(coeffs[None], (n_chan,) + coeffs.shape)
     gathered = lax.all_to_all(spread, "chan", 0, 0, tiled=False)
     me = lax.axis_index("chan")
-    my_modes = lax.dynamic_slice_in_dim(modes_low, me * chans, chans, axis=0)
-    removed = jnp.einsum("cm,jmbi->cjbi", my_modes, gathered, preferred_element_type=jnp.float32)
+    my_modes = lax.dynamic_slice_in_dim(modes_t, me * chans, chans, axis=1)
+    removed = jnp.einsum("mc,jmbi->cjbi", my_modes, gathered, preferred_element_type=jnp.float32)
     cleaned = (chunks.transpose(1, 0, 2, 3).astype(jnp.float32) - removed).astype(jnp.bfloat16)
     cleaned = cleaned.reshape(chans, pix_group)
     return (cleaned, basis)

time: 146 us -> 146 us (level)
  no operation moved by 1% of the time
where the time goes in v15:
time: 146 us
  blocking collectives  61.9 us (42%)
  Pallas kernels  37.2 us (25%)
  waiting for transfers between devices  17.1 us (12%)
  starting transfers between devices  10.8 us (7%)
  local copies, waits for them, and re-layouts  10.4 us (7%)
  matrix products  4.02 us (3%)
  other arithmetic  3.72 us (3%)
    all_to_all x1, blocking collectives, sum_all(): got = lax.all_to_all(pieces, AXES, 0, 0, tiled=False)  23.5 us
    pallas_call x2, Pallas kernels, smooth(): pl.pallas_call(smooth_kernel, out_shape=jax.ShapeDtypeStruct((parts, step...  23.1 us
    all_to_all x1, blocking collectives, local(): got.append(lax.all_to_all(c_part, 'chan', 0, 0, tiled=True))  19.4 us
    all_to_all x1, blocking collectives, sum_all(): return lax.all_to_all(spread, AXES, 0, 0, tiled=False)  19.1 us
    all_to_all x1, waiting for transfers between devices, local(): gathered = lax.all_to_all(spread, 'chan', 0, 0, tiled=False)  15 us
    pallas_call x1, Pallas kernels, sweeps(): pl.pallas_call(functools.partial(sweep_kernel, iters=iters, nb=nb, bs=bs,...  14.1 us
    unnamed x9, local copies, waits for them, and re-layouts  7.73 us
    all_to_all x1, starting transfers between devices, local(): got.append(lax.all_to_all(c_part, 'chan', 0, 0, tiled=True))  5.96 us
  transfers between devices with their start and end apart: 2, of which 2 were waited for; matrix products, arithmetic and copies ran while one was open for 1% of the time, Pallas kernels for 8%

profile of v15, /device:TPU:1, one launch (start us, length us, event | category | flops | bytes accessed | tf_op | source)
XLA Modules:
  0.0 145.8 jit_solution(15602908566655535811)
XLA Ops:
  0.6 1.7 %slice_bitcast_fusion.1 = (bf16[4,8,128,128]{3,1,2,0:T(8,128)(2,1)S(1)}, bf16[4,8,128,128]{3,1,2,0:T(8,128)(2,1)S(1)}) fusion(bf16[64,16384]{1,0:T(8,128)(2,1)} %param.4), kind=kLoop, calls=%fused_computation.11 | loop fusion | bytes 4194304
  2.3 1.2 copy.21
  3.5 11.4 %shard_map.59 = bf16[8,32,16,128]{3,2,1,0:T(8,128)(2,1)} custom-call(s32[9,64,128]{2,1,0:T(8,128)} %bitcast.42, bf16[32,128,128]{2,1,0:T(8,128)(2,1)} %bitcast.38, bf16[64,9,128,128]{3,2,1,0:T(8,128)(2,1)} %beam_ref.3), custom_call_target="tpu_custom_call" | custom-call | tf_op jit(solution)/shard_map/pallas_call | solution.py:35
  14.9 6.0 %all-to-all-start = ((bf16[8,32,16,128]{3,2,1,0:T(8,128)(2,1)}), bf16[8,32,16,128]{3,2,1,0:T(8,128)(2,1)S(1)}, u32[]{:S(2)}, u32[]{:S(2)}) async-start(bf16[8,32,16,128]{3,2,1,0:T(8,128)(2,1)} %shard_map.59), calls=%async_computation | async-start | bytes 2097152 | tf_op jit(solution)/shard_map/all_to_all | solution.py:147
  20.9 1.2 copy.22
  22.1 11.7 %shard_map.60 = bf16[8,32,16,128]{3,2,1,0:T(8,128)(2,1)} custom-call(s32[9,64,128]{2,1,0:T(8,128)} %bitcast.43, bf16[32,128,128]{2,1,0:T(8,128)(2,1)} %bitcast.39, bf16[64,9,128,128]{3,2,1,0:T(8,128)(2,1)} %beam_ref.3), custom_call_target="tpu_custom_call" | custom-call | tf_op jit(solution)/shard_map/pallas_call | solution.py:35
  33.8 2.1 %all-to-all-done = bf16[8,32,16,128]{3,2,1,0:T(8,128)(2,1)S(1)} async-done(((bf16[8,32,16,128]{3,2,1,0:T(8,128)(2,1)}), bf16[8,32,16,128]{3,2,1,0:T(8,128)(2,1)S(1)}, u32[]{:S(2)}, u32[]{:S(2)}) %all-to-all-start) | async-done | bytes 1048608 | tf_op jit(solution)/shard_map/all_to_all | solution.py:147
  35.8 19.4 %all_to_all.32 = bf16[8,32,16,128]{3,2,1,0:T(8,128)(2,1)S(1)} all-to-all(bf16[8,32,16,128]{3,2,1,0:T(8,128)(2,1)} %shard_map.60), channel_id=1, replica_groups=mesh['chan'=8,'pix'=16] {'chan'}, dimensions={0} | all-to-all | bytes 2097152 | tf_op jit(solution)/shard_map/all_to_all | solution.py:147
  55.4 1.3 fusion.5
  57.1 0.5 copy.15
  57.6 23.5 %all_to_all.33 = f32[128,1,1280]{2,1,0:T(1,128)S(1)} all-to-all(f32[128,1,1280]{2,1,0:T(1,128)S(1)} %copy.15), channel_id=1, replica_groups=mesh['chan'=8,'pix'=16] {'chan','pix'}, dimensions={0} | all-to-all | bytes 1310720 | tf_op jit(solution)/shard_map/all_to_all | solution.py:112
  81.1 0.4 reduce_sum.9
  81.5 0.3 broadcast_in_dim.4
  81.8 19.1 %all_to_all.34 = f32[128,1,1280]{2,1,0:T(1,128)S(1)} all-to-all(f32[128,1,1280]{2,1,0:T(1,128)S(1)} %broadcast_in_dim.4), channel_id=1, replica_groups=mesh['chan'=8,'pix'=16] {'chan','pix'}, dimensions={0} | all-to-all | bytes 1310720 | tf_op jit(solution)/shard_map/all_to_all | solution.py:115
  100.9 0.9 copy.36
  101.8 14.1 %shard_map.61 = (f32[32,512]{1,0:T(8,128)}, bf16[32,512]{1,0:T(8,128)(2,1)}) custom-call(f32[128,1280]{1,0:T(8,128)} %bitcast.40, f32[32,512]{1,0:T(8,128)} %bitcast.44), custom_call_target="tpu_custom_call" | custom-call | tf_op jit(solution)/shard_map/pallas_call | solution.py:102
  115.9 1.2 fusion.8
  117.2 1.1 broadcast_in_dim.5
  118.3 4.8 %all-to-all-start.4 = ((bf16[8,32,16,128]{3,1,2,0:T(8,128)(2,1)}), bf16[8,32,16,128]{3,1,2,0:T(8,128)(2,1)S(1)}, u32[]{:S(2)}, u32[]{:S(2)}) async-start(bf16[8,32,16,128]{3,1,2,0:T(8,128)(2,1)} %broadcast_in_dim.5), calls=%async_computation.4 | async-start | bytes 2097152 | tf_op jit(solution)/shard_map/all_to_all | solution.py:162
  123.1 15.0 %all-to-all-done.4 = bf16[8,32,16,128]{3,1,2,0:T(8,128)(2,1)S(1)} async-done(((bf16[8,32,16,128]{3,1,2,0:T(8,128)(2,1)}), bf16[8,32,16,128]{3,1,2,0:T(8,128)(2,1)S(1)}, u32[]{:S(2)}, u32[]{:S(2)}) %all-to-all-start.4) | async-done | bytes 1048608 | tf_op jit(solution)/shard_map/all_to_all | solution.py:162
  138.1 1.5 %fusion.16 = f32[64,8,16,128]{3,0,2,1:T(8,128)S(1)} fusion(bf16[8,32,16,128]{3,1,2,0:T(8,128)(2,1)S(1)} %all-to-all-done.4, bf16[32,512]{1,0:T(8,128)(2,1)} %get-tuple-element.4, s32[]{:T(128)S(6)} %select_n.3), kind=kOutput, calls=%fused_computation.24 | convolution fusion | flops 67108864 | bytes 5251076 | tf_op jit(solution)/shard_map/mc,jmbi->cjbi/dot_general | solution.py:165
  139.6 2.8 %fusion = bf16[64,8,16,128]{3,2,0,1:T(8,128)(2,1)S(1)} fusion(f32[64,8,16,128]{3,0,2,1:T(8,128)S(1)} %fusion.16, bf16[8,32,16,128]{3,2,1,0:T(8,128)(2,1)S(1)} %copy-done.1, bf16[8,32,16,128]{3,2,1,0:T(8,128)(2,1)S(1)} %copy-done), kind=kLoop, calls=%fused_computation.1 | loop fusion | flops 4194304 | bytes 8388608 | tf_op jit(solution)/shard_map/convert_element_type | solution.py:166
  142.5 0.6 copy.18
  143.1 2.8 %copy.35 = bf16[8,8,128,128]{3,1,2,0:T(8,128)(2,1)} copy(bf16[8,8,128,128]{3,2,1,0:T(8,128)(2,1)S(1)} %bitcast.37) | data formatting | bytes 4194304
  (11 shorter events, 0.6 us)
Async XLA Ops:
  14.9 20.9 %all-to-all-start = ((bf16[8,32,16,128]{3,2,1,0:T(8,128)(2,1)}), bf16[8,32,16,128]{3,2,1,0:T(8,128)(2,1)S(1)}, u32[]{:S(2)}, u32[]{:S(2)}) async-start(bf16[8,32,16,128]{3,2,1,0:T(8,128)(2,1)} %shard_map.59), calls=%async_computation | async-start | bytes 2097152 | tf_op jit(solution)/shard_map/all_to_all | solution.py:147
  118.3 19.8 %all-to-all-start.4 = ((bf16[8,32,16,128]{3,1,2,0:T(8,128)(2,1)}), bf16[8,32,16,128]{3,1,2,0:T(8,128)(2,1)S(1)}, u32[]{:S(2)}, u32[]{:S(2)}) async-start(bf16[8,32,16,128]{3,1,2,0:T(8,128)(2,1)} %broadcast_in_dim.5), calls=%async_computation.4 | async-start | bytes 2097152 | tf_op jit(solution)/shard_map/all_to_all | solution.py:162
  123.1 16.5 %copy-start = (bf16[8,32,16,128]{3,2,1,0:T(8,128)(2,1)S(1)}, bf16[8,32,16,128]{3,2,1,0:T(8,128)(2,1)}, u32[]{:S(2)}) copy-start(bf16[8,32,16,128]{3,2,1,0:T(8,128)(2,1)} %shard_map.59) | copy-start | bytes 3145732
  123.1 16.5 %copy-start.1 = (bf16[8,32,16,128]{3,2,1,0:T(8,128)(2,1)S(1)}, bf16[8,32,16,128]{3,2,1,0:T(8,128)(2,1)}, u32[]{:S(2)}) copy-start(bf16[8,32,16,128]{3,2,1,0:T(8,128)(2,1)} %shard_map.60) | copy-start | bytes 3145732
